TPU v7x, 128 devices: a whole 4x4x4 slice. The times are simulated.
128 devices in a mesh: row: 8 (over x, core), col: 16 (over z, y).
Axes of the slice: x: 4, y: 4, z: 4, core: 2. Of those that a mesh axis runs over, the one named last changes fastest.
Arguments:
- start_field: float32 [256, 512, 512], P('row', 'col'), may hold values from -6 to 6
- source: float32 [256, 512, 512], P('row', 'col'), may hold values from -9 to 9
- conductance: float32 [256, 512, 512], P('row', 'col'), may hold values from 0.25 to 4
Outputs:
- solution: float32 [256, 512, 512], P('row', 'col')
All inputs are finite; a program needn't handle non-finite values.
Results may differ from a plain program's by a relative error of at most 0.00015.
Values sent between devices are 32-bit elements; how exact they have to be, the bound alone decides.
No kernel may reach another device: no remote copies, remote signals or barrier semaphores. Data moves between devices by JAX's collectives and lax.ppermute only.
A program may use at most 128 MiB of HBM per device.

v0:
```python
import functools

import jax
import jax.numpy as jnp
from jax import lax
from jax.experimental import pallas as pl
from jax.experimental.pallas import tpu as pltpu
from jax.sharding import PartitionSpec as P

damping = 2.0 / 3.0


def exchange(stack, width):
    for axis, dim in (("row", 1), ("col", 2)):
        count = lax.axis_size(axis)
        forward = [(i, i + 1) for i in range(count - 1)]
        backward = [(i + 1, i) for i in range(count - 1)]
        size = stack.shape[dim]
        low = lax.ppermute(lax.slice_in_dim(stack, size - width, size, axis=dim), axis, forward)
        high = lax.ppermute(lax.slice_in_dim(stack, 0, width, axis=dim), axis, backward)
        stack = jnp.concatenate([low, stack, high], axis=dim)
    return stack


def trim(field, k):
    if k == 0:
        return field
    return field[k:-k, k:-k]


def grid_mask(nx, ny, halo):
    rows = lax.axis_size("row")
    cols = lax.axis_size("col")
    gx = lax.axis_index("row") * nx - halo + lax.broadcasted_iota(jnp.int32, (nx + 2 * halo, 1, 1), 0)
    gy = lax.axis_index("col") * ny - halo + lax.broadcasted_iota(jnp.int32, (1, ny + 2 * halo, 1), 1)
    return ((gx >= 0) & (gx < nx * rows)) & ((gy >= 0) & (gy < ny * cols))


def z_lo(field):
    depth_idx = lax.broadcasted_iota(jnp.int32, field.shape, field.ndim - 1)
    return jnp.where(depth_idx == 0, 0.0, jnp.roll(field, 1, field.ndim - 1))


def z_hi(field):
    depth_idx = lax.broadcasted_iota(jnp.int32, field.shape, field.ndim - 1)
    return jnp.where(depth_idx == field.shape[-1] - 1, 0.0, jnp.roll(field, -1, field.ndim - 1))


def coefs(cond, scale):
    half = 0.5 * scale
    centre = cond[1:-1, 1:-1]
    wxm = (centre + cond[:-2, 1:-1]) * half
    wxp = (cond[2:, 1:-1] + centre) * half
    wym = (centre + cond[1:-1, :-2]) * half
    wyp = (cond[1:-1, 2:] + centre) * half
    wzm = (centre + z_lo(centre)) * half
    wzp = (z_hi(centre) + centre) * half
    diagonal = wxm + wxp + wym + wyp + wzm + wzp
    return wxm, wxp, wym, wyp, wzm, wzp, diagonal


def operate(field, cond, scale):
    wxm, wxp, wym, wyp, wzm, wzp, diagonal = coefs(cond, scale)
    centre = field[1:-1, 1:-1]
    beside = wxm * field[:-2, 1:-1] + wxp * field[2:, 1:-1]
    beside = beside + wym * field[1:-1, :-2] + wyp * field[1:-1, 2:]
    beside = beside + wzm * z_lo(centre) + wzp * z_hi(centre)
    return diagonal * centre - beside, diagonal, centre


def sweep(field, rhs, cond, scale, mask):
    image, diagonal, centre = operate(field, cond, scale)
    return jnp.where(mask, centre + damping * (rhs - image) / diagonal, 0.0)


def first_guess(rhs, cond, scale, mask):
    diagonal = coefs(cond, scale)[6]
    return jnp.where(mask, damping * rhs / diagonal, 0.0)


def restrict_mean(field):
    depth = field.shape[2]
    planar = field.reshape(field.shape[0] // 2, 2, field.shape[1] // 2, 2, depth).sum(axis=(1, 3))
    fine_idx = lax.broadcasted_iota(jnp.int32, (depth, depth // 2), 0)
    coarse_idx = lax.broadcasted_iota(jnp.int32, (depth, depth // 2), 1)
    table = jnp.where(fine_idx // 2 == coarse_idx, 0.125, 0.0).astype(jnp.float32)
    return jnp.dot(
        planar, table, precision=lax.Precision.HIGHEST, preferred_element_type=jnp.float32
    )


def prolong_copy(field):
    depth = field.shape[2]
    coarse_idx = lax.broadcasted_iota(jnp.int32, (depth, 2 * depth), 0)
    fine_idx = lax.broadcasted_iota(jnp.int32, (depth, 2 * depth), 1)
    table = jnp.where(fine_idx // 2 == coarse_idx, 1.0, 0.0).astype(jnp.float32)
    deeper = jnp.dot(
        field, table, precision=lax.Precision.HIGHEST, preferred_element_type=jnp.float32
    )
    return jnp.repeat(jnp.repeat(deeper, 2, 0), 2, 1)


CHUNK = 8


def _plane_kernel(off_ref, u_ref, ulo_ref, uhi_ref, b_ref, k_ref, klo_ref, khi_ref, o_ref, *,
                  scale, extent_x, extent_y, residual):
    step = pl.program_id(0)
    _, depth_y, depth_z = o_ref.shape
    half = 0.5 * scale
    y_idx = lax.broadcasted_iota(jnp.int32, (depth_y, depth_z), 0) + off_ref[1]
    z_idx = lax.broadcasted_iota(jnp.int32, (depth_y, depth_z), 1)
    y_ok = (y_idx >= 0) & (y_idx < extent_y)
    z_first = z_idx == 0
    z_last = z_idx == depth_z - 1

    def y_lo(a):
        return pltpu.roll(a, 1, 0)

    def y_hi(a):
        return pltpu.roll(a, depth_y - 1, 0)

    def z_lo(a):
        return jnp.where(z_first, 0.0, pltpu.roll(a, 1, 1))

    def z_hi(a):
        return jnp.where(z_last, 0.0, pltpu.roll(a, depth_z - 1, 1))

    for p in range(CHUNK):
        km = klo_ref[0] if p == 0 else k_ref[p - 1]
        kp = khi_ref[0] if p == CHUNK - 1 else k_ref[p + 1]
        kc = k_ref[p]
        um = ulo_ref[0] if p == 0 else u_ref[p - 1]
        up = uhi_ref[0] if p == CHUNK - 1 else u_ref[p + 1]
        uc = u_ref[p]
        wxm = (kc + km) * half
        wxp = (kp + kc) * half
        wym = (kc + y_lo(kc)) * half
        wyp = (y_hi(kc) + kc) * half
        wzm = (kc + z_lo(kc)) * half
        wzp = (z_hi(kc) + kc) * half
        diagonal = wxm + wxp + wym + wyp + wzm + wzp
        beside = wxm * um + wxp * up
        beside = beside + wym * y_lo(uc) + wyp * y_hi(uc)
        beside = beside + wzm * z_lo(uc) + wzp * z_hi(uc)
        image = diagonal * uc - beside
        if residual:
            o_ref[p] = b_ref[p] - image
        else:
            x_idx = off_ref[0] + step * CHUNK + p
            ok = y_ok & (x_idx >= 0) & (x_idx < extent_x)
            o_ref[p] = jnp.where(ok, uc + damping * (b_ref[p] - image) / diagonal, 0.0)


def plane_step(offsets, u, b, k, scale, extent_x, extent_y, residual=False):
    (u_arr, u_i), (b_arr, b_i), (k_arr, k_i) = u, b, k
    depth_x, depth_y, depth_z = u_arr.shape[-3:]
    chunks = depth_x // CHUNK

    def spec(arr, idx, kind):
        lead = (None,) if arr.ndim == 4 else ()
        pre = (idx,) if arr.ndim == 4 else ()
        if kind == "main":
            return pl.BlockSpec(lead + (CHUNK, depth_y, depth_z), lambda i, off: pre + (i, 0, 0))
        if kind == "lo":
            return pl.BlockSpec(lead + (1, depth_y, depth_z),
                                lambda i, off: pre + (jnp.maximum(i * CHUNK - 1, 0), 0, 0))
        return pl.BlockSpec(lead + (1, depth_y, depth_z),
                            lambda i, off: pre + (jnp.minimum(i * CHUNK + CHUNK, depth_x - 1), 0, 0))

    kernel = functools.partial(_plane_kernel, scale=scale, extent_x=extent_x,
                               extent_y=extent_y, residual=residual)
    grid_spec = pltpu.PrefetchScalarGridSpec(
        num_scalar_prefetch=1,
        grid=(chunks,),
        in_specs=[spec(u_arr, u_i, "main"), spec(u_arr, u_i, "lo"), spec(u_arr, u_i, "hi"),
                  spec(b_arr, b_i, "main"),
                  spec(k_arr, k_i, "main"), spec(k_arr, k_i, "lo"), spec(k_arr, k_i, "hi")],
        out_specs=pl.BlockSpec((CHUNK, depth_y, depth_z), lambda i, off: (i, 0, 0)),
    )
    cells = depth_x * depth_y * depth_z
    return pl.pallas_call(
        kernel,
        grid_spec=grid_spec,
        out_shape=jax.ShapeDtypeStruct((depth_x, depth_y, depth_z), jnp.float32),
        compiler_params=pltpu.CompilerParams(dimension_semantics=("arbitrary",)),
        cost_estimate=pl.CostEstimate(flops=45 * cells, transcendentals=0, bytes_accessed=4 * 4 * cells),
    )(offsets, u_arr, u_arr, u_arr, b_arr, k_arr, k_arr, k_arr)


def on_device(start_field, source, conductance):
    nx, ny = start_field.shape[0], start_field.shape[1]
    mx, my = nx // 2, ny // 2
    lx, ly = nx // 4, ny // 4

    with jax.named_scope("level0_down"):
        fine = exchange(jnp.stack([start_field, source, conductance]), 4)
        extent_x, extent_y = nx * lax.axis_size("row"), ny * lax.axis_size("col")
        offsets = jnp.stack([lax.axis_index("row") * nx - 4, lax.axis_index("col") * ny - 4]).astype(jnp.int32)
        u1 = plane_step(offsets, (fine, 0), (fine, 1), (fine, 2), 1.0, extent_x, extent_y)
        u2 = plane_step(offsets, (u1, None), (fine, 1), (fine, 2), 1.0, extent_x, extent_y)
        residual = plane_step(offsets, (u2, None), (fine, 1), (fine, 2), 1.0, extent_x, extent_y, residual=True)
        mid_rhs = restrict_mean(trim(residual, 4))
        mid_cond = restrict_mean(conductance)

    with jax.named_scope("level1_down"):
        mid = exchange(jnp.stack([mid_rhs, mid_cond]), 4)
        rhs1, k1 = mid[0], mid[1]
        e1 = first_guess(trim(rhs1, 1), k1, 0.25, grid_mask(mx, my, 3))
        e1 = sweep(e1, trim(rhs1, 2), trim(k1, 1), 0.25, grid_mask(mx, my, 2))
        image = operate(trim(e1, 1), trim(k1, 3), 0.25)[0]
        low_rhs = restrict_mean(mid_rhs - image)
        low_cond = restrict_mean(mid_cond)

    with jax.named_scope("level2"):
        low = exchange(jnp.stack([low_rhs, low_cond]), 5)
        rhs2, k2 = low[0], low[1]
        e2 = first_guess(trim(rhs2, 1), k2, 0.0625, grid_mask(lx, ly, 4))
        for halo in (3, 2, 1):
            e2 = sweep(e2, trim(rhs2, 5 - halo), trim(k2, 4 - halo), 0.0625, grid_mask(lx, ly, halo))

    with jax.named_scope("level1_up"):
        e1 = e1 + prolong_copy(e2)
        e1 = sweep(e1, trim(rhs1, 3), trim(k1, 2), 0.25, grid_mask(mx, my, 1))

    with jax.named_scope("level0_up"):
        u3 = u2 + jnp.pad(prolong_copy(e1), ((2, 2), (2, 2), (0, 0)))
        u4 = plane_step(offsets, (u3, None), (fine, 1), (fine, 2), 1.0, extent_x, extent_y)
        u5 = trim(plane_step(offsets, (u4, None), (fine, 1), (fine, 2), 1.0, extent_x, extent_y), 4)
    return u5


def solution(mesh):
    placed = (P("row", "col", None), P("row", "col", None), P("row", "col", None))
    return jax.shard_map(
        on_device, mesh=mesh, in_specs=placed, out_specs=P("row", "col", None), check_vma=False
    )
```

profile of v0, /device:TPU:27, one launch (start us, length us, event | category | flops | bytes accessed | tf_op | source)
XLA Modules:
  0.0 190.8 jit_solution(14282910348687107981)
XLA Ops:
  0.0 2.8 %pad_maximum_fusion.9 = (f32[3,4,32,512]{3,2,1,0:T(8,128)}, f32[3,4,32,512]{3,2,1,0:T(8,128)}) fusion(f32[1,32,32,512]{3,2,1,0:T(8,128)} %bitcast.41, f32[1,32,32,512]{3,2,1,0:T(8,128)} %bitcast.44, f32[1,32,32,512]{3,2,1,0:T(8,128)} %bitcast.47), kind=kLoop, calls=%fused_computation.12 | loop fusion | flops 786432 | bytes 7864320 | tf_op jit(solution)/shard_map/level0_down/slice | solution.py:19
  2.9 3.7 %collective-permute-start = (f32[3,4,32,512]{3,2,1,0:T(8,128)}, f32[3,4,32,512]{3,2,1,0:T(8,128)S(1)}, u32[]{:S(2)}, u32[]{:S(2)}) collective-permute-start(f32[3,4,32,512]{3,2,1,0:T(8,128)} %get-tuple-element.7), channel_id=1, source_target_pairs={{0,16},{16,32},{32,48},{48,64},{64,80},{80,96},{96,112},{1,17},{17... | collective-permute-start | bytes 2359304 | tf_op jit(solution)/shard_map/level0_down/ppermute | solution.py:19
  6.5 1.9 %collective-permute-start.1 = (f32[3,4,32,512]{3,2,1,0:T(8,128)}, f32[3,4,32,512]{3,2,1,0:T(8,128)}, u32[]{:S(2)}, u32[]{:S(2)}) collective-permute-start(f32[3,4,32,512]{3,2,1,0:T(8,128)} %get-tuple-element.8), channel_id=1, source_target_pairs={{16,0},{32,16},{48,32},{64,48},{80,64},{96,80},{112,96},{17,1},{33... | collective-permute-start | bytes 2359304 | tf_op jit(solution)/shard_map/level0_down/ppermute | solution.py:20
  8.7 2.2 %reshape.403 = f32[16,2,16,2,512]{4,3,2,1,0:T(2,128)} reshape(f32[32,32,512]{2,1,0:T(8,128)S(1)} %copy-done.1) | data formatting | bytes 4194304 | tf_op jit(solution)/shard_map/level0_down/reshape | solution.py:83
  10.9 4.0 %reduce_sum.37 = f32[16,16,512]{2,1,0:T(8,128)} reduce(f32[16,2,16,2,512]{4,3,2,1,0:T(2,128)} %reshape.403, f32[]{:T(128)} %constant.162.clone.1), dimensions={1,3}, to_apply=%region_1.2 | reduce | flops 393216 | bytes 2621444 | tf_op jit(solution)/shard_map/level0_down/reduce_sum | solution.py:83
  15.1 0.7 collective-permute-done
  15.8 4.4 %collective-permute-done.1 = f32[3,4,32,512]{3,2,1,0:T(8,128)} collective-permute-done((f32[3,4,32,512]{3,2,1,0:T(8,128)}, f32[3,4,32,512]{3,2,1,0:T(8,128)}, u32[]{:S(2)}, u32[]{:S(2)}) %collective-permute-start.1) | collective-permute-done | bytes 786464 | tf_op jit(solution)/shard_map/level0_down/ppermute | solution.py:20
  20.2 2.4 %pad_maximum_fusion.6 = (f32[3,40,4,512]{3,2,1,0:T(4,128)S(1)}, f32[3,40,4,512]{3,2,1,0:T(4,128)S(1)}) fusion(f32[3,4,32,512]{3,2,1,0:T(8,128)} %collective-permute-done.1, f32[3,4,32,512]{3,2,1,0:T(8,128)S(1)} %collective-permute-done, f32[1,32,32,512]{3,2,1,0:T(8,128)S(1)} %bitcast.42, f32[1,32,32,512]{3,2,1,0:T(8,128)} %bitcast.45, ...), kind=kLoop, calls=%fused_computation.9 | loop fusion | flops 1966080 | bytes 9830400 | tf_op jit(solution)/shard_map/level0_down/slice | solution.py:19
  22.5 3.2 %collective-permute-start.2 = (f32[3,40,4,512]{3,2,1,0:T(4,128)S(1)}, f32[3,40,4,512]{3,2,1,0:T(4,128)S(1)}, u32[]{:S(2)}, u32[]{:S(2)}) collective-permute-start(f32[3,40,4,512]{3,2,1,0:T(4,128)S(1)} %get-tuple-element.5), channel_id=1, source_target_pairs={{0,1},{1,2},{2,3},{3,4},{4,5},{5,6},{6,7},{7,8},{8,9},{9,10},{10,1... | collective-permute-start | bytes 2949128 | tf_op jit(solution)/shard_map/level0_down/ppermute | solution.py:19
  25.7 2.3 %collective-permute-start.3 = (f32[3,40,4,512]{3,2,1,0:T(4,128)S(1)}, f32[3,40,4,512]{3,2,1,0:T(4,128)S(1)}, u32[]{:S(2)}, u32[]{:S(2)}) collective-permute-start(f32[3,40,4,512]{3,2,1,0:T(4,128)S(1)} %get-tuple-element.6), channel_id=1, source_target_pairs={{1,0},{2,1},{3,2},{4,3},{5,4},{6,5},{7,6},{8,7},{9,8},{10,9},{11,1... | collective-permute-start | bytes 2949128 | tf_op jit(solution)/shard_map/level0_down/ppermute | solution.py:20
  28.0 0.7 pad_add_fusion.1.off_ref
  28.9 0.8 fusion.12
  29.7 17.7 %collective-permute-done.2 = f32[3,40,4,512]{3,2,1,0:T(4,128)S(1)} collective-permute-done((f32[3,40,4,512]{3,2,1,0:T(4,128)S(1)}, f32[3,40,4,512]{3,2,1,0:T(4,128)S(1)}, u32[]{:S(2)}, u32[]{:S(2)}) %collective-permute-start.2) | collective-permute-done | bytes 983072 | tf_op jit(solution)/shard_map/level0_down/ppermute | solution.py:19
  47.4 5.3 %collective-permute-done.3 = f32[3,40,4,512]{3,2,1,0:T(4,128)S(1)} collective-permute-done((f32[3,40,4,512]{3,2,1,0:T(4,128)S(1)}, f32[3,40,4,512]{3,2,1,0:T(4,128)S(1)}, u32[]{:S(2)}, u32[]{:S(2)}) %collective-permute-start.3) | collective-permute-done | bytes 983072 | tf_op jit(solution)/shard_map/level0_down/ppermute | solution.py:20
  52.7 7.0 %pad_maximum_fusion.u_ref.ulo_ref.uhi_ref.b_ref.k_ref.klo_ref.khi_ref = f32[3,40,40,512]{3,2,1,0:T(8,128)} fusion(f32[3,40,4,512]{3,2,1,0:T(4,128)S(1)} %collective-permute-done.3, f32[3,4,32,512]{3,2,1,0:T(8,128)} %collective-permute-done.1, f32[1,32,32,512]{3,2,1,0:T(8,128)S(1)} %bitcast.43, f32[1,32,32,512]{3,2,1,0:T(8,128)S(1)} %bitcast.46, ...), kind=kLoop, calls=%fused_computation | loop fusion | flops 14745600 | bytes 19660800 | tf_op jit(solution)/shard_map/level0_down/concatenate | solution.py:21
  59.8 11.2 %level0_down.3.u_ref.ulo_ref.uhi_ref = f32[40,40,512]{2,1,0:T(8,128)} custom-call(s32[2]{0:T(128)} %pad_add_fusion.1.off_ref, f32[3,40,40,512]{3,2,1,0:T(8,128)} %pad_maximum_fusion.u_ref.ulo_ref.uhi_ref.b_ref.k_ref.klo_ref.khi_ref, f32[3,40,40,512]{3,2,1,0:T(8,128)} %pad_maximum_fusion.u_ref.ulo_ref.uhi_ref.b_ref.k_ref.klo_ref.khi_ref, ...), custom_call_target="tpu_custom_call" | custom-call | flops 36864000 | bytes 13107200 | tf_op jit(solution)/shard_map/level0_down/pallas_call | solution.py:182
  71.0 11.3 %level0_down.4.u_ref.ulo_ref.uhi_ref = f32[40,40,512]{2,1,0:T(8,128)} custom-call(s32[2]{0:T(128)} %pad_add_fusion.1.off_ref, f32[40,40,512]{2,1,0:T(8,128)} %level0_down.3.u_ref.ulo_ref.uhi_ref, f32[40,40,512]{2,1,0:T(8,128)} %level0_down.3.u_ref.ulo_ref.uhi_ref, f32[40,40,512]{2,1,0:T(8,128)} %level0_down.3.u_ref.ulo_ref.uhi_ref, ...), custom_call_target="tpu_custom_call" | custom-call | flops 36864000 | bytes 13107200 | tf_op jit(solution)/shard_map/level0_down/pallas_call | solution.py:182
  82.3 10.9 %level0_down.5 = f32[40,40,512]{2,1,0:T(8,128)} custom-call(s32[2]{0:T(128)} %pad_add_fusion.1.off_ref, f32[40,40,512]{2,1,0:T(8,128)} %level0_down.4.u_ref.ulo_ref.uhi_ref, f32[40,40,512]{2,1,0:T(8,128)} %level0_down.4.u_ref.ulo_ref.uhi_ref, f32[40,40,512]{2,1,0:T(8,128)} %level0_down.4.u_ref.ulo_ref.uhi_ref, ...), custom_call_target="tpu_custom_call" | custom-call | flops 36864000 | bytes 13107200 | tf_op jit(solution)/shard_map/level0_down/pallas_call | solution.py:182
  93.2 2.1 %slice.734 = f32[32,32,512]{2,1,0:T(8,128)S(1)} slice(f32[40,40,512]{2,1,0:T(8,128)} %level0_down.5), slice={[4:36], [4:36], [0:512]} | slice | bytes 4194304 | tf_op jit(solution)/shard_map/level0_down/slice | solution.py:28
  95.3 2.2 %reshape.402 = f32[16,2,16,2,512]{4,3,2,1,0:T(2,128)} reshape(f32[32,32,512]{2,1,0:T(8,128)S(1)} %slice.734) | data formatting | bytes 4194304 | tf_op jit(solution)/shard_map/level0_down/reshape | solution.py:83
  97.5 3.2 %reduce_sum.36 = f32[16,16,512]{2,1,0:T(8,128)S(1)} reduce(f32[16,2,16,2,512]{4,3,2,1,0:T(2,128)} %reshape.402, f32[]{:T(128)} %constant.162.clone.1), dimensions={1,3}, to_apply=%region_0.0 | reduce | flops 393216 | bytes 2621444 | tf_op jit(solution)/shard_map/level0_down/reduce_sum | solution.py:83
  100.7 0.8 fusion.14
  101.5 3.5 %collective-permute-start.4 = (f32[2,4,16,256]{3,2,1,0:T(8,128)S(1)}, f32[2,4,16,256]{3,2,1,0:T(8,128)S(1)}, u32[]{:S(2)}, u32[]{:S(2)}) collective-permute-start(f32[2,4,16,256]{3,2,1,0:T(8,128)S(1)} %get-tuple-element.33), channel_id=1, source_target_pairs={{0,16},{16,32},{32,48},{48,64},{64,80},{80,96},{96,112},{1,17},{17... | collective-permute-start | bytes 393224 | tf_op jit(solution)/shard_map/level1_down/ppermute | solution.py:19
  105.0 1.9 %collective-permute-start.5 = (f32[2,4,16,256]{3,2,1,0:T(8,128)S(1)}, f32[2,4,16,256]{3,2,1,0:T(8,128)S(1)}, u32[]{:S(2)}, u32[]{:S(2)}) collective-permute-start(f32[2,4,16,256]{3,2,1,0:T(8,128)S(1)} %get-tuple-element.34), channel_id=1, source_target_pairs={{16,0},{32,16},{48,32},{64,48},{80,64},{96,80},{112,96},{17,1},{33... | collective-permute-start | bytes 393224 | tf_op jit(solution)/shard_map/level1_down/ppermute | solution.py:20
  106.9 0.1 reshape.405
  107.1 0.2 reduce_sum.39
  107.3 0.4 convolution_bitcast_fusion
  107.7 3.6 %collective-permute-done.5 = f32[2,4,16,256]{3,2,1,0:T(8,128)S(1)} collective-permute-done((f32[2,4,16,256]{3,2,1,0:T(8,128)S(1)}, f32[2,4,16,256]{3,2,1,0:T(8,128)S(1)}, u32[]{:S(2)}, u32[]{:S(2)}) %collective-permute-start.5) | collective-permute-done | bytes 131104 | tf_op jit(solution)/shard_map/level1_down/ppermute | solution.py:20
  111.4 1.9 %collective-permute-start.6 = (f32[2,24,4,256]{3,2,1,0:T(4,128)S(1)}, f32[2,24,4,256]{3,2,1,0:T(4,128)S(1)}, u32[]{:S(2)}, u32[]{:S(2)}) collective-permute-start(f32[2,24,4,256]{3,2,1,0:T(4,128)S(1)} %get-tuple-element.11), channel_id=1, source_target_pairs={{0,1},{1,2},{2,3},{3,4},{4,5},{5,6},{6,7},{7,8},{8,9},{9,10},{10,1... | collective-permute-start | bytes 589832 | tf_op jit(solution)/shard_map/level1_down/ppermute | solution.py:19
  113.3 3.6 %collective-permute-start.7 = (f32[2,24,4,256]{3,2,1,0:T(4,128)S(1)}, f32[2,24,4,256]{3,2,1,0:T(4,128)S(1)}, u32[]{:S(2)}, u32[]{:S(2)}) collective-permute-start(f32[2,24,4,256]{3,2,1,0:T(4,128)S(1)} %get-tuple-element.12), channel_id=1, source_target_pairs={{1,0},{2,1},{3,2},{4,3},{5,4},{6,5},{7,6},{8,7},{9,8},{10,9},{11,1... | collective-permute-start | bytes 589832 | tf_op jit(solution)/shard_map/level1_down/ppermute | solution.py:20
  116.9 2.2 %collective-permute-done.6 = f32[2,24,4,256]{3,2,1,0:T(4,128)S(1)} collective-permute-done((f32[2,24,4,256]{3,2,1,0:T(4,128)S(1)}, f32[2,24,4,256]{3,2,1,0:T(4,128)S(1)}, u32[]{:S(2)}, u32[]{:S(2)}) %collective-permute-start.6) | collective-permute-done | bytes 196640 | tf_op jit(solution)/shard_map/level1_down/ppermute | solution.py:19
  119.1 3.7 %collective-permute-done.7 = f32[2,24,4,256]{3,2,1,0:T(4,128)S(1)} collective-permute-done((f32[2,24,4,256]{3,2,1,0:T(4,128)S(1)}, f32[2,24,4,256]{3,2,1,0:T(4,128)S(1)}, u32[]{:S(2)}, u32[]{:S(2)}) %collective-permute-start.7) | collective-permute-done | bytes 196640 | tf_op jit(solution)/shard_map/level1_down/ppermute | solution.py:20
  122.9 0.2 pad_maximum_fusion.1
  123.1 0.2 fusion.230
  123.5 0.6 fusion.5
  124.1 0.2 fusion.233
  124.4 0.2 fusion.229
  124.8 1.2 fusion.39
  126.5 0.6 fusion.66
  127.2 0.2 reduce_sum.38
  127.4 0.4 convolution_bitcast_fusion.1
  127.8 3.3 %collective-permute-start.8 = (f32[2,5,8,128]{3,2,1,0:T(8,128)S(1)}, f32[2,5,8,128]{3,2,1,0:T(8,128)S(1)}, u32[]{:S(2)}, u32[]{:S(2)}) collective-permute-start(f32[2,5,8,128]{3,2,1,0:T(8,128)S(1)} %get-tuple-element.75), channel_id=1, source_target_pairs={{0,16},{16,32},{32,48},{48,64},{64,80},{80,96},{96,112},{1,17},{17... | collective-permute-start | bytes 122888 | tf_op jit(solution)/shard_map/level2/ppermute | solution.py:19
  131.1 1.9 %collective-permute-start.9 = (f32[2,5,8,128]{3,2,1,0:T(8,128)S(1)}, f32[2,5,8,128]{3,2,1,0:T(8,128)S(1)}, u32[]{:S(2)}, u32[]{:S(2)}) collective-permute-start(f32[2,5,8,128]{3,2,1,0:T(8,128)S(1)} %get-tuple-element.76), channel_id=1, source_target_pairs={{16,0},{32,16},{48,32},{64,48},{80,64},{96,80},{112,96},{17,1},{33... | collective-permute-start | bytes 122888 | tf_op jit(solution)/shard_map/level2/ppermute | solution.py:20
  133.0 0.2 fusion.225
  133.2 3.2 %collective-permute-done.9 = f32[2,5,8,128]{3,2,1,0:T(8,128)S(1)} collective-permute-done((f32[2,5,8,128]{3,2,1,0:T(8,128)S(1)}, f32[2,5,8,128]{3,2,1,0:T(8,128)S(1)}, u32[]{:S(2)}, u32[]{:S(2)}) %collective-permute-start.9) | collective-permute-done | bytes 40992 | tf_op jit(solution)/shard_map/level2/ppermute | solution.py:20
  136.4 1.9 %collective-permute-start.10 = (f32[2,18,5,128]{3,2,1,0:T(8,128)S(1)}, f32[2,18,5,128]{3,2,1,0:T(8,128)S(1)}, u32[]{:S(2)}, u32[]{:S(2)}) collective-permute-start(f32[2,18,5,128]{3,2,1,0:T(8,128)S(1)} %get-tuple-element.61), channel_id=1, source_target_pairs={{0,1},{1,2},{2,3},{3,4},{4,5},{5,6},{6,7},{7,8},{8,9},{9,10},{10,1... | collective-permute-start | bytes 276488 | tf_op jit(solution)/shard_map/level2/ppermute | solution.py:19
  138.4 3.4 %collective-permute-start.11 = (f32[2,18,5,128]{3,2,1,0:T(8,128)S(1)}, f32[2,18,5,128]{3,2,1,0:T(8,128)S(1)}, u32[]{:S(2)}, u32[]{:S(2)}) collective-permute-start(f32[2,18,5,128]{3,2,1,0:T(8,128)S(1)} %get-tuple-element.62), channel_id=1, source_target_pairs={{1,0},{2,1},{3,2},{4,3},{5,4},{6,5},{7,6},{8,7},{9,8},{10,9},{11,1... | collective-permute-start | bytes 276488 | tf_op jit(solution)/shard_map/level2/ppermute | solution.py:20
  141.7 0.8 fusion.224
  142.6 4.0 %collective-permute-done.11 = f32[2,18,5,128]{3,2,1,0:T(8,128)S(1)} collective-permute-done((f32[2,18,5,128]{3,2,1,0:T(8,128)S(1)}, f32[2,18,5,128]{3,2,1,0:T(8,128)S(1)}, u32[]{:S(2)}, u32[]{:S(2)}) %collective-permute-start.11) | collective-permute-done | bytes 92192 | tf_op jit(solution)/shard_map/level2/ppermute | solution.py:20
  147.0 0.2 fusion.105
  147.6 0.3 fusion.137
  148.3 0.3 fusion.158
  148.9 0.5 fusion.110
  149.7 0.3 reshape.407
  150.0 0.2 fusion.234
  150.4 0.5 copy-done.5
  151.0 2.1 %fusion.10 = f32[18,18,512]{2,1,0:T(8,128)S(1)} fusion(f32[20,20,256]{2,1,0:T(8,128)S(1)} %add.699, f32[24,24,256]{2,1,0:T(8,128)S(1)} %get-tuple-element.9, f32[18,18,255]{2,1,0:T(8,128)S(1)} %get-tuple-element.36, f32[18,18,1]{2,1,0:T(8,128)S(1)} %get-tuple-element.38, f32[18,18,1]{2,1,0:T(8,128)S(1)} %get-tuple-element.37, ...), kind=kOutput, calls=%fused_computation.32 | convolution fusion | flops 513567744 | bytes 8192512 | tf_op jit(solution)/shard_map/level0_up/dot_general | solution.py:97
  153.1 0.2 broadcast_in_dim.195
  153.3 2.4 %broadcast_in_dim.196 = f32[36,18,2,512]{3,2,1,0:T(2,128)} broadcast(f32[36,18,512]{2,1,0:T(8,128)S(1)} %bitcast.50), dimensions={0,1,3} | broadcast | bytes 3981312 | tf_op jit(solution)/shard_map/level0_up/broadcast_in_dim | solution.py:100
  155.7 4.8 %reshape.409 = f32[36,36,512]{2,1,0:T(8,128)} reshape(f32[36,18,2,512]{3,2,1,0:T(2,128)} %broadcast_in_dim.196) | data formatting | bytes 5308416 | tf_op jit(solution)/shard_map/level0_up/reshape | solution.py:100
  160.6 4.3 %pad_add_fusion.u_ref.ulo_ref.uhi_ref = f32[40,40,512]{2,1,0:T(8,128)} fusion(f32[40,40,512]{2,1,0:T(8,128)S(1)} %copy-done, f32[36,36,512]{2,1,0:T(8,128)} %reshape.409), kind=kLoop, calls=%fused_computation.1 | loop fusion | flops 819200 | bytes 9207808 | tf_op jit(solution)/shard_map/level0_up/add | solution.py:227
  164.9 11.3 %level0_up.2.u_ref.ulo_ref.uhi_ref = f32[40,40,512]{2,1,0:T(8,128)} custom-call(s32[2]{0:T(128)} %pad_add_fusion.1.off_ref, f32[40,40,512]{2,1,0:T(8,128)} %pad_add_fusion.u_ref.ulo_ref.uhi_ref, f32[40,40,512]{2,1,0:T(8,128)} %pad_add_fusion.u_ref.ulo_ref.uhi_ref, f32[40,40,512]{2,1,0:T(8,128)} %pad_add_fusion.u_ref.ulo_ref.uhi_ref, ...), custom_call_target="tpu_custom_call" | custom-call | flops 36864000 | bytes 13107200 | tf_op jit(solution)/shard_map/level0_up/pallas_call | solution.py:182
  176.1 11.2 %level0_up.3 = f32[40,40,512]{2,1,0:T(8,128)} custom-call(s32[2]{0:T(128)} %pad_add_fusion.1.off_ref, f32[40,40,512]{2,1,0:T(8,128)} %level0_up.2.u_ref.ulo_ref.uhi_ref, f32[40,40,512]{2,1,0:T(8,128)} %level0_up.2.u_ref.ulo_ref.uhi_ref, f32[40,40,512]{2,1,0:T(8,128)} %level0_up.2.u_ref.ulo_ref.uhi_ref, ...), custom_call_target="tpu_custom_call" | custom-call | flops 36864000 | bytes 13107200 | tf_op jit(solution)/shard_map/level0_up/pallas_call | solution.py:182
  187.3 3.4 %slice.876 = f32[32,32,512]{2,1,0:T(8,128)} slice(f32[40,40,512]{2,1,0:T(8,128)} %level0_up.3), slice={[4:36], [4:36], [0:512]} | slice | bytes 4194304 | tf_op jit(solution)/shard_map/level0_up/slice | solution.py:28
  (70 shorter events, 3.8 us)
Async XLA Ops:
  0.0 8.6 %copy-start.1 = (f32[32,32,512]{2,1,0:T(8,128)S(1)}, f32[32,32,512]{2,1,0:T(8,128)}, u32[]{:S(2)}) copy-start(f32[32,32,512]{2,1,0:T(8,128)} %param.5) | copy-start | bytes 6291460
  2.9 12.9 %collective-permute-start = (f32[3,4,32,512]{3,2,1,0:T(8,128)}, f32[3,4,32,512]{3,2,1,0:T(8,128)S(1)}, u32[]{:S(2)}, u32[]{:S(2)}) collective-permute-start(f32[3,4,32,512]{3,2,1,0:T(8,128)} %get-tuple-element.7), channel_id=1, source_target_pairs={{0,16},{16,32},{32,48},{48,64},{64,80},{80,96},{96,112},{1,17},{17... | collective-permute-start | bytes 2359304 | tf_op jit(solution)/shard_map/level0_down/ppermute | solution.py:19
  6.5 13.6 %collective-permute-start.1 = (f32[3,4,32,512]{3,2,1,0:T(8,128)}, f32[3,4,32,512]{3,2,1,0:T(8,128)}, u32[]{:S(2)}, u32[]{:S(2)}) collective-permute-start(f32[3,4,32,512]{3,2,1,0:T(8,128)} %get-tuple-element.8), channel_id=1, source_target_pairs={{16,0},{32,16},{48,32},{64,48},{80,64},{96,80},{112,96},{17,1},{33... | collective-permute-start | bytes 2359304 | tf_op jit(solution)/shard_map/level0_down/ppermute | solution.py:20
  15.1 13.8 %copy-start.4 = (f32[16,16,512]{2,1,0:T(8,128)S(1)}, f32[16,16,512]{2,1,0:T(8,128)}, u32[]{:S(2)}) copy-start(f32[16,16,512]{2,1,0:T(8,128)} %reduce_sum.37) | copy-start | bytes 1572868
  20.2 32.6 %copy-start.2 = (f32[32,32,512]{2,1,0:T(8,128)S(1)}, f32[32,32,512]{2,1,0:T(8,128)}, u32[]{:S(2)}) copy-start(f32[32,32,512]{2,1,0:T(8,128)} %param.4) | copy-start | bytes 6291460
  20.2 32.6 %copy-start.3 = (f32[32,32,512]{2,1,0:T(8,128)S(1)}, f32[32,32,512]{2,1,0:T(8,128)}, u32[]{:S(2)}) copy-start(f32[32,32,512]{2,1,0:T(8,128)} %param.3) | copy-start | bytes 6291460
  22.5 24.9 %collective-permute-start.2 = (f32[3,40,4,512]{3,2,1,0:T(4,128)S(1)}, f32[3,40,4,512]{3,2,1,0:T(4,128)S(1)}, u32[]{:S(2)}, u32[]{:S(2)}) collective-permute-start(f32[3,40,4,512]{3,2,1,0:T(4,128)S(1)} %get-tuple-element.5), channel_id=1, source_target_pairs={{0,1},{1,2},{2,3},{3,4},{4,5},{5,6},{6,7},{7,8},{8,9},{9,10},{10,1... | collective-permute-start | bytes 2949128 | tf_op jit(solution)/shard_map/level0_down/ppermute | solution.py:19
  25.7 27.0 %collective-permute-start.3 = (f32[3,40,4,512]{3,2,1,0:T(4,128)S(1)}, f32[3,40,4,512]{3,2,1,0:T(4,128)S(1)}, u32[]{:S(2)}, u32[]{:S(2)}) collective-permute-start(f32[3,40,4,512]{3,2,1,0:T(4,128)S(1)} %get-tuple-element.6), channel_id=1, source_target_pairs={{1,0},{2,1},{3,2},{4,3},{5,4},{6,5},{7,6},{8,7},{9,8},{10,9},{11,1... | collective-permute-start | bytes 2949128 | tf_op jit(solution)/shard_map/level0_down/ppermute | solution.py:20
  101.5 6.1 %collective-permute-start.4 = (f32[2,4,16,256]{3,2,1,0:T(8,128)S(1)}, f32[2,4,16,256]{3,2,1,0:T(8,128)S(1)}, u32[]{:S(2)}, u32[]{:S(2)}) collective-permute-start(f32[2,4,16,256]{3,2,1,0:T(8,128)S(1)} %get-tuple-element.33), channel_id=1, source_target_pairs={{0,16},{16,32},{32,48},{48,64},{64,80},{80,96},{96,112},{1,17},{17... | collective-permute-start | bytes 393224 | tf_op jit(solution)/shard_map/level1_down/ppermute | solution.py:19
  105.0 6.3 %collective-permute-start.5 = (f32[2,4,16,256]{3,2,1,0:T(8,128)S(1)}, f32[2,4,16,256]{3,2,1,0:T(8,128)S(1)}, u32[]{:S(2)}, u32[]{:S(2)}) collective-permute-start(f32[2,4,16,256]{3,2,1,0:T(8,128)S(1)} %get-tuple-element.34), channel_id=1, source_target_pairs={{16,0},{32,16},{48,32},{64,48},{80,64},{96,80},{112,96},{17,1},{33... | collective-permute-start | bytes 393224 | tf_op jit(solution)/shard_map/level1_down/ppermute | solution.py:20
  111.4 7.8 %collective-permute-start.6 = (f32[2,24,4,256]{3,2,1,0:T(4,128)S(1)}, f32[2,24,4,256]{3,2,1,0:T(4,128)S(1)}, u32[]{:S(2)}, u32[]{:S(2)}) collective-permute-start(f32[2,24,4,256]{3,2,1,0:T(4,128)S(1)} %get-tuple-element.11), channel_id=1, source_target_pairs={{0,1},{1,2},{2,3},{3,4},{4,5},{5,6},{6,7},{7,8},{8,9},{9,10},{10,1... | collective-permute-start | bytes 589832 | tf_op jit(solution)/shard_map/level1_down/ppermute | solution.py:19
  113.3 9.6 %collective-permute-start.7 = (f32[2,24,4,256]{3,2,1,0:T(4,128)S(1)}, f32[2,24,4,256]{3,2,1,0:T(4,128)S(1)}, u32[]{:S(2)}, u32[]{:S(2)}) collective-permute-start(f32[2,24,4,256]{3,2,1,0:T(4,128)S(1)} %get-tuple-element.12), channel_id=1, source_target_pairs={{1,0},{2,1},{3,2},{4,3},{5,4},{6,5},{7,6},{8,7},{9,8},{10,9},{11,1... | collective-permute-start | bytes 589832 | tf_op jit(solution)/shard_map/level1_down/ppermute | solution.py:20
  127.8 5.4 %collective-permute-start.8 = (f32[2,5,8,128]{3,2,1,0:T(8,128)S(1)}, f32[2,5,8,128]{3,2,1,0:T(8,128)S(1)}, u32[]{:S(2)}, u32[]{:S(2)}) collective-permute-start(f32[2,5,8,128]{3,2,1,0:T(8,128)S(1)} %get-tuple-element.75), channel_id=1, source_target_pairs={{0,16},{16,32},{32,48},{48,64},{64,80},{80,96},{96,112},{1,17},{17... | collective-permute-start | bytes 122888 | tf_op jit(solution)/shard_map/level2/ppermute | solution.py:19
  131.1 5.3 %collective-permute-start.9 = (f32[2,5,8,128]{3,2,1,0:T(8,128)S(1)}, f32[2,5,8,128]{3,2,1,0:T(8,128)S(1)}, u32[]{:S(2)}, u32[]{:S(2)}) collective-permute-start(f32[2,5,8,128]{3,2,1,0:T(8,128)S(1)} %get-tuple-element.76), channel_id=1, source_target_pairs={{16,0},{32,16},{48,32},{64,48},{80,64},{96,80},{112,96},{17,1},{33... | collective-permute-start | bytes 122888 | tf_op jit(solution)/shard_map/level2/ppermute | solution.py:20
  136.4 6.2 %collective-permute-start.10 = (f32[2,18,5,128]{3,2,1,0:T(8,128)S(1)}, f32[2,18,5,128]{3,2,1,0:T(8,128)S(1)}, u32[]{:S(2)}, u32[]{:S(2)}) collective-permute-start(f32[2,18,5,128]{3,2,1,0:T(8,128)S(1)} %get-tuple-element.61), channel_id=1, source_target_pairs={{0,1},{1,2},{2,3},{3,4},{4,5},{5,6},{6,7},{7,8},{8,9},{9,10},{10,1... | collective-permute-start | bytes 276488 | tf_op jit(solution)/shard_map/level2/ppermute | solution.py:19
  138.4 8.3 %collective-permute-start.11 = (f32[2,18,5,128]{3,2,1,0:T(8,128)S(1)}, f32[2,18,5,128]{3,2,1,0:T(8,128)S(1)}, u32[]{:S(2)}, u32[]{:S(2)}) collective-permute-start(f32[2,18,5,128]{3,2,1,0:T(8,128)S(1)} %get-tuple-element.62), channel_id=1, source_target_pairs={{1,0},{2,1},{3,2},{4,3},{5,4},{6,5},{7,6},{8,7},{9,8},{10,9},{11,1... | collective-permute-start | bytes 276488 | tf_op jit(solution)/shard_map/level2/ppermute | solution.py:20
  150.0 0.9 copy-start.5
  150.0 1.0 copy-start.6
  155.7 4.8 %copy-start = (f32[40,40,512]{2,1,0:T(8,128)S(1)}, f32[40,40,512]{2,1,0:T(8,128)}, u32[]{:S(2)}) copy-start(f32[40,40,512]{2,1,0:T(8,128)} %level0_down.4.u_ref.ulo_ref.uhi_ref) | copy-start | bytes 9830404
where the time goes:
time: 192 us; the launch traced here: 191 us
  Pallas kernels  55.8 us (29%)
  waiting for transfers between devices  44.9 us (23%)
  starting transfers between devices  32.4 us (17%)
  other arithmetic  28.9 us (15%)
  local copies, waits for them, and re-layouts  23.1 us (12%)
  matrix products  4.9 us (3%)
    pallas_call x5, Pallas kernels, plane_step(): pl.pallas_call(kernel, grid_spec=grid_spec, out_shape=jax.ShapeDtypeStruc...  55.8 us
    ppermute x6, waiting for transfers between devices, exchange(): lax.ppermute(lax.slice_in_dim(stack, 0, width, axis=dim), axis, backward)  24.3 us
    ppermute x6, waiting for transfers between devices, exchange(): lax.ppermute(lax.slice_in_dim(stack, size - width, size, axis=dim), axis,...  20.6 us
    ppermute x6, starting transfers between devices, exchange(): lax.ppermute(lax.slice_in_dim(stack, size - width, size, axis=dim), axis,...  17.5 us
    ppermute x6, starting transfers between devices, exchange(): lax.ppermute(lax.slice_in_dim(stack, 0, width, axis=dim), axis, backward)  15 us
    reduce_sum x4, other arithmetic, restrict_mean(): field.reshape(field.shape[0] // 2, 2, field.shape[1] // 2, 2, depth)  7.53 us
    concatenate x4, other arithmetic, exchange(): stack = jnp.concatenate([low, stack, high], axis=dim)  7.29 us
    slice x2, local copies, waits for them, and re-layouts, trim(): return field[k:-k, k:-k]  5.57 us
  transfers between devices with their start and end apart: 12, of which 10 were waited for; matrix products, arithmetic and copies ran while one was open for 5% of the time, Pallas kernels for 0%

commit v1 on v0

--- a/solution.py
+++ b/solution.py
@@ -107,18 +107,12 @@
                   scale, extent_x, extent_y, residual):
     step = pl.program_id(0)
     _, depth_y, depth_z = o_ref.shape
+    tiles = depth_y // 8
     half = 0.5 * scale
-    y_idx = lax.broadcasted_iota(jnp.int32, (depth_y, depth_z), 0) + off_ref[1]
-    z_idx = lax.broadcasted_iota(jnp.int32, (depth_y, depth_z), 1)
-    y_ok = (y_idx >= 0) & (y_idx < extent_y)
+    z_idx = lax.broadcasted_iota(jnp.int32, (8, depth_z), 1)
     z_first = z_idx == 0
     z_last = z_idx == depth_z - 1
-
-    def y_lo(a):
-        return pltpu.roll(a, 1, 0)
-
-    def y_hi(a):
-        return pltpu.roll(a, depth_y - 1, 0)
+    row_idx = lax.broadcasted_iota(jnp.int32, (8, depth_z), 0)
 
     def z_lo(a):
         return jnp.where(z_first, 0.0, pltpu.roll(a, 1, 1))
@@ -126,30 +120,43 @@
     def z_hi(a):
         return jnp.where(z_last, 0.0, pltpu.roll(a, depth_z - 1, 1))
 
+    def rows(ref, plane, t, shift):
+        if shift == 0:
+            return ref[plane, pl.ds(8 * t, 8), :]
+        if shift < 0 and t == 0:
+            return pltpu.roll(ref[plane, pl.ds(0, 8), :], 1, 0)
+        if shift > 0 and t == tiles - 1:
+            return pltpu.roll(ref[plane, pl.ds(8 * t, 8), :], 7, 0)
+        return ref[plane, pl.ds(8 * t + shift, 8), :]
+
     for p in range(CHUNK):
-        km = klo_ref[0] if p == 0 else k_ref[p - 1]
-        kp = khi_ref[0] if p == CHUNK - 1 else k_ref[p + 1]
-        kc = k_ref[p]
-        um = ulo_ref[0] if p == 0 else u_ref[p - 1]
-        up = uhi_ref[0] if p == CHUNK - 1 else u_ref[p + 1]
-        uc = u_ref[p]
-        wxm = (kc + km) * half
-        wxp = (kp + kc) * half
-        wym = (kc + y_lo(kc)) * half
-        wyp = (y_hi(kc) + kc) * half
-        wzm = (kc + z_lo(kc)) * half
-        wzp = (z_hi(kc) + kc) * half
-        diagonal = wxm + wxp + wym + wyp + wzm + wzp
-        beside = wxm * um + wxp * up
-        beside = beside + wym * y_lo(uc) + wyp * y_hi(uc)
-        beside = beside + wzm * z_lo(uc) + wzp * z_hi(uc)
-        image = diagonal * uc - beside
-        if residual:
-            o_ref[p] = b_ref[p] - image
-        else:
-            x_idx = off_ref[0] + step * CHUNK + p
-            ok = y_ok & (x_idx >= 0) & (x_idx < extent_x)
-            o_ref[p] = jnp.where(ok, uc + damping * (b_ref[p] - image) / diagonal, 0.0)
+        k_m = (klo_ref, 0) if p == 0 else (k_ref, p - 1)
+        k_p = (khi_ref, 0) if p == CHUNK - 1 else (k_ref, p + 1)
+        u_m = (ulo_ref, 0) if p == 0 else (u_ref, p - 1)
+        u_p = (uhi_ref, 0) if p == CHUNK - 1 else (u_ref, p + 1)
+        x_idx = off_ref[0] + step * CHUNK + p
+        x_ok = (x_idx >= 0) & (x_idx < extent_x)
+        for t in range(tiles):
+            kc = rows(k_ref, p, t, 0)
+            uc = rows(u_ref, p, t, 0)
+            sxm = kc + rows(k_m[0], k_m[1], t, 0)
+            sxp = rows(k_p[0], k_p[1], t, 0) + kc
+            sym = kc + rows(k_ref, p, t, -1)
+            syp = rows(k_ref, p, t, 1) + kc
+            szm = kc + z_lo(kc)
+            szp = z_hi(kc) + kc
+            total = sxm + sxp + sym + syp + szm + szp
+            beside = sxm * rows(u_m[0], u_m[1], t, 0) + sxp * rows(u_p[0], u_p[1], t, 0)
+            beside = beside + sym * rows(u_ref, p, t, -1) + syp * rows(u_ref, p, t, 1)
+            beside = beside + szm * z_lo(uc) + szp * z_hi(uc)
+            image = (total * uc - beside) * half
+            if residual:
+                o_ref[p, pl.ds(8 * t, 8), :] = b_ref[p, pl.ds(8 * t, 8), :] - image
+            else:
+                y_idx = off_ref[1] + 8 * t + row_idx
+                ok = x_ok & (y_idx >= 0) & (y_idx < extent_y)
+                fresh = uc + damping * (b_ref[p, pl.ds(8 * t, 8), :] - image) / (total * half)
+                o_ref[p, pl.ds(8 * t, 8), :] = jnp.where(ok, fresh, 0.0)
 
 
 def plane_step(offsets, u, b, k, scale, extent_x, extent_y, residual=False):

time: 192 us -> 188 us (0.979)
  Pallas kernels: 55.8 us -> 52.3 us
    pallas_call x5, Pallas kernels: 55.8 us -> 52.3 us  [plane_step(): pl.pallas_call(kernel, grid_spec=grid_spec, out_shape=jax.ShapeDtypeStruc...]
where the time goes in v1:
time: 188 us; the launch traced here: 187 us
  Pallas kernels  52.3 us (28%)
  waiting for transfers between devices  44.9 us (24%)
  starting transfers between devices  32.4 us (17%)
  other arithmetic  28.9 us (15%)
  local copies, waits for them, and re-layouts  23.1 us (12%)
  matrix products  4.9 us (3%)
    pallas_call x5, Pallas kernels, plane_step(): pl.pallas_call(kernel, grid_spec=grid_spec, out_shape=jax.ShapeDtypeStruc...  52.3 us
    ppermute x6, waiting for transfers between devices, exchange(): lax.ppermute(lax.slice_in_dim(stack, 0, width, axis=dim), axis, backward)  24.3 us
    ppermute x6, waiting for transfers between devices, exchange(): lax.ppermute(lax.slice_in_dim(stack, size - width, size, axis=dim), axis,...  20.6 us
    ppermute x6, starting transfers between devices, exchange(): lax.ppermute(lax.slice_in_dim(stack, size - width, size, axis=dim), axis,...  17.5 us
    ppermute x6, starting transfers between devices, exchange(): lax.ppermute(lax.slice_in_dim(stack, 0, width, axis=dim), axis, backward)  15 us
    reduce_sum x4, other arithmetic, restrict_mean(): field.reshape(field.shape[0] // 2, 2, field.shape[1] // 2, 2, depth)  7.53 us
    concatenate x4, other arithmetic, exchange(): stack = jnp.concatenate([low, stack, high], axis=dim)  7.29 us
    slice x2, local copies, waits for them, and re-layouts, trim(): return field[k:-k, k:-k]  5.57 us
  transfers between devices with their start and end apart: 12, of which 10 were waited for; matrix products, arithmetic and copies ran while one was open for 5% of the time, Pallas kernels for 0%

profile of v1, /device:TPU:27, one launch (start us, length us, event | category | flops | bytes accessed | tf_op | source)
XLA Modules:
  0.0 187.2 jit_solution(6874121898249533154)
XLA Ops:
  0.0 2.8 %pad_maximum_fusion.9 = (f32[3,4,32,512]{3,2,1,0:T(8,128)}, f32[3,4,32,512]{3,2,1,0:T(8,128)}) fusion(f32[1,32,32,512]{3,2,1,0:T(8,128)} %bitcast.41, f32[1,32,32,512]{3,2,1,0:T(8,128)} %bitcast.44, f32[1,32,32,512]{3,2,1,0:T(8,128)} %bitcast.47), kind=kLoop, calls=%fused_computation.12 | loop fusion | flops 786432 | bytes 7864320 | tf_op jit(solution)/shard_map/level0_down/slice | solution.py:19
  2.9 3.7 %collective-permute-start = (f32[3,4,32,512]{3,2,1,0:T(8,128)}, f32[3,4,32,512]{3,2,1,0:T(8,128)S(1)}, u32[]{:S(2)}, u32[]{:S(2)}) collective-permute-start(f32[3,4,32,512]{3,2,1,0:T(8,128)} %get-tuple-element.7), channel_id=1, source_target_pairs={{0,16},{16,32},{32,48},{48,64},{64,80},{80,96},{96,112},{1,17},{17... | collective-permute-start | bytes 2359304 | tf_op jit(solution)/shard_map/level0_down/ppermute | solution.py:19
  6.5 1.9 %collective-permute-start.1 = (f32[3,4,32,512]{3,2,1,0:T(8,128)}, f32[3,4,32,512]{3,2,1,0:T(8,128)}, u32[]{:S(2)}, u32[]{:S(2)}) collective-permute-start(f32[3,4,32,512]{3,2,1,0:T(8,128)} %get-tuple-element.8), channel_id=1, source_target_pairs={{16,0},{32,16},{48,32},{64,48},{80,64},{96,80},{112,96},{17,1},{33... | collective-permute-start | bytes 2359304 | tf_op jit(solution)/shard_map/level0_down/ppermute | solution.py:20
  8.7 2.2 %reshape.403 = f32[16,2,16,2,512]{4,3,2,1,0:T(2,128)} reshape(f32[32,32,512]{2,1,0:T(8,128)S(1)} %copy-done.1) | data formatting | bytes 4194304 | tf_op jit(solution)/shard_map/level0_down/reshape | solution.py:83
  10.9 4.0 %reduce_sum.37 = f32[16,16,512]{2,1,0:T(8,128)} reduce(f32[16,2,16,2,512]{4,3,2,1,0:T(2,128)} %reshape.403, f32[]{:T(128)} %constant.162.clone.1), dimensions={1,3}, to_apply=%region_1.2 | reduce | flops 393216 | bytes 2621444 | tf_op jit(solution)/shard_map/level0_down/reduce_sum | solution.py:83
  15.1 0.7 collective-permute-done
  15.8 4.4 %collective-permute-done.1 = f32[3,4,32,512]{3,2,1,0:T(8,128)} collective-permute-done((f32[3,4,32,512]{3,2,1,0:T(8,128)}, f32[3,4,32,512]{3,2,1,0:T(8,128)}, u32[]{:S(2)}, u32[]{:S(2)}) %collective-permute-start.1) | collective-permute-done | bytes 786464 | tf_op jit(solution)/shard_map/level0_down/ppermute | solution.py:20
  20.2 2.4 %pad_maximum_fusion.6 = (f32[3,40,4,512]{3,2,1,0:T(4,128)S(1)}, f32[3,40,4,512]{3,2,1,0:T(4,128)S(1)}) fusion(f32[3,4,32,512]{3,2,1,0:T(8,128)} %collective-permute-done.1, f32[3,4,32,512]{3,2,1,0:T(8,128)S(1)} %collective-permute-done, f32[1,32,32,512]{3,2,1,0:T(8,128)S(1)} %bitcast.42, f32[1,32,32,512]{3,2,1,0:T(8,128)} %bitcast.45, ...), kind=kLoop, calls=%fused_computation.9 | loop fusion | flops 1966080 | bytes 9830400 | tf_op jit(solution)/shard_map/level0_down/slice | solution.py:19
  22.5 3.2 %collective-permute-start.2 = (f32[3,40,4,512]{3,2,1,0:T(4,128)S(1)}, f32[3,40,4,512]{3,2,1,0:T(4,128)S(1)}, u32[]{:S(2)}, u32[]{:S(2)}) collective-permute-start(f32[3,40,4,512]{3,2,1,0:T(4,128)S(1)} %get-tuple-element.5), channel_id=1, source_target_pairs={{0,1},{1,2},{2,3},{3,4},{4,5},{5,6},{6,7},{7,8},{8,9},{9,10},{10,1... | collective-permute-start | bytes 2949128 | tf_op jit(solution)/shard_map/level0_down/ppermute | solution.py:19
  25.7 2.3 %collective-permute-start.3 = (f32[3,40,4,512]{3,2,1,0:T(4,128)S(1)}, f32[3,40,4,512]{3,2,1,0:T(4,128)S(1)}, u32[]{:S(2)}, u32[]{:S(2)}) collective-permute-start(f32[3,40,4,512]{3,2,1,0:T(4,128)S(1)} %get-tuple-element.6), channel_id=1, source_target_pairs={{1,0},{2,1},{3,2},{4,3},{5,4},{6,5},{7,6},{8,7},{9,8},{10,9},{11,1... | collective-permute-start | bytes 2949128 | tf_op jit(solution)/shard_map/level0_down/ppermute | solution.py:20
  28.0 0.7 pad_add_fusion.1.off_ref
  28.9 0.8 fusion.12
  29.7 17.7 %collective-permute-done.2 = f32[3,40,4,512]{3,2,1,0:T(4,128)S(1)} collective-permute-done((f32[3,40,4,512]{3,2,1,0:T(4,128)S(1)}, f32[3,40,4,512]{3,2,1,0:T(4,128)S(1)}, u32[]{:S(2)}, u32[]{:S(2)}) %collective-permute-start.2) | collective-permute-done | bytes 983072 | tf_op jit(solution)/shard_map/level0_down/ppermute | solution.py:19
  47.4 5.3 %collective-permute-done.3 = f32[3,40,4,512]{3,2,1,0:T(4,128)S(1)} collective-permute-done((f32[3,40,4,512]{3,2,1,0:T(4,128)S(1)}, f32[3,40,4,512]{3,2,1,0:T(4,128)S(1)}, u32[]{:S(2)}, u32[]{:S(2)}) %collective-permute-start.3) | collective-permute-done | bytes 983072 | tf_op jit(solution)/shard_map/level0_down/ppermute | solution.py:20
  52.7 7.0 %pad_maximum_fusion.u_ref.ulo_ref.uhi_ref.b_ref.k_ref.klo_ref.khi_ref = f32[3,40,40,512]{3,2,1,0:T(8,128)} fusion(f32[3,40,4,512]{3,2,1,0:T(4,128)S(1)} %collective-permute-done.3, f32[3,4,32,512]{3,2,1,0:T(8,128)} %collective-permute-done.1, f32[1,32,32,512]{3,2,1,0:T(8,128)S(1)} %bitcast.43, f32[1,32,32,512]{3,2,1,0:T(8,128)S(1)} %bitcast.46, ...), kind=kLoop, calls=%fused_computation | loop fusion | flops 14745600 | bytes 19660800 | tf_op jit(solution)/shard_map/level0_down/concatenate | solution.py:21
  59.8 10.5 %level0_down.3.u_ref.ulo_ref.uhi_ref = f32[40,40,512]{2,1,0:T(8,128)} custom-call(s32[2]{0:T(128)} %pad_add_fusion.1.off_ref, f32[3,40,40,512]{3,2,1,0:T(8,128)} %pad_maximum_fusion.u_ref.ulo_ref.uhi_ref.b_ref.k_ref.klo_ref.khi_ref, f32[3,40,40,512]{3,2,1,0:T(8,128)} %pad_maximum_fusion.u_ref.ulo_ref.uhi_ref.b_ref.k_ref.klo_ref.khi_ref, ...), custom_call_target="tpu_custom_call" | custom-call | flops 36864000 | bytes 13107200 | tf_op jit(solution)/shard_map/level0_down/pallas_call | solution.py:189
  70.3 10.6 %level0_down.4.u_ref.ulo_ref.uhi_ref = f32[40,40,512]{2,1,0:T(8,128)} custom-call(s32[2]{0:T(128)} %pad_add_fusion.1.off_ref, f32[40,40,512]{2,1,0:T(8,128)} %level0_down.3.u_ref.ulo_ref.uhi_ref, f32[40,40,512]{2,1,0:T(8,128)} %level0_down.3.u_ref.ulo_ref.uhi_ref, f32[40,40,512]{2,1,0:T(8,128)} %level0_down.3.u_ref.ulo_ref.uhi_ref, ...), custom_call_target="tpu_custom_call" | custom-call | flops 36864000 | bytes 13107200 | tf_op jit(solution)/shard_map/level0_down/pallas_call | solution.py:189
  80.9 10.0 %level0_down.5 = f32[40,40,512]{2,1,0:T(8,128)} custom-call(s32[2]{0:T(128)} %pad_add_fusion.1.off_ref, f32[40,40,512]{2,1,0:T(8,128)} %level0_down.4.u_ref.ulo_ref.uhi_ref, f32[40,40,512]{2,1,0:T(8,128)} %level0_down.4.u_ref.ulo_ref.uhi_ref, f32[40,40,512]{2,1,0:T(8,128)} %level0_down.4.u_ref.ulo_ref.uhi_ref, ...), custom_call_target="tpu_custom_call" | custom-call | flops 36864000 | bytes 13107200 | tf_op jit(solution)/shard_map/level0_down/pallas_call | solution.py:189
  90.9 2.1 %slice.734 = f32[32,32,512]{2,1,0:T(8,128)S(1)} slice(f32[40,40,512]{2,1,0:T(8,128)} %level0_down.5), slice={[4:36], [4:36], [0:512]} | slice | bytes 4194304 | tf_op jit(solution)/shard_map/level0_down/slice | solution.py:28
  93.1 2.2 %reshape.402 = f32[16,2,16,2,512]{4,3,2,1,0:T(2,128)} reshape(f32[32,32,512]{2,1,0:T(8,128)S(1)} %slice.734) | data formatting | bytes 4194304 | tf_op jit(solution)/shard_map/level0_down/reshape | solution.py:83
  95.3 3.2 %reduce_sum.36 = f32[16,16,512]{2,1,0:T(8,128)S(1)} reduce(f32[16,2,16,2,512]{4,3,2,1,0:T(2,128)} %reshape.402, f32[]{:T(128)} %constant.162.clone.1), dimensions={1,3}, to_apply=%region_0.0 | reduce | flops 393216 | bytes 2621444 | tf_op jit(solution)/shard_map/level0_down/reduce_sum | solution.py:83
  98.5 0.8 fusion.14
  99.3 3.5 %collective-permute-start.4 = (f32[2,4,16,256]{3,2,1,0:T(8,128)S(1)}, f32[2,4,16,256]{3,2,1,0:T(8,128)S(1)}, u32[]{:S(2)}, u32[]{:S(2)}) collective-permute-start(f32[2,4,16,256]{3,2,1,0:T(8,128)S(1)} %get-tuple-element.33), channel_id=1, source_target_pairs={{0,16},{16,32},{32,48},{48,64},{64,80},{80,96},{96,112},{1,17},{17... | collective-permute-start | bytes 393224 | tf_op jit(solution)/shard_map/level1_down/ppermute | solution.py:19
  102.8 1.9 %collective-permute-start.5 = (f32[2,4,16,256]{3,2,1,0:T(8,128)S(1)}, f32[2,4,16,256]{3,2,1,0:T(8,128)S(1)}, u32[]{:S(2)}, u32[]{:S(2)}) collective-permute-start(f32[2,4,16,256]{3,2,1,0:T(8,128)S(1)} %get-tuple-element.34), channel_id=1, source_target_pairs={{16,0},{32,16},{48,32},{64,48},{80,64},{96,80},{112,96},{17,1},{33... | collective-permute-start | bytes 393224 | tf_op jit(solution)/shard_map/level1_down/ppermute | solution.py:20
  104.7 0.1 reshape.405
  104.9 0.2 reduce_sum.39
  105.1 0.4 convolution_bitcast_fusion
  105.4 3.6 %collective-permute-done.5 = f32[2,4,16,256]{3,2,1,0:T(8,128)S(1)} collective-permute-done((f32[2,4,16,256]{3,2,1,0:T(8,128)S(1)}, f32[2,4,16,256]{3,2,1,0:T(8,128)S(1)}, u32[]{:S(2)}, u32[]{:S(2)}) %collective-permute-start.5) | collective-permute-done | bytes 131104 | tf_op jit(solution)/shard_map/level1_down/ppermute | solution.py:20
  109.1 1.9 %collective-permute-start.6 = (f32[2,24,4,256]{3,2,1,0:T(4,128)S(1)}, f32[2,24,4,256]{3,2,1,0:T(4,128)S(1)}, u32[]{:S(2)}, u32[]{:S(2)}) collective-permute-start(f32[2,24,4,256]{3,2,1,0:T(4,128)S(1)} %get-tuple-element.11), channel_id=1, source_target_pairs={{0,1},{1,2},{2,3},{3,4},{4,5},{5,6},{6,7},{7,8},{8,9},{9,10},{10,1... | collective-permute-start | bytes 589832 | tf_op jit(solution)/shard_map/level1_down/ppermute | solution.py:19
  111.1 3.6 %collective-permute-start.7 = (f32[2,24,4,256]{3,2,1,0:T(4,128)S(1)}, f32[2,24,4,256]{3,2,1,0:T(4,128)S(1)}, u32[]{:S(2)}, u32[]{:S(2)}) collective-permute-start(f32[2,24,4,256]{3,2,1,0:T(4,128)S(1)} %get-tuple-element.12), channel_id=1, source_target_pairs={{1,0},{2,1},{3,2},{4,3},{5,4},{6,5},{7,6},{8,7},{9,8},{10,9},{11,1... | collective-permute-start | bytes 589832 | tf_op jit(solution)/shard_map/level1_down/ppermute | solution.py:20
  114.7 2.2 %collective-permute-done.6 = f32[2,24,4,256]{3,2,1,0:T(4,128)S(1)} collective-permute-done((f32[2,24,4,256]{3,2,1,0:T(4,128)S(1)}, f32[2,24,4,256]{3,2,1,0:T(4,128)S(1)}, u32[]{:S(2)}, u32[]{:S(2)}) %collective-permute-start.6) | collective-permute-done | bytes 196640 | tf_op jit(solution)/shard_map/level1_down/ppermute | solution.py:19
  116.9 3.7 %collective-permute-done.7 = f32[2,24,4,256]{3,2,1,0:T(4,128)S(1)} collective-permute-done((f32[2,24,4,256]{3,2,1,0:T(4,128)S(1)}, f32[2,24,4,256]{3,2,1,0:T(4,128)S(1)}, u32[]{:S(2)}, u32[]{:S(2)}) %collective-permute-start.7) | collective-permute-done | bytes 196640 | tf_op jit(solution)/shard_map/level1_down/ppermute | solution.py:20
  120.6 0.2 pad_maximum_fusion.1
  120.9 0.2 fusion.230
  121.3 0.6 fusion.5
  121.9 0.2 fusion.233
  122.2 0.2 fusion.229
  122.6 1.2 fusion.39
  124.3 0.6 fusion.66
  125.0 0.2 reduce_sum.38
  125.2 0.4 convolution_bitcast_fusion.1
  125.6 3.3 %collective-permute-start.8 = (f32[2,5,8,128]{3,2,1,0:T(8,128)S(1)}, f32[2,5,8,128]{3,2,1,0:T(8,128)S(1)}, u32[]{:S(2)}, u32[]{:S(2)}) collective-permute-start(f32[2,5,8,128]{3,2,1,0:T(8,128)S(1)} %get-tuple-element.75), channel_id=1, source_target_pairs={{0,16},{16,32},{32,48},{48,64},{64,80},{80,96},{96,112},{1,17},{17... | collective-permute-start | bytes 122888 | tf_op jit(solution)/shard_map/level2/ppermute | solution.py:19
  128.9 1.9 %collective-permute-start.9 = (f32[2,5,8,128]{3,2,1,0:T(8,128)S(1)}, f32[2,5,8,128]{3,2,1,0:T(8,128)S(1)}, u32[]{:S(2)}, u32[]{:S(2)}) collective-permute-start(f32[2,5,8,128]{3,2,1,0:T(8,128)S(1)} %get-tuple-element.76), channel_id=1, source_target_pairs={{16,0},{32,16},{48,32},{64,48},{80,64},{96,80},{112,96},{17,1},{33... | collective-permute-start | bytes 122888 | tf_op jit(solution)/shard_map/level2/ppermute | solution.py:20
  130.8 0.2 fusion.225
  131.0 3.2 %collective-permute-done.9 = f32[2,5,8,128]{3,2,1,0:T(8,128)S(1)} collective-permute-done((f32[2,5,8,128]{3,2,1,0:T(8,128)S(1)}, f32[2,5,8,128]{3,2,1,0:T(8,128)S(1)}, u32[]{:S(2)}, u32[]{:S(2)}) %collective-permute-start.9) | collective-permute-done | bytes 40992 | tf_op jit(solution)/shard_map/level2/ppermute | solution.py:20
  134.2 1.9 %collective-permute-start.10 = (f32[2,18,5,128]{3,2,1,0:T(8,128)S(1)}, f32[2,18,5,128]{3,2,1,0:T(8,128)S(1)}, u32[]{:S(2)}, u32[]{:S(2)}) collective-permute-start(f32[2,18,5,128]{3,2,1,0:T(8,128)S(1)} %get-tuple-element.61), channel_id=1, source_target_pairs={{0,1},{1,2},{2,3},{3,4},{4,5},{5,6},{6,7},{7,8},{8,9},{9,10},{10,1... | collective-permute-start | bytes 276488 | tf_op jit(solution)/shard_map/level2/ppermute | solution.py:19
  136.2 3.4 %collective-permute-start.11 = (f32[2,18,5,128]{3,2,1,0:T(8,128)S(1)}, f32[2,18,5,128]{3,2,1,0:T(8,128)S(1)}, u32[]{:S(2)}, u32[]{:S(2)}) collective-permute-start(f32[2,18,5,128]{3,2,1,0:T(8,128)S(1)} %get-tuple-element.62), channel_id=1, source_target_pairs={{1,0},{2,1},{3,2},{4,3},{5,4},{6,5},{7,6},{8,7},{9,8},{10,9},{11,1... | collective-permute-start | bytes 276488 | tf_op jit(solution)/shard_map/level2/ppermute | solution.py:20
  139.5 0.8 fusion.224
  140.4 4.0 %collective-permute-done.11 = f32[2,18,5,128]{3,2,1,0:T(8,128)S(1)} collective-permute-done((f32[2,18,5,128]{3,2,1,0:T(8,128)S(1)}, f32[2,18,5,128]{3,2,1,0:T(8,128)S(1)}, u32[]{:S(2)}, u32[]{:S(2)}) %collective-permute-start.11) | collective-permute-done | bytes 92192 | tf_op jit(solution)/shard_map/level2/ppermute | solution.py:20
  144.8 0.2 fusion.105
  145.4 0.3 fusion.137
  146.1 0.3 fusion.158
  146.7 0.5 fusion.110
  147.4 0.3 reshape.407
  147.8 0.2 fusion.234
  148.2 0.5 copy-done.5
  148.8 2.1 %fusion.10 = f32[18,18,512]{2,1,0:T(8,128)S(1)} fusion(f32[20,20,256]{2,1,0:T(8,128)S(1)} %add.699, f32[24,24,256]{2,1,0:T(8,128)S(1)} %get-tuple-element.9, f32[18,18,255]{2,1,0:T(8,128)S(1)} %get-tuple-element.36, f32[18,18,1]{2,1,0:T(8,128)S(1)} %get-tuple-element.38, f32[18,18,1]{2,1,0:T(8,128)S(1)} %get-tuple-element.37, ...), kind=kOutput, calls=%fused_computation.32 | convolution fusion | flops 513567744 | bytes 8192512 | tf_op jit(solution)/shard_map/level0_up/dot_general | solution.py:97
  150.9 0.2 broadcast_in_dim.195
  151.1 2.4 %broadcast_in_dim.196 = f32[36,18,2,512]{3,2,1,0:T(2,128)} broadcast(f32[36,18,512]{2,1,0:T(8,128)S(1)} %bitcast.50), dimensions={0,1,3} | broadcast | bytes 3981312 | tf_op jit(solution)/shard_map/level0_up/broadcast_in_dim | solution.py:100
  153.5 4.8 %reshape.409 = f32[36,36,512]{2,1,0:T(8,128)} reshape(f32[36,18,2,512]{3,2,1,0:T(2,128)} %broadcast_in_dim.196) | data formatting | bytes 5308416 | tf_op jit(solution)/shard_map/level0_up/reshape | solution.py:100
  158.4 4.3 %pad_add_fusion.u_ref.ulo_ref.uhi_ref = f32[40,40,512]{2,1,0:T(8,128)} fusion(f32[40,40,512]{2,1,0:T(8,128)S(1)} %copy-done, f32[36,36,512]{2,1,0:T(8,128)} %reshape.409), kind=kLoop, calls=%fused_computation.1 | loop fusion | flops 819200 | bytes 9207808 | tf_op jit(solution)/shard_map/level0_up/add | solution.py:234
  162.6 10.6 %level0_up.2.u_ref.ulo_ref.uhi_ref = f32[40,40,512]{2,1,0:T(8,128)} custom-call(s32[2]{0:T(128)} %pad_add_fusion.1.off_ref, f32[40,40,512]{2,1,0:T(8,128)} %pad_add_fusion.u_ref.ulo_ref.uhi_ref, f32[40,40,512]{2,1,0:T(8,128)} %pad_add_fusion.u_ref.ulo_ref.uhi_ref, f32[40,40,512]{2,1,0:T(8,128)} %pad_add_fusion.u_ref.ulo_ref.uhi_ref, ...), custom_call_target="tpu_custom_call" | custom-call | flops 36864000 | bytes 13107200 | tf_op jit(solution)/shard_map/level0_up/pallas_call | solution.py:189
  173.2 10.5 %level0_up.3 = f32[40,40,512]{2,1,0:T(8,128)} custom-call(s32[2]{0:T(128)} %pad_add_fusion.1.off_ref, f32[40,40,512]{2,1,0:T(8,128)} %level0_up.2.u_ref.ulo_ref.uhi_ref, f32[40,40,512]{2,1,0:T(8,128)} %level0_up.2.u_ref.ulo_ref.uhi_ref, f32[40,40,512]{2,1,0:T(8,128)} %level0_up.2.u_ref.ulo_ref.uhi_ref, ...), custom_call_target="tpu_custom_call" | custom-call | flops 36864000 | bytes 13107200 | tf_op jit(solution)/shard_map/level0_up/pallas_call | solution.py:189
  183.7 3.4 %slice.876 = f32[32,32,512]{2,1,0:T(8,128)} slice(f32[40,40,512]{2,1,0:T(8,128)} %level0_up.3), slice={[4:36], [4:36], [0:512]} | slice | bytes 4194304 | tf_op jit(solution)/shard_map/level0_up/slice | solution.py:28
  (70 shorter events, 3.8 us)
Async XLA Ops:
  0.0 8.6 %copy-start.1 = (f32[32,32,512]{2,1,0:T(8,128)S(1)}, f32[32,32,512]{2,1,0:T(8,128)}, u32[]{:S(2)}) copy-start(f32[32,32,512]{2,1,0:T(8,128)} %param.5) | copy-start | bytes 6291460
  2.9 12.9 %collective-permute-start = (f32[3,4,32,512]{3,2,1,0:T(8,128)}, f32[3,4,32,512]{3,2,1,0:T(8,128)S(1)}, u32[]{:S(2)}, u32[]{:S(2)}) collective-permute-start(f32[3,4,32,512]{3,2,1,0:T(8,128)} %get-tuple-element.7), channel_id=1, source_target_pairs={{0,16},{16,32},{32,48},{48,64},{64,80},{80,96},{96,112},{1,17},{17... | collective-permute-start | bytes 2359304 | tf_op jit(solution)/shard_map/level0_down/ppermute | solution.py:19
  6.5 13.6 %collective-permute-start.1 = (f32[3,4,32,512]{3,2,1,0:T(8,128)}, f32[3,4,32,512]{3,2,1,0:T(8,128)}, u32[]{:S(2)}, u32[]{:S(2)}) collective-permute-start(f32[3,4,32,512]{3,2,1,0:T(8,128)} %get-tuple-element.8), channel_id=1, source_target_pairs={{16,0},{32,16},{48,32},{64,48},{80,64},{96,80},{112,96},{17,1},{33... | collective-permute-start | bytes 2359304 | tf_op jit(solution)/shard_map/level0_down/ppermute | solution.py:20
  15.1 13.8 %copy-start.4 = (f32[16,16,512]{2,1,0:T(8,128)S(1)}, f32[16,16,512]{2,1,0:T(8,128)}, u32[]{:S(2)}) copy-start(f32[16,16,512]{2,1,0:T(8,128)} %reduce_sum.37) | copy-start | bytes 1572868
  20.2 32.6 %copy-start.2 = (f32[32,32,512]{2,1,0:T(8,128)S(1)}, f32[32,32,512]{2,1,0:T(8,128)}, u32[]{:S(2)}) copy-start(f32[32,32,512]{2,1,0:T(8,128)} %param.4) | copy-start | bytes 6291460
  20.2 32.6 %copy-start.3 = (f32[32,32,512]{2,1,0:T(8,128)S(1)}, f32[32,32,512]{2,1,0:T(8,128)}, u32[]{:S(2)}) copy-start(f32[32,32,512]{2,1,0:T(8,128)} %param.3) | copy-start | bytes 6291460
  22.5 24.9 %collective-permute-start.2 = (f32[3,40,4,512]{3,2,1,0:T(4,128)S(1)}, f32[3,40,4,512]{3,2,1,0:T(4,128)S(1)}, u32[]{:S(2)}, u32[]{:S(2)}) collective-permute-start(f32[3,40,4,512]{3,2,1,0:T(4,128)S(1)} %get-tuple-element.5), channel_id=1, source_target_pairs={{0,1},{1,2},{2,3},{3,4},{4,5},{5,6},{6,7},{7,8},{8,9},{9,10},{10,1... | collective-permute-start | bytes 2949128 | tf_op jit(solution)/shard_map/level0_down/ppermute | solution.py:19
  25.7 27.0 %collective-permute-start.3 = (f32[3,40,4,512]{3,2,1,0:T(4,128)S(1)}, f32[3,40,4,512]{3,2,1,0:T(4,128)S(1)}, u32[]{:S(2)}, u32[]{:S(2)}) collective-permute-start(f32[3,40,4,512]{3,2,1,0:T(4,128)S(1)} %get-tuple-element.6), channel_id=1, source_target_pairs={{1,0},{2,1},{3,2},{4,3},{5,4},{6,5},{7,6},{8,7},{9,8},{10,9},{11,1... | collective-permute-start | bytes 2949128 | tf_op jit(solution)/shard_map/level0_down/ppermute | solution.py:20
  99.3 6.1 %collective-permute-start.4 = (f32[2,4,16,256]{3,2,1,0:T(8,128)S(1)}, f32[2,4,16,256]{3,2,1,0:T(8,128)S(1)}, u32[]{:S(2)}, u32[]{:S(2)}) collective-permute-start(f32[2,4,16,256]{3,2,1,0:T(8,128)S(1)} %get-tuple-element.33), channel_id=1, source_target_pairs={{0,16},{16,32},{32,48},{48,64},{64,80},{80,96},{96,112},{1,17},{17... | collective-permute-start | bytes 393224 | tf_op jit(solution)/shard_map/level1_down/ppermute | solution.py:19
  102.8 6.3 %collective-permute-start.5 = (f32[2,4,16,256]{3,2,1,0:T(8,128)S(1)}, f32[2,4,16,256]{3,2,1,0:T(8,128)S(1)}, u32[]{:S(2)}, u32[]{:S(2)}) collective-permute-start(f32[2,4,16,256]{3,2,1,0:T(8,128)S(1)} %get-tuple-element.34), channel_id=1, source_target_pairs={{16,0},{32,16},{48,32},{64,48},{80,64},{96,80},{112,96},{17,1},{33... | collective-permute-start | bytes 393224 | tf_op jit(solution)/shard_map/level1_down/ppermute | solution.py:20
  109.1 7.8 %collective-permute-start.6 = (f32[2,24,4,256]{3,2,1,0:T(4,128)S(1)}, f32[2,24,4,256]{3,2,1,0:T(4,128)S(1)}, u32[]{:S(2)}, u32[]{:S(2)}) collective-permute-start(f32[2,24,4,256]{3,2,1,0:T(4,128)S(1)} %get-tuple-element.11), channel_id=1, source_target_pairs={{0,1},{1,2},{2,3},{3,4},{4,5},{5,6},{6,7},{7,8},{8,9},{9,10},{10,1... | collective-permute-start | bytes 589832 | tf_op jit(solution)/shard_map/level1_down/ppermute | solution.py:19
  111.1 9.6 %collective-permute-start.7 = (f32[2,24,4,256]{3,2,1,0:T(4,128)S(1)}, f32[2,24,4,256]{3,2,1,0:T(4,128)S(1)}, u32[]{:S(2)}, u32[]{:S(2)}) collective-permute-start(f32[2,24,4,256]{3,2,1,0:T(4,128)S(1)} %get-tuple-element.12), channel_id=1, source_target_pairs={{1,0},{2,1},{3,2},{4,3},{5,4},{6,5},{7,6},{8,7},{9,8},{10,9},{11,1... | collective-permute-start | bytes 589832 | tf_op jit(solution)/shard_map/level1_down/ppermute | solution.py:20
  125.6 5.4 %collective-permute-start.8 = (f32[2,5,8,128]{3,2,1,0:T(8,128)S(1)}, f32[2,5,8,128]{3,2,1,0:T(8,128)S(1)}, u32[]{:S(2)}, u32[]{:S(2)}) collective-permute-start(f32[2,5,8,128]{3,2,1,0:T(8,128)S(1)} %get-tuple-element.75), channel_id=1, source_target_pairs={{0,16},{16,32},{32,48},{48,64},{64,80},{80,96},{96,112},{1,17},{17... | collective-permute-start | bytes 122888 | tf_op jit(solution)/shard_map/level2/ppermute | solution.py:19
  128.9 5.3 %collective-permute-start.9 = (f32[2,5,8,128]{3,2,1,0:T(8,128)S(1)}, f32[2,5,8,128]{3,2,1,0:T(8,128)S(1)}, u32[]{:S(2)}, u32[]{:S(2)}) collective-permute-start(f32[2,5,8,128]{3,2,1,0:T(8,128)S(1)} %get-tuple-element.76), channel_id=1, source_target_pairs={{16,0},{32,16},{48,32},{64,48},{80,64},{96,80},{112,96},{17,1},{33... | collective-permute-start | bytes 122888 | tf_op jit(solution)/shard_map/level2/ppermute | solution.py:20
  134.2 6.2 %collective-permute-start.10 = (f32[2,18,5,128]{3,2,1,0:T(8,128)S(1)}, f32[2,18,5,128]{3,2,1,0:T(8,128)S(1)}, u32[]{:S(2)}, u32[]{:S(2)}) collective-permute-start(f32[2,18,5,128]{3,2,1,0:T(8,128)S(1)} %get-tuple-element.61), channel_id=1, source_target_pairs={{0,1},{1,2},{2,3},{3,4},{4,5},{5,6},{6,7},{7,8},{8,9},{9,10},{10,1... | collective-permute-start | bytes 276488 | tf_op jit(solution)/shard_map/level2/ppermute | solution.py:19
  136.2 8.3 %collective-permute-start.11 = (f32[2,18,5,128]{3,2,1,0:T(8,128)S(1)}, f32[2,18,5,128]{3,2,1,0:T(8,128)S(1)}, u32[]{:S(2)}, u32[]{:S(2)}) collective-permute-start(f32[2,18,5,128]{3,2,1,0:T(8,128)S(1)} %get-tuple-element.62), channel_id=1, source_target_pairs={{1,0},{2,1},{3,2},{4,3},{5,4},{6,5},{7,6},{8,7},{9,8},{10,9},{11,1... | collective-permute-start | bytes 276488 | tf_op jit(solution)/shard_map/level2/ppermute | solution.py:20
  147.7 0.9 copy-start.5
  147.7 1.0 copy-start.6
  153.5 4.8 %copy-start = (f32[40,40,512]{2,1,0:T(8,128)S(1)}, f32[40,40,512]{2,1,0:T(8,128)}, u32[]{:S(2)}) copy-start(f32[40,40,512]{2,1,0:T(8,128)} %level0_down.4.u_ref.ulo_ref.uhi_ref) | copy-start | bytes 9830404

commit v2 on v1

--- a/solution.py
+++ b/solution.py
@@ -104,10 +104,11 @@
 
 
 def _plane_kernel(off_ref, u_ref, ulo_ref, uhi_ref, b_ref, k_ref, klo_ref, khi_ref, o_ref, *,
-                  scale, extent_x, extent_y, residual):
+                  scale, extent_x, extent_y, residual, chunk, inner):
     step = pl.program_id(0)
-    _, depth_y, depth_z = o_ref.shape
-    tiles = depth_y // 8
+    depth_y, depth_z = u_ref.shape[-2], u_ref.shape[-1]
+    first = 4 if inner else 0
+    tiles = (depth_y - 2 * first) // 8
     half = 0.5 * scale
     z_idx = lax.broadcasted_iota(jnp.int32, (8, depth_z), 1)
     z_first = z_idx == 0
@@ -121,20 +122,21 @@
         return jnp.where(z_last, 0.0, pltpu.roll(a, depth_z - 1, 1))
 
     def rows(ref, plane, t, shift):
+        start = first + 8 * t
         if shift == 0:
-            return ref[plane, pl.ds(8 * t, 8), :]
-        if shift < 0 and t == 0:
+            return ref[plane, pl.ds(start, 8), :]
+        if shift < 0 and start == 0:
             return pltpu.roll(ref[plane, pl.ds(0, 8), :], 1, 0)
-        if shift > 0 and t == tiles - 1:
-            return pltpu.roll(ref[plane, pl.ds(8 * t, 8), :], 7, 0)
-        return ref[plane, pl.ds(8 * t + shift, 8), :]
-
-    for p in range(CHUNK):
+        if shift > 0 and start + 8 == depth_y:
+            return pltpu.roll(ref[plane, pl.ds(start, 8), :], 7, 0)
+        return ref[plane, pl.ds(start + shift, 8), :]
+
+    for p in range(chunk):
         k_m = (klo_ref, 0) if p == 0 else (k_ref, p - 1)
-        k_p = (khi_ref, 0) if p == CHUNK - 1 else (k_ref, p + 1)
+        k_p = (khi_ref, 0) if p == chunk - 1 else (k_ref, p + 1)
         u_m = (ulo_ref, 0) if p == 0 else (u_ref, p - 1)
-        u_p = (uhi_ref, 0) if p == CHUNK - 1 else (u_ref, p + 1)
-        x_idx = off_ref[0] + step * CHUNK + p
+        u_p = (uhi_ref, 0) if p == chunk - 1 else (u_ref, p + 1)
+        x_idx = off_ref[0] + first + step * chunk + p
         x_ok = (x_idx >= 0) & (x_idx < extent_x)
         for t in range(tiles):
             kc = rows(k_ref, p, t, 0)
@@ -150,46 +152,53 @@
             beside = beside + sym * rows(u_ref, p, t, -1) + syp * rows(u_ref, p, t, 1)
             beside = beside + szm * z_lo(uc) + szp * z_hi(uc)
             image = (total * uc - beside) * half
+            rhs = rows(b_ref, p, t, 0)
+            out_rows = pl.ds(8 * t if inner else first + 8 * t, 8)
             if residual:
-                o_ref[p, pl.ds(8 * t, 8), :] = b_ref[p, pl.ds(8 * t, 8), :] - image
+                o_ref[p, out_rows, :] = rhs - image
             else:
-                y_idx = off_ref[1] + 8 * t + row_idx
+                y_idx = off_ref[1] + first + 8 * t + row_idx
                 ok = x_ok & (y_idx >= 0) & (y_idx < extent_y)
-                fresh = uc + damping * (b_ref[p, pl.ds(8 * t, 8), :] - image) / (total * half)
-                o_ref[p, pl.ds(8 * t, 8), :] = jnp.where(ok, fresh, 0.0)
-
-
-def plane_step(offsets, u, b, k, scale, extent_x, extent_y, residual=False):
+                fresh = uc + damping * (rhs - image) / (total * half)
+                o_ref[p, out_rows, :] = jnp.where(ok, fresh, 0.0)
+
+
+def plane_step(offsets, u, b, k, scale, extent_x, extent_y, residual=False, inner=False):
     (u_arr, u_i), (b_arr, b_i), (k_arr, k_i) = u, b, k
     depth_x, depth_y, depth_z = u_arr.shape[-3:]
-    chunks = depth_x // CHUNK
+    chunk = 4 if inner else CHUNK
+    lead_blocks = 1 if inner else 0
+    chunks = (depth_x - 8 * lead_blocks) // chunk
 
     def spec(arr, idx, kind):
         lead = (None,) if arr.ndim == 4 else ()
         pre = (idx,) if arr.ndim == 4 else ()
         if kind == "main":
-            return pl.BlockSpec(lead + (CHUNK, depth_y, depth_z), lambda i, off: pre + (i, 0, 0))
+            return pl.BlockSpec(lead + (chunk, depth_y, depth_z),
+                                lambda i, off: pre + (i + lead_blocks, 0, 0))
         if kind == "lo":
             return pl.BlockSpec(lead + (1, depth_y, depth_z),
-                                lambda i, off: pre + (jnp.maximum(i * CHUNK - 1, 0), 0, 0))
+                                lambda i, off: pre + (jnp.maximum((i + lead_blocks) * chunk - 1, 0), 0, 0))
         return pl.BlockSpec(lead + (1, depth_y, depth_z),
-                            lambda i, off: pre + (jnp.minimum(i * CHUNK + CHUNK, depth_x - 1), 0, 0))
-
-    kernel = functools.partial(_plane_kernel, scale=scale, extent_x=extent_x,
-                               extent_y=extent_y, residual=residual)
+                            lambda i, off: pre + (jnp.minimum((i + lead_blocks) * chunk + chunk, depth_x - 1), 0, 0))
+
+    kernel = functools.partial(_plane_kernel, scale=scale, extent_x=extent_x, extent_y=extent_y,
+                               residual=residual, chunk=chunk, inner=inner)
+    out_x = depth_x - 8 if inner else depth_x
+    out_y = depth_y - 8 if inner else depth_y
     grid_spec = pltpu.PrefetchScalarGridSpec(
         num_scalar_prefetch=1,
         grid=(chunks,),
         in_specs=[spec(u_arr, u_i, "main"), spec(u_arr, u_i, "lo"), spec(u_arr, u_i, "hi"),
                   spec(b_arr, b_i, "main"),
                   spec(k_arr, k_i, "main"), spec(k_arr, k_i, "lo"), spec(k_arr, k_i, "hi")],
-        out_specs=pl.BlockSpec((CHUNK, depth_y, depth_z), lambda i, off: (i, 0, 0)),
-    )
-    cells = depth_x * depth_y * depth_z
+        out_specs=pl.BlockSpec((chunk, out_y, depth_z), lambda i, off: (i, 0, 0)),
+    )
+    cells = out_x * out_y * depth_z
     return pl.pallas_call(
         kernel,
         grid_spec=grid_spec,
-        out_shape=jax.ShapeDtypeStruct((depth_x, depth_y, depth_z), jnp.float32),
+        out_shape=jax.ShapeDtypeStruct((out_x, out_y, depth_z), jnp.float32),
         compiler_params=pltpu.CompilerParams(dimension_semantics=("arbitrary",)),
         cost_estimate=pl.CostEstimate(flops=45 * cells, transcendentals=0, bytes_accessed=4 * 4 * cells),
     )(offsets, u_arr, u_arr, u_arr, b_arr, k_arr, k_arr, k_arr)
@@ -206,8 +215,9 @@
         offsets = jnp.stack([lax.axis_index("row") * nx - 4, lax.axis_index("col") * ny - 4]).astype(jnp.int32)
         u1 = plane_step(offsets, (fine, 0), (fine, 1), (fine, 2), 1.0, extent_x, extent_y)
         u2 = plane_step(offsets, (u1, None), (fine, 1), (fine, 2), 1.0, extent_x, extent_y)
-        residual = plane_step(offsets, (u2, None), (fine, 1), (fine, 2), 1.0, extent_x, extent_y, residual=True)
-        mid_rhs = restrict_mean(trim(residual, 4))
+        residual = plane_step(offsets, (u2, None), (fine, 1), (fine, 2), 1.0, extent_x, extent_y,
+                              residual=True, inner=True)
+        mid_rhs = restrict_mean(residual)
         mid_cond = restrict_mean(conductance)
 
     with jax.named_scope("level1_down"):
@@ -233,7 +243,7 @@
     with jax.named_scope("level0_up"):
         u3 = u2 + jnp.pad(prolong_copy(e1), ((2, 2), (2, 2), (0, 0)))
         u4 = plane_step(offsets, (u3, None), (fine, 1), (fine, 2), 1.0, extent_x, extent_y)
-        u5 = trim(plane_step(offsets, (u4, None), (fine, 1), (fine, 2), 1.0, extent_x, extent_y), 4)
+        u5 = plane_step(offsets, (u4, None), (fine, 1), (fine, 2), 1.0, extent_x, extent_y, inner=True)
     return u5
 
 

time: 188 us -> 183 us (0.973)
  local copies, waits for them, and re-layouts: 23.1 us -> 17.8 us
    slice x2 -> x0, local copies, waits for them, and re-layouts: 5.57 us -> none  [trim(): return field[k:-k, k:-k]]
  transfers between devices with their start and end apart: 12 -> 12, of which waited for: 10 -> 10; matrix products, arithmetic and copies ran while one was open for 5% -> 6% of each run, Pallas kernels for 0% -> 0%
where the time goes in v2:
time: 183 us; the launch traced here: 182 us
  Pallas kernels  53.8 us (29%)
  waiting for transfers between devices  44.9 us (25%)
  starting transfers between devices  32.4 us (18%)
  other arithmetic  27.3 us (15%)
  local copies, waits for them, and re-layouts  17.8 us (10%)
  matrix products  4.9 us (3%)
    pallas_call x5, Pallas kernels, plane_step(): pl.pallas_call(kernel, grid_spec=grid_spec, out_shape=jax.ShapeDtypeStruc...  53.8 us
    ppermute x6, waiting for transfers between devices, exchange(): lax.ppermute(lax.slice_in_dim(stack, 0, width, axis=dim), axis, backward)  24.3 us
    ppermute x6, waiting for transfers between devices, exchange(): lax.ppermute(lax.slice_in_dim(stack, size - width, size, axis=dim), axis,...  20.6 us
    ppermute x6, starting transfers between devices, exchange(): lax.ppermute(lax.slice_in_dim(stack, size - width, size, axis=dim), axis,...  17.5 us
    ppermute x6, starting transfers between devices, exchange(): lax.ppermute(lax.slice_in_dim(stack, 0, width, axis=dim), axis, backward)  15 us
    concatenate x4, other arithmetic, exchange(): stack = jnp.concatenate([low, stack, high], axis=dim)  7.29 us
    reduce_sum x4, other arithmetic, restrict_mean(): field.reshape(field.shape[0] // 2, 2, field.shape[1] // 2, 2, depth)  5.89 us
    slice x4, other arithmetic, exchange(): lax.slice_in_dim(stack, size - width, size, axis=dim)  5.3 us
  transfers between devices with their start and end apart: 12, of which 10 were waited for; matrix products, arithmetic and copies ran while one was open for 6% of the time, Pallas kernels for 0%

profile of v2, /device:TPU:27, one launch (start us, length us, event | category | flops | bytes accessed | tf_op | source)
XLA Modules:
  0.0 181.7 jit_solution(2866620278976088941)
XLA Ops:
  0.0 2.8 %pad_maximum_fusion.9 = (f32[3,4,32,512]{3,2,1,0:T(8,128)}, f32[3,4,32,512]{3,2,1,0:T(8,128)}) fusion(f32[1,32,32,512]{3,2,1,0:T(8,128)} %bitcast.41, f32[1,32,32,512]{3,2,1,0:T(8,128)} %bitcast.44, f32[1,32,32,512]{3,2,1,0:T(8,128)} %bitcast.47), kind=kLoop, calls=%fused_computation.12 | loop fusion | flops 786432 | bytes 7864320 | tf_op jit(solution)/shard_map/level0_down/slice | solution.py:19
  2.9 3.7 %collective-permute-start = (f32[3,4,32,512]{3,2,1,0:T(8,128)}, f32[3,4,32,512]{3,2,1,0:T(8,128)S(1)}, u32[]{:S(2)}, u32[]{:S(2)}) collective-permute-start(f32[3,4,32,512]{3,2,1,0:T(8,128)} %get-tuple-element.7), channel_id=1, source_target_pairs={{0,16},{16,32},{32,48},{48,64},{64,80},{80,96},{96,112},{1,17},{17... | collective-permute-start | bytes 2359304 | tf_op jit(solution)/shard_map/level0_down/ppermute | solution.py:19
  6.5 1.9 %collective-permute-start.1 = (f32[3,4,32,512]{3,2,1,0:T(8,128)}, f32[3,4,32,512]{3,2,1,0:T(8,128)}, u32[]{:S(2)}, u32[]{:S(2)}) collective-permute-start(f32[3,4,32,512]{3,2,1,0:T(8,128)} %get-tuple-element.8), channel_id=1, source_target_pairs={{16,0},{32,16},{48,32},{64,48},{80,64},{96,80},{112,96},{17,1},{33... | collective-permute-start | bytes 2359304 | tf_op jit(solution)/shard_map/level0_down/ppermute | solution.py:20
  8.7 2.2 %reshape.403 = f32[16,2,16,2,512]{4,3,2,1,0:T(2,128)} reshape(f32[32,32,512]{2,1,0:T(8,128)S(1)} %copy-done.1) | data formatting | bytes 4194304 | tf_op jit(solution)/shard_map/level0_down/reshape | solution.py:83
  10.9 4.0 %reduce_sum.37 = f32[16,16,512]{2,1,0:T(8,128)} reduce(f32[16,2,16,2,512]{4,3,2,1,0:T(2,128)} %reshape.403, f32[]{:T(128)} %constant.162.clone.1), dimensions={1,3}, to_apply=%region_1.2 | reduce | flops 393216 | bytes 2621444 | tf_op jit(solution)/shard_map/level0_down/reduce_sum | solution.py:83
  15.1 0.7 collective-permute-done
  15.8 4.4 %collective-permute-done.1 = f32[3,4,32,512]{3,2,1,0:T(8,128)} collective-permute-done((f32[3,4,32,512]{3,2,1,0:T(8,128)}, f32[3,4,32,512]{3,2,1,0:T(8,128)}, u32[]{:S(2)}, u32[]{:S(2)}) %collective-permute-start.1) | collective-permute-done | bytes 786464 | tf_op jit(solution)/shard_map/level0_down/ppermute | solution.py:20
  20.2 2.4 %pad_maximum_fusion.6 = (f32[3,40,4,512]{3,2,1,0:T(4,128)S(1)}, f32[3,40,4,512]{3,2,1,0:T(4,128)S(1)}) fusion(f32[3,4,32,512]{3,2,1,0:T(8,128)} %collective-permute-done.1, f32[3,4,32,512]{3,2,1,0:T(8,128)S(1)} %collective-permute-done, f32[1,32,32,512]{3,2,1,0:T(8,128)S(1)} %bitcast.42, f32[1,32,32,512]{3,2,1,0:T(8,128)} %bitcast.45, ...), kind=kLoop, calls=%fused_computation.9 | loop fusion | flops 1966080 | bytes 9830400 | tf_op jit(solution)/shard_map/level0_down/slice | solution.py:19
  22.5 3.2 %collective-permute-start.2 = (f32[3,40,4,512]{3,2,1,0:T(4,128)S(1)}, f32[3,40,4,512]{3,2,1,0:T(4,128)S(1)}, u32[]{:S(2)}, u32[]{:S(2)}) collective-permute-start(f32[3,40,4,512]{3,2,1,0:T(4,128)S(1)} %get-tuple-element.5), channel_id=1, source_target_pairs={{0,1},{1,2},{2,3},{3,4},{4,5},{5,6},{6,7},{7,8},{8,9},{9,10},{10,1... | collective-permute-start | bytes 2949128 | tf_op jit(solution)/shard_map/level0_down/ppermute | solution.py:19
  25.7 2.3 %collective-permute-start.3 = (f32[3,40,4,512]{3,2,1,0:T(4,128)S(1)}, f32[3,40,4,512]{3,2,1,0:T(4,128)S(1)}, u32[]{:S(2)}, u32[]{:S(2)}) collective-permute-start(f32[3,40,4,512]{3,2,1,0:T(4,128)S(1)} %get-tuple-element.6), channel_id=1, source_target_pairs={{1,0},{2,1},{3,2},{4,3},{5,4},{6,5},{7,6},{8,7},{9,8},{10,9},{11,1... | collective-permute-start | bytes 2949128 | tf_op jit(solution)/shard_map/level0_down/ppermute | solution.py:20
  28.0 0.7 pad_add_fusion.1.off_ref
  28.9 0.8 fusion.12
  29.7 17.7 %collective-permute-done.2 = f32[3,40,4,512]{3,2,1,0:T(4,128)S(1)} collective-permute-done((f32[3,40,4,512]{3,2,1,0:T(4,128)S(1)}, f32[3,40,4,512]{3,2,1,0:T(4,128)S(1)}, u32[]{:S(2)}, u32[]{:S(2)}) %collective-permute-start.2) | collective-permute-done | bytes 983072 | tf_op jit(solution)/shard_map/level0_down/ppermute | solution.py:19
  47.4 5.3 %collective-permute-done.3 = f32[3,40,4,512]{3,2,1,0:T(4,128)S(1)} collective-permute-done((f32[3,40,4,512]{3,2,1,0:T(4,128)S(1)}, f32[3,40,4,512]{3,2,1,0:T(4,128)S(1)}, u32[]{:S(2)}, u32[]{:S(2)}) %collective-permute-start.3) | collective-permute-done | bytes 983072 | tf_op jit(solution)/shard_map/level0_down/ppermute | solution.py:20
  52.7 7.0 %pad_maximum_fusion.u_ref.ulo_ref.uhi_ref.b_ref.k_ref.klo_ref.khi_ref = f32[3,40,40,512]{3,2,1,0:T(8,128)} fusion(f32[3,40,4,512]{3,2,1,0:T(4,128)S(1)} %collective-permute-done.3, f32[3,4,32,512]{3,2,1,0:T(8,128)} %collective-permute-done.1, f32[1,32,32,512]{3,2,1,0:T(8,128)S(1)} %bitcast.43, f32[1,32,32,512]{3,2,1,0:T(8,128)S(1)} %bitcast.46, ...), kind=kLoop, calls=%fused_computation | loop fusion | flops 14745600 | bytes 19660800 | tf_op jit(solution)/shard_map/level0_down/concatenate | solution.py:21
  59.8 10.5 %level0_down.3.u_ref.ulo_ref.uhi_ref = f32[40,40,512]{2,1,0:T(8,128)} custom-call(s32[2]{0:T(128)} %pad_add_fusion.1.off_ref, f32[3,40,40,512]{3,2,1,0:T(8,128)} %pad_maximum_fusion.u_ref.ulo_ref.uhi_ref.b_ref.k_ref.klo_ref.khi_ref, f32[3,40,40,512]{3,2,1,0:T(8,128)} %pad_maximum_fusion.u_ref.ulo_ref.uhi_ref.b_ref.k_ref.klo_ref.khi_ref, ...), custom_call_target="tpu_custom_call" | custom-call | flops 36864000 | bytes 13107200 | tf_op jit(solution)/shard_map/level0_down/pallas_call | solution.py:198
  70.3 10.6 %level0_down.4.u_ref.ulo_ref.uhi_ref = f32[40,40,512]{2,1,0:T(8,128)} custom-call(s32[2]{0:T(128)} %pad_add_fusion.1.off_ref, f32[40,40,512]{2,1,0:T(8,128)} %level0_down.3.u_ref.ulo_ref.uhi_ref, f32[40,40,512]{2,1,0:T(8,128)} %level0_down.3.u_ref.ulo_ref.uhi_ref, f32[40,40,512]{2,1,0:T(8,128)} %level0_down.3.u_ref.ulo_ref.uhi_ref, ...), custom_call_target="tpu_custom_call" | custom-call | flops 36864000 | bytes 13107200 | tf_op jit(solution)/shard_map/level0_down/pallas_call | solution.py:198
  80.9 10.8 %level0_down.5 = f32[32,32,512]{2,1,0:T(8,128)} custom-call(s32[2]{0:T(128)} %pad_add_fusion.1.off_ref, f32[40,40,512]{2,1,0:T(8,128)} %level0_down.4.u_ref.ulo_ref.uhi_ref, f32[40,40,512]{2,1,0:T(8,128)} %level0_down.4.u_ref.ulo_ref.uhi_ref, f32[40,40,512]{2,1,0:T(8,128)} %level0_down.4.u_ref.ulo_ref.uhi_ref, ...), custom_call_target="tpu_custom_call" | custom-call | flops 23592960 | bytes 8388608 | tf_op jit(solution)/shard_map/level0_down/pallas_call | solution.py:198
  91.7 2.5 %reshape.402 = f32[16,2,16,2,512]{4,3,2,1,0:T(2,128)S(1)} reshape(f32[32,32,512]{2,1,0:T(8,128)} %level0_down.5) | data formatting | bytes 4194304 | tf_op jit(solution)/shard_map/level0_down/reshape | solution.py:83
  94.2 1.5 reduce_sum.36
  95.7 0.8 fusion.14
  96.5 3.5 %collective-permute-start.4 = (f32[2,4,16,256]{3,2,1,0:T(8,128)S(1)}, f32[2,4,16,256]{3,2,1,0:T(8,128)S(1)}, u32[]{:S(2)}, u32[]{:S(2)}) collective-permute-start(f32[2,4,16,256]{3,2,1,0:T(8,128)S(1)} %get-tuple-element.33), channel_id=1, source_target_pairs={{0,16},{16,32},{32,48},{48,64},{64,80},{80,96},{96,112},{1,17},{17... | collective-permute-start | bytes 393224 | tf_op jit(solution)/shard_map/level1_down/ppermute | solution.py:19
  100.0 1.9 %collective-permute-start.5 = (f32[2,4,16,256]{3,2,1,0:T(8,128)S(1)}, f32[2,4,16,256]{3,2,1,0:T(8,128)S(1)}, u32[]{:S(2)}, u32[]{:S(2)}) collective-permute-start(f32[2,4,16,256]{3,2,1,0:T(8,128)S(1)} %get-tuple-element.34), channel_id=1, source_target_pairs={{16,0},{32,16},{48,32},{64,48},{80,64},{96,80},{112,96},{17,1},{33... | collective-permute-start | bytes 393224 | tf_op jit(solution)/shard_map/level1_down/ppermute | solution.py:20
  101.9 0.1 reshape.405
  102.1 0.2 reduce_sum.39
  102.3 0.4 convolution_bitcast_fusion
  102.7 3.6 %collective-permute-done.5 = f32[2,4,16,256]{3,2,1,0:T(8,128)S(1)} collective-permute-done((f32[2,4,16,256]{3,2,1,0:T(8,128)S(1)}, f32[2,4,16,256]{3,2,1,0:T(8,128)S(1)}, u32[]{:S(2)}, u32[]{:S(2)}) %collective-permute-start.5) | collective-permute-done | bytes 131104 | tf_op jit(solution)/shard_map/level1_down/ppermute | solution.py:20
  106.4 1.9 %collective-permute-start.6 = (f32[2,24,4,256]{3,2,1,0:T(4,128)S(1)}, f32[2,24,4,256]{3,2,1,0:T(4,128)S(1)}, u32[]{:S(2)}, u32[]{:S(2)}) collective-permute-start(f32[2,24,4,256]{3,2,1,0:T(4,128)S(1)} %get-tuple-element.11), channel_id=1, source_target_pairs={{0,1},{1,2},{2,3},{3,4},{4,5},{5,6},{6,7},{7,8},{8,9},{9,10},{10,1... | collective-permute-start | bytes 589832 | tf_op jit(solution)/shard_map/level1_down/ppermute | solution.py:19
  108.3 3.6 %collective-permute-start.7 = (f32[2,24,4,256]{3,2,1,0:T(4,128)S(1)}, f32[2,24,4,256]{3,2,1,0:T(4,128)S(1)}, u32[]{:S(2)}, u32[]{:S(2)}) collective-permute-start(f32[2,24,4,256]{3,2,1,0:T(4,128)S(1)} %get-tuple-element.12), channel_id=1, source_target_pairs={{1,0},{2,1},{3,2},{4,3},{5,4},{6,5},{7,6},{8,7},{9,8},{10,9},{11,1... | collective-permute-start | bytes 589832 | tf_op jit(solution)/shard_map/level1_down/ppermute | solution.py:20
  112.0 2.2 %collective-permute-done.6 = f32[2,24,4,256]{3,2,1,0:T(4,128)S(1)} collective-permute-done((f32[2,24,4,256]{3,2,1,0:T(4,128)S(1)}, f32[2,24,4,256]{3,2,1,0:T(4,128)S(1)}, u32[]{:S(2)}, u32[]{:S(2)}) %collective-permute-start.6) | collective-permute-done | bytes 196640 | tf_op jit(solution)/shard_map/level1_down/ppermute | solution.py:19
  114.1 3.7 %collective-permute-done.7 = f32[2,24,4,256]{3,2,1,0:T(4,128)S(1)} collective-permute-done((f32[2,24,4,256]{3,2,1,0:T(4,128)S(1)}, f32[2,24,4,256]{3,2,1,0:T(4,128)S(1)}, u32[]{:S(2)}, u32[]{:S(2)}) %collective-permute-start.7) | collective-permute-done | bytes 196640 | tf_op jit(solution)/shard_map/level1_down/ppermute | solution.py:20
  117.9 0.2 pad_maximum_fusion.1
  118.1 0.2 fusion.230
  118.5 0.6 fusion.5
  119.1 0.2 fusion.233
  119.5 0.2 fusion.229
  119.8 1.2 fusion.39
  121.5 0.6 fusion.66
  122.1 0.1 reshape.404
  122.2 0.2 reduce_sum.38
  122.4 0.4 convolution_bitcast_fusion.1
  122.8 3.3 %collective-permute-start.8 = (f32[2,5,8,128]{3,2,1,0:T(8,128)S(1)}, f32[2,5,8,128]{3,2,1,0:T(8,128)S(1)}, u32[]{:S(2)}, u32[]{:S(2)}) collective-permute-start(f32[2,5,8,128]{3,2,1,0:T(8,128)S(1)} %get-tuple-element.75), channel_id=1, source_target_pairs={{0,16},{16,32},{32,48},{48,64},{64,80},{80,96},{96,112},{1,17},{17... | collective-permute-start | bytes 122888 | tf_op jit(solution)/shard_map/level2/ppermute | solution.py:19
  126.1 1.9 %collective-permute-start.9 = (f32[2,5,8,128]{3,2,1,0:T(8,128)S(1)}, f32[2,5,8,128]{3,2,1,0:T(8,128)S(1)}, u32[]{:S(2)}, u32[]{:S(2)}) collective-permute-start(f32[2,5,8,128]{3,2,1,0:T(8,128)S(1)} %get-tuple-element.76), channel_id=1, source_target_pairs={{16,0},{32,16},{48,32},{64,48},{80,64},{96,80},{112,96},{17,1},{33... | collective-permute-start | bytes 122888 | tf_op jit(solution)/shard_map/level2/ppermute | solution.py:20
  128.0 0.2 fusion.225
  128.2 3.2 %collective-permute-done.9 = f32[2,5,8,128]{3,2,1,0:T(8,128)S(1)} collective-permute-done((f32[2,5,8,128]{3,2,1,0:T(8,128)S(1)}, f32[2,5,8,128]{3,2,1,0:T(8,128)S(1)}, u32[]{:S(2)}, u32[]{:S(2)}) %collective-permute-start.9) | collective-permute-done | bytes 40992 | tf_op jit(solution)/shard_map/level2/ppermute | solution.py:20
  131.4 1.9 %collective-permute-start.10 = (f32[2,18,5,128]{3,2,1,0:T(8,128)S(1)}, f32[2,18,5,128]{3,2,1,0:T(8,128)S(1)}, u32[]{:S(2)}, u32[]{:S(2)}) collective-permute-start(f32[2,18,5,128]{3,2,1,0:T(8,128)S(1)} %get-tuple-element.61), channel_id=1, source_target_pairs={{0,1},{1,2},{2,3},{3,4},{4,5},{5,6},{6,7},{7,8},{8,9},{9,10},{10,1... | collective-permute-start | bytes 276488 | tf_op jit(solution)/shard_map/level2/ppermute | solution.py:19
  133.4 3.4 %collective-permute-start.11 = (f32[2,18,5,128]{3,2,1,0:T(8,128)S(1)}, f32[2,18,5,128]{3,2,1,0:T(8,128)S(1)}, u32[]{:S(2)}, u32[]{:S(2)}) collective-permute-start(f32[2,18,5,128]{3,2,1,0:T(8,128)S(1)} %get-tuple-element.62), channel_id=1, source_target_pairs={{1,0},{2,1},{3,2},{4,3},{5,4},{6,5},{7,6},{8,7},{9,8},{10,9},{11,1... | collective-permute-start | bytes 276488 | tf_op jit(solution)/shard_map/level2/ppermute | solution.py:20
  136.7 0.8 fusion.224
  137.6 4.0 %collective-permute-done.11 = f32[2,18,5,128]{3,2,1,0:T(8,128)S(1)} collective-permute-done((f32[2,18,5,128]{3,2,1,0:T(8,128)S(1)}, f32[2,18,5,128]{3,2,1,0:T(8,128)S(1)}, u32[]{:S(2)}, u32[]{:S(2)}) %collective-permute-start.11) | collective-permute-done | bytes 92192 | tf_op jit(solution)/shard_map/level2/ppermute | solution.py:20
  142.0 0.2 fusion.105
  142.6 0.3 fusion.137
  143.3 0.3 fusion.158
  144.0 0.5 fusion.110
  144.5 0.1 broadcast_in_dim.191
  144.7 0.3 reshape.407
  145.1 0.2 fusion.234
  145.4 0.5 copy-done.5
  146.0 2.1 %fusion.10 = f32[18,18,512]{2,1,0:T(8,128)S(1)} fusion(f32[20,20,256]{2,1,0:T(8,128)S(1)} %add.699, f32[24,24,256]{2,1,0:T(8,128)S(1)} %get-tuple-element.9, f32[18,18,255]{2,1,0:T(8,128)S(1)} %get-tuple-element.36, f32[18,18,1]{2,1,0:T(8,128)S(1)} %get-tuple-element.38, f32[18,18,1]{2,1,0:T(8,128)S(1)} %get-tuple-element.37, ...), kind=kOutput, calls=%fused_computation.32 | convolution fusion | flops 513567744 | bytes 8192512 | tf_op jit(solution)/shard_map/level0_up/dot_general | solution.py:97
  148.1 0.2 broadcast_in_dim.195
  148.3 2.4 %broadcast_in_dim.196 = f32[36,18,2,512]{3,2,1,0:T(2,128)} broadcast(f32[36,18,512]{2,1,0:T(8,128)S(1)} %bitcast.50), dimensions={0,1,3} | broadcast | bytes 3981312 | tf_op jit(solution)/shard_map/level0_up/broadcast_in_dim | solution.py:100
  150.7 4.8 %reshape.409 = f32[36,36,512]{2,1,0:T(8,128)} reshape(f32[36,18,2,512]{3,2,1,0:T(2,128)} %broadcast_in_dim.196) | data formatting | bytes 5308416 | tf_op jit(solution)/shard_map/level0_up/reshape | solution.py:100
  155.6 4.3 %pad_add_fusion.u_ref.ulo_ref.uhi_ref = f32[40,40,512]{2,1,0:T(8,128)} fusion(f32[40,40,512]{2,1,0:T(8,128)S(1)} %copy-done, f32[36,36,512]{2,1,0:T(8,128)} %reshape.409), kind=kLoop, calls=%fused_computation.1 | loop fusion | flops 819200 | bytes 9207808 | tf_op jit(solution)/shard_map/level0_up/add | solution.py:244
  159.9 10.6 %level0_up.2.u_ref.ulo_ref.uhi_ref = f32[40,40,512]{2,1,0:T(8,128)} custom-call(s32[2]{0:T(128)} %pad_add_fusion.1.off_ref, f32[40,40,512]{2,1,0:T(8,128)} %pad_add_fusion.u_ref.ulo_ref.uhi_ref, f32[40,40,512]{2,1,0:T(8,128)} %pad_add_fusion.u_ref.ulo_ref.uhi_ref, f32[40,40,512]{2,1,0:T(8,128)} %pad_add_fusion.u_ref.ulo_ref.uhi_ref, ...), custom_call_target="tpu_custom_call" | custom-call | flops 36864000 | bytes 13107200 | tf_op jit(solution)/shard_map/level0_up/pallas_call | solution.py:198
  170.5 11.3 %level0_up.3 = f32[32,32,512]{2,1,0:T(8,128)} custom-call(s32[2]{0:T(128)} %pad_add_fusion.1.off_ref, f32[40,40,512]{2,1,0:T(8,128)} %level0_up.2.u_ref.ulo_ref.uhi_ref, f32[40,40,512]{2,1,0:T(8,128)} %level0_up.2.u_ref.ulo_ref.uhi_ref, f32[40,40,512]{2,1,0:T(8,128)} %level0_up.2.u_ref.ulo_ref.uhi_ref, ...), custom_call_target="tpu_custom_call" | custom-call | flops 23592960 | bytes 8388608 | tf_op jit(solution)/shard_map/level0_up/pallas_call | solution.py:198
  (68 shorter events, 3.5 us)
Async XLA Ops:
  0.0 8.6 %copy-start.1 = (f32[32,32,512]{2,1,0:T(8,128)S(1)}, f32[32,32,512]{2,1,0:T(8,128)}, u32[]{:S(2)}) copy-start(f32[32,32,512]{2,1,0:T(8,128)} %param.5) | copy-start | bytes 6291460
  2.9 12.9 %collective-permute-start = (f32[3,4,32,512]{3,2,1,0:T(8,128)}, f32[3,4,32,512]{3,2,1,0:T(8,128)S(1)}, u32[]{:S(2)}, u32[]{:S(2)}) collective-permute-start(f32[3,4,32,512]{3,2,1,0:T(8,128)} %get-tuple-element.7), channel_id=1, source_target_pairs={{0,16},{16,32},{32,48},{48,64},{64,80},{80,96},{96,112},{1,17},{17... | collective-permute-start | bytes 2359304 | tf_op jit(solution)/shard_map/level0_down/ppermute | solution.py:19
  6.5 13.6 %collective-permute-start.1 = (f32[3,4,32,512]{3,2,1,0:T(8,128)}, f32[3,4,32,512]{3,2,1,0:T(8,128)}, u32[]{:S(2)}, u32[]{:S(2)}) collective-permute-start(f32[3,4,32,512]{3,2,1,0:T(8,128)} %get-tuple-element.8), channel_id=1, source_target_pairs={{16,0},{32,16},{48,32},{64,48},{80,64},{96,80},{112,96},{17,1},{33... | collective-permute-start | bytes 2359304 | tf_op jit(solution)/shard_map/level0_down/ppermute | solution.py:20
  15.1 13.8 %copy-start.4 = (f32[16,16,512]{2,1,0:T(8,128)S(1)}, f32[16,16,512]{2,1,0:T(8,128)}, u32[]{:S(2)}) copy-start(f32[16,16,512]{2,1,0:T(8,128)} %reduce_sum.37) | copy-start | bytes 1572868
  20.2 32.6 %copy-start.2 = (f32[32,32,512]{2,1,0:T(8,128)S(1)}, f32[32,32,512]{2,1,0:T(8,128)}, u32[]{:S(2)}) copy-start(f32[32,32,512]{2,1,0:T(8,128)} %param.4) | copy-start | bytes 6291460
  20.2 32.6 %copy-start.3 = (f32[32,32,512]{2,1,0:T(8,128)S(1)}, f32[32,32,512]{2,1,0:T(8,128)}, u32[]{:S(2)}) copy-start(f32[32,32,512]{2,1,0:T(8,128)} %param.3) | copy-start | bytes 6291460
  22.5 24.9 %collective-permute-start.2 = (f32[3,40,4,512]{3,2,1,0:T(4,128)S(1)}, f32[3,40,4,512]{3,2,1,0:T(4,128)S(1)}, u32[]{:S(2)}, u32[]{:S(2)}) collective-permute-start(f32[3,40,4,512]{3,2,1,0:T(4,128)S(1)} %get-tuple-element.5), channel_id=1, source_target_pairs={{0,1},{1,2},{2,3},{3,4},{4,5},{5,6},{6,7},{7,8},{8,9},{9,10},{10,1... | collective-permute-start | bytes 2949128 | tf_op jit(solution)/shard_map/level0_down/ppermute | solution.py:19
  25.7 27.0 %collective-permute-start.3 = (f32[3,40,4,512]{3,2,1,0:T(4,128)S(1)}, f32[3,40,4,512]{3,2,1,0:T(4,128)S(1)}, u32[]{:S(2)}, u32[]{:S(2)}) collective-permute-start(f32[3,40,4,512]{3,2,1,0:T(4,128)S(1)} %get-tuple-element.6), channel_id=1, source_target_pairs={{1,0},{2,1},{3,2},{4,3},{5,4},{6,5},{7,6},{8,7},{9,8},{10,9},{11,1... | collective-permute-start | bytes 2949128 | tf_op jit(solution)/shard_map/level0_down/ppermute | solution.py:20
  96.5 6.1 %collective-permute-start.4 = (f32[2,4,16,256]{3,2,1,0:T(8,128)S(1)}, f32[2,4,16,256]{3,2,1,0:T(8,128)S(1)}, u32[]{:S(2)}, u32[]{:S(2)}) collective-permute-start(f32[2,4,16,256]{3,2,1,0:T(8,128)S(1)} %get-tuple-element.33), channel_id=1, source_target_pairs={{0,16},{16,32},{32,48},{48,64},{64,80},{80,96},{96,112},{1,17},{17... | collective-permute-start | bytes 393224 | tf_op jit(solution)/shard_map/level1_down/ppermute | solution.py:19
  100.0 6.3 %collective-permute-start.5 = (f32[2,4,16,256]{3,2,1,0:T(8,128)S(1)}, f32[2,4,16,256]{3,2,1,0:T(8,128)S(1)}, u32[]{:S(2)}, u32[]{:S(2)}) collective-permute-start(f32[2,4,16,256]{3,2,1,0:T(8,128)S(1)} %get-tuple-element.34), channel_id=1, source_target_pairs={{16,0},{32,16},{48,32},{64,48},{80,64},{96,80},{112,96},{17,1},{33... | collective-permute-start | bytes 393224 | tf_op jit(solution)/shard_map/level1_down/ppermute | solution.py:20
  106.4 7.8 %collective-permute-start.6 = (f32[2,24,4,256]{3,2,1,0:T(4,128)S(1)}, f32[2,24,4,256]{3,2,1,0:T(4,128)S(1)}, u32[]{:S(2)}, u32[]{:S(2)}) collective-permute-start(f32[2,24,4,256]{3,2,1,0:T(4,128)S(1)} %get-tuple-element.11), channel_id=1, source_target_pairs={{0,1},{1,2},{2,3},{3,4},{4,5},{5,6},{6,7},{7,8},{8,9},{9,10},{10,1... | collective-permute-start | bytes 589832 | tf_op jit(solution)/shard_map/level1_down/ppermute | solution.py:19
  108.3 9.6 %collective-permute-start.7 = (f32[2,24,4,256]{3,2,1,0:T(4,128)S(1)}, f32[2,24,4,256]{3,2,1,0:T(4,128)S(1)}, u32[]{:S(2)}, u32[]{:S(2)}) collective-permute-start(f32[2,24,4,256]{3,2,1,0:T(4,128)S(1)} %get-tuple-element.12), channel_id=1, source_target_pairs={{1,0},{2,1},{3,2},{4,3},{5,4},{6,5},{7,6},{8,7},{9,8},{10,9},{11,1... | collective-permute-start | bytes 589832 | tf_op jit(solution)/shard_map/level1_down/ppermute | solution.py:20
  122.8 5.4 %collective-permute-start.8 = (f32[2,5,8,128]{3,2,1,0:T(8,128)S(1)}, f32[2,5,8,128]{3,2,1,0:T(8,128)S(1)}, u32[]{:S(2)}, u32[]{:S(2)}) collective-permute-start(f32[2,5,8,128]{3,2,1,0:T(8,128)S(1)} %get-tuple-element.75), channel_id=1, source_target_pairs={{0,16},{16,32},{32,48},{48,64},{64,80},{80,96},{96,112},{1,17},{17... | collective-permute-start | bytes 122888 | tf_op jit(solution)/shard_map/level2/ppermute | solution.py:19
  126.1 5.3 %collective-permute-start.9 = (f32[2,5,8,128]{3,2,1,0:T(8,128)S(1)}, f32[2,5,8,128]{3,2,1,0:T(8,128)S(1)}, u32[]{:S(2)}, u32[]{:S(2)}) collective-permute-start(f32[2,5,8,128]{3,2,1,0:T(8,128)S(1)} %get-tuple-element.76), channel_id=1, source_target_pairs={{16,0},{32,16},{48,32},{64,48},{80,64},{96,80},{112,96},{17,1},{33... | collective-permute-start | bytes 122888 | tf_op jit(solution)/shard_map/level2/ppermute | solution.py:20
  131.4 6.2 %collective-permute-start.10 = (f32[2,18,5,128]{3,2,1,0:T(8,128)S(1)}, f32[2,18,5,128]{3,2,1,0:T(8,128)S(1)}, u32[]{:S(2)}, u32[]{:S(2)}) collective-permute-start(f32[2,18,5,128]{3,2,1,0:T(8,128)S(1)} %get-tuple-element.61), channel_id=1, source_target_pairs={{0,1},{1,2},{2,3},{3,4},{4,5},{5,6},{6,7},{7,8},{8,9},{9,10},{10,1... | collective-permute-start | bytes 276488 | tf_op jit(solution)/shard_map/level2/ppermute | solution.py:19
  133.4 8.3 %collective-permute-start.11 = (f32[2,18,5,128]{3,2,1,0:T(8,128)S(1)}, f32[2,18,5,128]{3,2,1,0:T(8,128)S(1)}, u32[]{:S(2)}, u32[]{:S(2)}) collective-permute-start(f32[2,18,5,128]{3,2,1,0:T(8,128)S(1)} %get-tuple-element.62), channel_id=1, source_target_pairs={{1,0},{2,1},{3,2},{4,3},{5,4},{6,5},{7,6},{8,7},{9,8},{10,9},{11,1... | collective-permute-start | bytes 276488 | tf_op jit(solution)/shard_map/level2/ppermute | solution.py:20
  145.0 0.9 copy-start.5
  145.0 1.0 copy-start.6
  150.7 4.8 %copy-start = (f32[40,40,512]{2,1,0:T(8,128)S(1)}, f32[40,40,512]{2,1,0:T(8,128)}, u32[]{:S(2)}) copy-start(f32[40,40,512]{2,1,0:T(8,128)} %level0_down.4.u_ref.ulo_ref.uhi_ref) | copy-start | bytes 9830404

commit v3 on v2

--- a/solution.py
+++ b/solution.py
@@ -204,6 +204,100 @@
     )(offsets, u_arr, u_arr, u_arr, b_arr, k_arr, k_arr, k_arr)
 
 
+def _sweep_planes(off_ref, u_ref, b_ref, k_ref, o_ref, *, scale, extent_x, extent_y, residual,
+                  planes, inner):
+    depth_y, depth_z = u_ref.shape[-2], u_ref.shape[-1]
+    first = 4 if inner else 0
+    tiles = (depth_y - 2 * first) // 8
+    half = 0.5 * scale
+    z_idx = lax.broadcasted_iota(jnp.int32, (8, depth_z), 1)
+    z_first = z_idx == 0
+    z_last = z_idx == depth_z - 1
+    row_idx = lax.broadcasted_iota(jnp.int32, (8, depth_z), 0)
+
+    def z_lo(a):
+        return jnp.where(z_first, 0.0, pltpu.roll(a, 1, 1))
+
+    def z_hi(a):
+        return jnp.where(z_last, 0.0, pltpu.roll(a, depth_z - 1, 1))
+
+    def rows(ref, plane, t, shift):
+        start = first + 8 * t
+        if shift == 0:
+            return ref[plane, pl.ds(start, 8), :]
+        if shift < 0 and start == 0:
+            return pltpu.roll(ref[plane, pl.ds(0, 8), :], 1, 0)
+        if shift > 0 and start + 8 == depth_y:
+            return pltpu.roll(ref[plane, pl.ds(start, 8), :], 7, 0)
+        return ref[plane, pl.ds(start + shift, 8), :]
+
+    def plane_body(p, carry):
+        x_idx = off_ref[0] + p
+        x_ok = (x_idx >= 0) & (x_idx < extent_x)
+        out_plane = p - first
+        for t in range(tiles):
+            kc = rows(k_ref, p, t, 0)
+            uc = rows(u_ref, p, t, 0)
+            sxm = kc + rows(k_ref, p - 1, t, 0)
+            sxp = rows(k_ref, p + 1, t, 0) + kc
+            sym = kc + rows(k_ref, p, t, -1)
+            syp = rows(k_ref, p, t, 1) + kc
+            szm = kc + z_lo(kc)
+            szp = z_hi(kc) + kc
+            total = sxm + sxp + sym + syp + szm + szp
+            beside = sxm * rows(u_ref, p - 1, t, 0) + sxp * rows(u_ref, p + 1, t, 0)
+            beside = beside + sym * rows(u_ref, p, t, -1) + syp * rows(u_ref, p, t, 1)
+            beside = beside + szm * z_lo(uc) + szp * z_hi(uc)
+            image = (total * uc - beside) * half
+            rhs = rows(b_ref, p, t, 0)
+            out_rows = pl.ds(8 * t if inner else first + 8 * t, 8)
+            if residual:
+                o_ref[out_plane, out_rows, :] = rhs - image
+            else:
+                y_idx = off_ref[1] + first + 8 * t + row_idx
+                ok = x_ok & (y_idx >= 0) & (y_idx < extent_y)
+                fresh = uc + damping * (rhs - image) / (total * half)
+                o_ref[out_plane, out_rows, :] = jnp.where(ok, fresh, 0.0)
+        return carry
+
+    lax.fori_loop(planes[0], planes[1], plane_body, 0)
+
+
+def _down_kernel(off_ref, s_ref, u2_ref, r_ref, u1_ref, *, extent_x, extent_y):
+    depth_x = s_ref.shape[1]
+    common = dict(scale=1.0, extent_x=extent_x, extent_y=extent_y)
+    _sweep_planes(off_ref, s_ref.at[0], s_ref.at[1], s_ref.at[2], u1_ref, residual=False,
+                  planes=(1, depth_x - 1), inner=False, **common)
+    _sweep_planes(off_ref, u1_ref, s_ref.at[1], s_ref.at[2], u2_ref, residual=False,
+                  planes=(2, depth_x - 2), inner=False, **common)
+    _sweep_planes(off_ref, u2_ref, s_ref.at[1], s_ref.at[2], r_ref, residual=True,
+                  planes=(4, depth_x - 4), inner=True, **common)
+
+
+def _up_kernel(off_ref, u3_ref, s_ref, u5_ref, u4_ref, *, extent_x, extent_y):
+    depth_x = s_ref.shape[1]
+    common = dict(scale=1.0, extent_x=extent_x, extent_y=extent_y)
+    _sweep_planes(off_ref, u3_ref, s_ref.at[1], s_ref.at[2], u4_ref, residual=False,
+                  planes=(3, depth_x - 3), inner=False, **common)
+    _sweep_planes(off_ref, u4_ref, s_ref.at[1], s_ref.at[2], u5_ref, residual=False,
+                  planes=(4, depth_x - 4), inner=True, **common)
+
+
+def _frame_call(kernel, offsets, arrays, outs, scratch, cells, passes):
+    vmem = pl.BlockSpec(memory_space=pltpu.VMEM)
+    return pl.pallas_call(
+        kernel,
+        grid=(1,),
+        out_shape=outs,
+        in_specs=[pl.BlockSpec(memory_space=pltpu.SMEM)] + [vmem] * len(arrays),
+        out_specs=[vmem] * len(outs) if isinstance(outs, (list, tuple)) else vmem,
+        scratch_shapes=scratch,
+        compiler_params=pltpu.CompilerParams(vmem_limit_bytes=60 * 1024 * 1024),
+        cost_estimate=pl.CostEstimate(flops=40 * cells * passes, transcendentals=0,
+                                      bytes_accessed=4 * 5 * cells),
+    )(offsets, *arrays)
+
+
 def on_device(start_field, source, conductance):
     nx, ny = start_field.shape[0], start_field.shape[1]
     mx, my = nx // 2, ny // 2
@@ -213,10 +307,12 @@
         fine = exchange(jnp.stack([start_field, source, conductance]), 4)
         extent_x, extent_y = nx * lax.axis_size("row"), ny * lax.axis_size("col")
         offsets = jnp.stack([lax.axis_index("row") * nx - 4, lax.axis_index("col") * ny - 4]).astype(jnp.int32)
-        u1 = plane_step(offsets, (fine, 0), (fine, 1), (fine, 2), 1.0, extent_x, extent_y)
-        u2 = plane_step(offsets, (u1, None), (fine, 1), (fine, 2), 1.0, extent_x, extent_y)
-        residual = plane_step(offsets, (u2, None), (fine, 1), (fine, 2), 1.0, extent_x, extent_y,
-                              residual=True, inner=True)
+        depth_x, depth_y, depth_z = fine.shape[1:]
+        frame = jax.ShapeDtypeStruct((depth_x, depth_y, depth_z), jnp.float32)
+        inner = jax.ShapeDtypeStruct((depth_x - 8, depth_y - 8, depth_z), jnp.float32)
+        kernel = functools.partial(_down_kernel, extent_x=extent_x, extent_y=extent_y)
+        u2, residual = _frame_call(kernel, offsets, [fine], [frame, inner],
+                                   [pltpu.VMEM(frame.shape, jnp.float32)], fine[0].size, 3)
         mid_rhs = restrict_mean(residual)
         mid_cond = restrict_mean(conductance)
 
@@ -242,8 +338,9 @@
 
     with jax.named_scope("level0_up"):
         u3 = u2 + jnp.pad(prolong_copy(e1), ((2, 2), (2, 2), (0, 0)))
-        u4 = plane_step(offsets, (u3, None), (fine, 1), (fine, 2), 1.0, extent_x, extent_y)
-        u5 = plane_step(offsets, (u4, None), (fine, 1), (fine, 2), 1.0, extent_x, extent_y, inner=True)
+        kernel = functools.partial(_up_kernel, extent_x=extent_x, extent_y=extent_y)
+        u5 = _frame_call(kernel, offsets, [u3, fine], inner, [pltpu.VMEM(frame.shape, jnp.float32)],
+                         fine[0].size, 2)
     return u5
 
 

time: 183 us -> 171 us (0.934)
  Pallas kernels: 53.8 us -> 44 us
    pallas_call x5 -> x2, Pallas kernels: 53.8 us -> 44 us  [_frame_call(): pl.pallas_call(kernel, grid=(1,), out_shape=outs, in_specs=[pl.BlockSpec(...]
where the time goes in v3:
time: 171 us
  waiting for transfers between devices  45.2 us (26%)
  Pallas kernels  44 us (26%)
  starting transfers between devices  32.2 us (19%)
  other arithmetic  27.3 us (16%)
  local copies, waits for them, and re-layouts  16.4 us (10%)
  matrix products  4.9 us (3%)
    pallas_call x2, Pallas kernels, _frame_call(): pl.pallas_call(kernel, grid=(1,), out_shape=outs, in_specs=[pl.BlockSpec(...  44 us
    ppermute x6, waiting for transfers between devices, exchange(): lax.ppermute(lax.slice_in_dim(stack, 0, width, axis=dim), axis, backward)  24.3 us
    ppermute x6, waiting for transfers between devices, exchange(): lax.ppermute(lax.slice_in_dim(stack, size - width, size, axis=dim), axis,...  20.9 us
    ppermute x6, starting transfers between devices, exchange(): lax.ppermute(lax.slice_in_dim(stack, size - width, size, axis=dim), axis,...  17.5 us
    ppermute x6, starting transfers between devices, exchange(): lax.ppermute(lax.slice_in_dim(stack, 0, width, axis=dim), axis, backward)  14.7 us
    concatenate x4, other arithmetic, exchange(): stack = jnp.concatenate([low, stack, high], axis=dim)  7.29 us
    reduce_sum x4, other arithmetic, restrict_mean(): field.reshape(field.shape[0] // 2, 2, field.shape[1] // 2, 2, depth)  5.89 us
    slice x4, other arithmetic, exchange(): lax.slice_in_dim(stack, size - width, size, axis=dim)  5.3 us
  transfers between devices with their start and end apart: 12, of which 10 were waited for; matrix products, arithmetic and copies ran while one was open for 6% of the time, Pallas kernels for 0%

profile of v3, /device:TPU:27, one launch (start us, length us, event | category | flops | bytes accessed | tf_op | source)
XLA Modules:
  0.0 170.6 jit_solution(17987629145604637663)
XLA Ops:
  0.0 2.8 %pad_maximum_fusion.9 = (f32[3,4,32,512]{3,2,1,0:T(8,128)}, f32[3,4,32,512]{3,2,1,0:T(8,128)}) fusion(f32[1,32,32,512]{3,2,1,0:T(8,128)} %bitcast.41, f32[1,32,32,512]{3,2,1,0:T(8,128)} %bitcast.44, f32[1,32,32,512]{3,2,1,0:T(8,128)} %bitcast.47), kind=kLoop, calls=%fused_computation.12 | loop fusion | flops 786432 | bytes 7864320 | tf_op jit(solution)/shard_map/level0_down/slice | solution.py:19
  2.9 3.7 %collective-permute-start = (f32[3,4,32,512]{3,2,1,0:T(8,128)}, f32[3,4,32,512]{3,2,1,0:T(8,128)S(1)}, u32[]{:S(2)}, u32[]{:S(2)}) collective-permute-start(f32[3,4,32,512]{3,2,1,0:T(8,128)} %get-tuple-element.11), channel_id=1, source_target_pairs={{0,16},{16,32},{32,48},{48,64},{64,80},{80,96},{96,112},{1,17},{17... | collective-permute-start | bytes 2359304 | tf_op jit(solution)/shard_map/level0_down/ppermute | solution.py:19
  6.5 1.9 %collective-permute-start.1 = (f32[3,4,32,512]{3,2,1,0:T(8,128)}, f32[3,4,32,512]{3,2,1,0:T(8,128)}, u32[]{:S(2)}, u32[]{:S(2)}) collective-permute-start(f32[3,4,32,512]{3,2,1,0:T(8,128)} %get-tuple-element.12), channel_id=1, source_target_pairs={{16,0},{32,16},{48,32},{64,48},{80,64},{96,80},{112,96},{17,1},{33... | collective-permute-start | bytes 2359304 | tf_op jit(solution)/shard_map/level0_down/ppermute | solution.py:20
  8.7 2.2 %reshape.403 = f32[16,2,16,2,512]{4,3,2,1,0:T(2,128)} reshape(f32[32,32,512]{2,1,0:T(8,128)S(1)} %copy-done) | data formatting | bytes 4194304 | tf_op jit(solution)/shard_map/level0_down/reshape | solution.py:83
  10.9 4.0 %reduce_sum.37 = f32[16,16,512]{2,1,0:T(8,128)} reduce(f32[16,2,16,2,512]{4,3,2,1,0:T(2,128)} %reshape.403, f32[]{:T(128)} %constant.162.clone.1), dimensions={1,3}, to_apply=%region_1.2 | reduce | flops 393216 | bytes 2621444 | tf_op jit(solution)/shard_map/level0_down/reduce_sum | solution.py:83
  15.1 0.7 collective-permute-done
  15.8 4.4 %collective-permute-done.1 = f32[3,4,32,512]{3,2,1,0:T(8,128)} collective-permute-done((f32[3,4,32,512]{3,2,1,0:T(8,128)}, f32[3,4,32,512]{3,2,1,0:T(8,128)}, u32[]{:S(2)}, u32[]{:S(2)}) %collective-permute-start.1) | collective-permute-done | bytes 786464 | tf_op jit(solution)/shard_map/level0_down/ppermute | solution.py:20
  20.2 2.4 %pad_maximum_fusion.6 = (f32[3,40,4,512]{3,2,1,0:T(4,128)S(1)}, f32[3,40,4,512]{3,2,1,0:T(4,128)S(1)}) fusion(f32[3,4,32,512]{3,2,1,0:T(8,128)} %collective-permute-done.1, f32[3,4,32,512]{3,2,1,0:T(8,128)S(1)} %collective-permute-done, f32[1,32,32,512]{3,2,1,0:T(8,128)S(1)} %bitcast.42, f32[1,32,32,512]{3,2,1,0:T(8,128)} %bitcast.45, ...), kind=kLoop, calls=%fused_computation.9 | loop fusion | flops 1966080 | bytes 9830400 | tf_op jit(solution)/shard_map/level0_down/slice | solution.py:19
  22.5 3.2 %collective-permute-start.2 = (f32[3,40,4,512]{3,2,1,0:T(4,128)S(1)}, f32[3,40,4,512]{3,2,1,0:T(4,128)S(1)}, u32[]{:S(2)}, u32[]{:S(2)}) collective-permute-start(f32[3,40,4,512]{3,2,1,0:T(4,128)S(1)} %get-tuple-element.9), channel_id=1, source_target_pairs={{0,1},{1,2},{2,3},{3,4},{4,5},{5,6},{6,7},{7,8},{8,9},{9,10},{10,1... | collective-permute-start | bytes 2949128 | tf_op jit(solution)/shard_map/level0_down/ppermute | solution.py:19
  25.7 2.1 %collective-permute-start.3 = (f32[3,40,4,512]{3,2,1,0:T(4,128)S(1)}, f32[3,40,4,512]{3,2,1,0:T(4,128)S(1)}, u32[]{:S(2)}, u32[]{:S(2)}) collective-permute-start(f32[3,40,4,512]{3,2,1,0:T(4,128)S(1)} %get-tuple-element.10), channel_id=1, source_target_pairs={{1,0},{2,1},{3,2},{4,3},{5,4},{6,5},{7,6},{8,7},{9,8},{10,9},{11,1... | collective-permute-start | bytes 2949128 | tf_op jit(solution)/shard_map/level0_down/ppermute | solution.py:20
  27.8 0.6 pad_add_fusion.1.off_ref
  28.7 0.8 fusion.12
  29.4 18.0 %collective-permute-done.2 = f32[3,40,4,512]{3,2,1,0:T(4,128)S(1)} collective-permute-done((f32[3,40,4,512]{3,2,1,0:T(4,128)S(1)}, f32[3,40,4,512]{3,2,1,0:T(4,128)S(1)}, u32[]{:S(2)}, u32[]{:S(2)}) %collective-permute-start.2) | collective-permute-done | bytes 983072 | tf_op jit(solution)/shard_map/level0_down/ppermute | solution.py:19
  47.4 5.3 %collective-permute-done.3 = f32[3,40,4,512]{3,2,1,0:T(4,128)S(1)} collective-permute-done((f32[3,40,4,512]{3,2,1,0:T(4,128)S(1)}, f32[3,40,4,512]{3,2,1,0:T(4,128)S(1)}, u32[]{:S(2)}, u32[]{:S(2)}) %collective-permute-start.3) | collective-permute-done | bytes 983072 | tf_op jit(solution)/shard_map/level0_down/ppermute | solution.py:20
  52.7 7.0 %pad_maximum_fusion.s_ref = f32[3,40,40,512]{3,2,1,0:T(8,128)} fusion(f32[3,40,4,512]{3,2,1,0:T(4,128)S(1)} %collective-permute-done.3, f32[3,4,32,512]{3,2,1,0:T(8,128)} %collective-permute-done.1, f32[1,32,32,512]{3,2,1,0:T(8,128)S(1)} %bitcast.43, f32[1,32,32,512]{3,2,1,0:T(8,128)S(1)} %bitcast.46, f32[1,32,32,512]{3,2,1,0:T(8,128)S(1)} %bitcast.49, ...), kind=kLoop, calls=%fused_computation | loop fusion | flops 14745600 | bytes 19660800 | tf_op jit(solution)/shard_map/level0_down/concatenate | solution.py:21
  59.8 24.9 %level0_down.1 = (f32[40,40,512]{2,1,0:T(8,128)}, f32[32,32,512]{2,1,0:T(8,128)}) custom-call(s32[2]{0:T(128)} %pad_add_fusion.1.off_ref, f32[3,40,40,512]{3,2,1,0:T(8,128)} %pad_maximum_fusion.s_ref), custom_call_target="tpu_custom_call" | custom-call | flops 98304000 | bytes 16384000 | tf_op jit(solution)/shard_map/level0_down/pallas_call | solution.py:288
  84.7 2.5 %reshape.402 = f32[16,2,16,2,512]{4,3,2,1,0:T(2,128)S(1)} reshape(f32[32,32,512]{2,1,0:T(8,128)} %get-tuple-element.8) | data formatting | bytes 4194304 | tf_op jit(solution)/shard_map/level0_down/reshape | solution.py:83
  87.2 1.5 reduce_sum.36
  88.7 0.8 fusion.14
  89.5 3.5 %collective-permute-start.4 = (f32[2,4,16,256]{3,2,1,0:T(8,128)S(1)}, f32[2,4,16,256]{3,2,1,0:T(8,128)S(1)}, u32[]{:S(2)}, u32[]{:S(2)}) collective-permute-start(f32[2,4,16,256]{3,2,1,0:T(8,128)S(1)} %get-tuple-element.37), channel_id=1, source_target_pairs={{0,16},{16,32},{32,48},{48,64},{64,80},{80,96},{96,112},{1,17},{17... | collective-permute-start | bytes 393224 | tf_op jit(solution)/shard_map/level1_down/ppermute | solution.py:19
  93.0 1.9 %collective-permute-start.5 = (f32[2,4,16,256]{3,2,1,0:T(8,128)S(1)}, f32[2,4,16,256]{3,2,1,0:T(8,128)S(1)}, u32[]{:S(2)}, u32[]{:S(2)}) collective-permute-start(f32[2,4,16,256]{3,2,1,0:T(8,128)S(1)} %get-tuple-element.38), channel_id=1, source_target_pairs={{16,0},{32,16},{48,32},{64,48},{80,64},{96,80},{112,96},{17,1},{33... | collective-permute-start | bytes 393224 | tf_op jit(solution)/shard_map/level1_down/ppermute | solution.py:20
  95.0 0.1 reshape.405
  95.1 0.2 reduce_sum.39
  95.3 0.4 convolution_bitcast_fusion
  95.7 3.6 %collective-permute-done.5 = f32[2,4,16,256]{3,2,1,0:T(8,128)S(1)} collective-permute-done((f32[2,4,16,256]{3,2,1,0:T(8,128)S(1)}, f32[2,4,16,256]{3,2,1,0:T(8,128)S(1)}, u32[]{:S(2)}, u32[]{:S(2)}) %collective-permute-start.5) | collective-permute-done | bytes 131104 | tf_op jit(solution)/shard_map/level1_down/ppermute | solution.py:20
  99.4 1.9 %collective-permute-start.6 = (f32[2,24,4,256]{3,2,1,0:T(4,128)S(1)}, f32[2,24,4,256]{3,2,1,0:T(4,128)S(1)}, u32[]{:S(2)}, u32[]{:S(2)}) collective-permute-start(f32[2,24,4,256]{3,2,1,0:T(4,128)S(1)} %get-tuple-element.15), channel_id=1, source_target_pairs={{0,1},{1,2},{2,3},{3,4},{4,5},{5,6},{6,7},{7,8},{8,9},{9,10},{10,1... | collective-permute-start | bytes 589832 | tf_op jit(solution)/shard_map/level1_down/ppermute | solution.py:19
  101.3 3.5 %collective-permute-start.7 = (f32[2,24,4,256]{3,2,1,0:T(4,128)S(1)}, f32[2,24,4,256]{3,2,1,0:T(4,128)S(1)}, u32[]{:S(2)}, u32[]{:S(2)}) collective-permute-start(f32[2,24,4,256]{3,2,1,0:T(4,128)S(1)} %get-tuple-element.16), channel_id=1, source_target_pairs={{1,0},{2,1},{3,2},{4,3},{5,4},{6,5},{7,6},{8,7},{9,8},{10,9},{11,1... | collective-permute-start | bytes 589832 | tf_op jit(solution)/shard_map/level1_down/ppermute | solution.py:20
  104.9 2.2 %collective-permute-done.6 = f32[2,24,4,256]{3,2,1,0:T(4,128)S(1)} collective-permute-done((f32[2,24,4,256]{3,2,1,0:T(4,128)S(1)}, f32[2,24,4,256]{3,2,1,0:T(4,128)S(1)}, u32[]{:S(2)}, u32[]{:S(2)}) %collective-permute-start.6) | collective-permute-done | bytes 196640 | tf_op jit(solution)/shard_map/level1_down/ppermute | solution.py:19
  107.1 3.7 %collective-permute-done.7 = f32[2,24,4,256]{3,2,1,0:T(4,128)S(1)} collective-permute-done((f32[2,24,4,256]{3,2,1,0:T(4,128)S(1)}, f32[2,24,4,256]{3,2,1,0:T(4,128)S(1)}, u32[]{:S(2)}, u32[]{:S(2)}) %collective-permute-start.7) | collective-permute-done | bytes 196640 | tf_op jit(solution)/shard_map/level1_down/ppermute | solution.py:20
  110.9 0.2 pad_maximum_fusion.1
  111.1 0.2 fusion.230
  111.4 0.1 fusion.231
  111.5 0.6 fusion.5
  112.1 0.2 fusion.233
  112.5 0.2 fusion.229
  112.8 1.2 fusion.39
  114.0 0.1 fusion.236
  114.3 0.1 fusion.227
  114.5 0.6 fusion.66
  115.1 0.1 reshape.404
  115.2 0.2 reduce_sum.38
  115.4 0.4 convolution_bitcast_fusion.1
  115.8 3.3 %collective-permute-start.8 = (f32[2,5,8,128]{3,2,1,0:T(8,128)S(1)}, f32[2,5,8,128]{3,2,1,0:T(8,128)S(1)}, u32[]{:S(2)}, u32[]{:S(2)}) collective-permute-start(f32[2,5,8,128]{3,2,1,0:T(8,128)S(1)} %get-tuple-element.79), channel_id=1, source_target_pairs={{0,16},{16,32},{32,48},{48,64},{64,80},{80,96},{96,112},{1,17},{17... | collective-permute-start | bytes 122888 | tf_op jit(solution)/shard_map/level2/ppermute | solution.py:19
  119.1 1.9 %collective-permute-start.9 = (f32[2,5,8,128]{3,2,1,0:T(8,128)S(1)}, f32[2,5,8,128]{3,2,1,0:T(8,128)S(1)}, u32[]{:S(2)}, u32[]{:S(2)}) collective-permute-start(f32[2,5,8,128]{3,2,1,0:T(8,128)S(1)} %get-tuple-element.80), channel_id=1, source_target_pairs={{16,0},{32,16},{48,32},{64,48},{80,64},{96,80},{112,96},{17,1},{33... | collective-permute-start | bytes 122888 | tf_op jit(solution)/shard_map/level2/ppermute | solution.py:20
  121.0 0.2 fusion.225
  121.2 3.2 %collective-permute-done.9 = f32[2,5,8,128]{3,2,1,0:T(8,128)S(1)} collective-permute-done((f32[2,5,8,128]{3,2,1,0:T(8,128)S(1)}, f32[2,5,8,128]{3,2,1,0:T(8,128)S(1)}, u32[]{:S(2)}, u32[]{:S(2)}) %collective-permute-start.9) | collective-permute-done | bytes 40992 | tf_op jit(solution)/shard_map/level2/ppermute | solution.py:20
  124.5 1.9 %collective-permute-start.10 = (f32[2,18,5,128]{3,2,1,0:T(8,128)S(1)}, f32[2,18,5,128]{3,2,1,0:T(8,128)S(1)}, u32[]{:S(2)}, u32[]{:S(2)}) collective-permute-start(f32[2,18,5,128]{3,2,1,0:T(8,128)S(1)} %get-tuple-element.65), channel_id=1, source_target_pairs={{0,1},{1,2},{2,3},{3,4},{4,5},{5,6},{6,7},{7,8},{8,9},{9,10},{10,1... | collective-permute-start | bytes 276488 | tf_op jit(solution)/shard_map/level2/ppermute | solution.py:19
  126.4 3.4 %collective-permute-start.11 = (f32[2,18,5,128]{3,2,1,0:T(8,128)S(1)}, f32[2,18,5,128]{3,2,1,0:T(8,128)S(1)}, u32[]{:S(2)}, u32[]{:S(2)}) collective-permute-start(f32[2,18,5,128]{3,2,1,0:T(8,128)S(1)} %get-tuple-element.66), channel_id=1, source_target_pairs={{1,0},{2,1},{3,2},{4,3},{5,4},{6,5},{7,6},{8,7},{9,8},{10,9},{11,1... | collective-permute-start | bytes 276488 | tf_op jit(solution)/shard_map/level2/ppermute | solution.py:20
  129.8 0.8 fusion.224
  130.6 4.0 %collective-permute-done.11 = f32[2,18,5,128]{3,2,1,0:T(8,128)S(1)} collective-permute-done((f32[2,18,5,128]{3,2,1,0:T(8,128)S(1)}, f32[2,18,5,128]{3,2,1,0:T(8,128)S(1)}, u32[]{:S(2)}, u32[]{:S(2)}) %collective-permute-start.11) | collective-permute-done | bytes 92192 | tf_op jit(solution)/shard_map/level2/ppermute | solution.py:20
  135.0 0.2 fusion.105
  135.6 0.3 fusion.137
  136.3 0.3 fusion.158
  137.0 0.5 fusion.110
  137.5 0.1 broadcast_in_dim.191
  137.7 0.3 reshape.407
  138.1 0.2 fusion.234
  138.4 0.5 copy-done.4
  139.0 2.1 %fusion.10 = f32[18,18,512]{2,1,0:T(8,128)S(1)} fusion(f32[20,20,256]{2,1,0:T(8,128)S(1)} %add.699, f32[24,24,256]{2,1,0:T(8,128)S(1)} %get-tuple-element.13, f32[18,18,255]{2,1,0:T(8,128)S(1)} %get-tuple-element.40, f32[18,18,1]{2,1,0:T(8,128)S(1)} %get-tuple-element.42, f32[18,18,1]{2,1,0:T(8,128)S(1)} %get-tuple-element.41, ...), kind=kOutput, calls=%fused_computation.32 | convolution fusion | flops 513567744 | bytes 8192512 | tf_op jit(solution)/shard_map/level0_up/dot_general | solution.py:97
  141.1 0.2 broadcast_in_dim.195
  141.4 2.4 %broadcast_in_dim.196 = f32[36,18,2,512]{3,2,1,0:T(2,128)} broadcast(f32[36,18,512]{2,1,0:T(8,128)S(1)} %bitcast.50), dimensions={0,1,3} | broadcast | bytes 3981312 | tf_op jit(solution)/shard_map/level0_up/broadcast_in_dim | solution.py:100
  143.8 3.4 %reshape.409 = f32[36,36,512]{2,1,0:T(8,128)S(1)} reshape(f32[36,18,2,512]{3,2,1,0:T(2,128)} %broadcast_in_dim.196) | data formatting | bytes 5308416 | tf_op jit(solution)/shard_map/level0_up/reshape | solution.py:100
  147.2 4.4 %pad_add_fusion.u3_ref = f32[40,40,512]{2,1,0:T(8,128)} fusion(f32[40,40,512]{2,1,0:T(8,128)} %get-tuple-element.7, f32[36,36,512]{2,1,0:T(8,128)S(1)} %reshape.409), kind=kLoop, calls=%fused_computation.1 | loop fusion | flops 819200 | bytes 9207808 | tf_op jit(solution)/shard_map/level0_up/add | solution.py:340
  151.6 19.0 %level0_up.1 = f32[32,32,512]{2,1,0:T(8,128)} custom-call(s32[2]{0:T(128)} %pad_add_fusion.1.off_ref, f32[40,40,512]{2,1,0:T(8,128)} %pad_add_fusion.u3_ref, f32[3,40,40,512]{3,2,1,0:T(8,128)} %pad_maximum_fusion.s_ref), custom_call_target="tpu_custom_call" | custom-call | flops 65536000 | bytes 16384000 | tf_op jit(solution)/shard_map/level0_up/pallas_call | solution.py:288
  (63 shorter events, 3.1 us)
Async XLA Ops:
  0.0 8.6 %copy-start = (f32[32,32,512]{2,1,0:T(8,128)S(1)}, f32[32,32,512]{2,1,0:T(8,128)}, u32[]{:S(2)}) copy-start(f32[32,32,512]{2,1,0:T(8,128)} %param.5) | copy-start | bytes 6291460
  2.9 12.9 %collective-permute-start = (f32[3,4,32,512]{3,2,1,0:T(8,128)}, f32[3,4,32,512]{3,2,1,0:T(8,128)S(1)}, u32[]{:S(2)}, u32[]{:S(2)}) collective-permute-start(f32[3,4,32,512]{3,2,1,0:T(8,128)} %get-tuple-element.11), channel_id=1, source_target_pairs={{0,16},{16,32},{32,48},{48,64},{64,80},{80,96},{96,112},{1,17},{17... | collective-permute-start | bytes 2359304 | tf_op jit(solution)/shard_map/level0_down/ppermute | solution.py:19
  6.5 13.6 %collective-permute-start.1 = (f32[3,4,32,512]{3,2,1,0:T(8,128)}, f32[3,4,32,512]{3,2,1,0:T(8,128)}, u32[]{:S(2)}, u32[]{:S(2)}) collective-permute-start(f32[3,4,32,512]{3,2,1,0:T(8,128)} %get-tuple-element.12), channel_id=1, source_target_pairs={{16,0},{32,16},{48,32},{64,48},{80,64},{96,80},{112,96},{17,1},{33... | collective-permute-start | bytes 2359304 | tf_op jit(solution)/shard_map/level0_down/ppermute | solution.py:20
  15.1 13.6 %copy-start.3 = (f32[16,16,512]{2,1,0:T(8,128)S(1)}, f32[16,16,512]{2,1,0:T(8,128)}, u32[]{:S(2)}) copy-start(f32[16,16,512]{2,1,0:T(8,128)} %reduce_sum.37) | copy-start | bytes 1572868
  20.2 32.6 %copy-start.1 = (f32[32,32,512]{2,1,0:T(8,128)S(1)}, f32[32,32,512]{2,1,0:T(8,128)}, u32[]{:S(2)}) copy-start(f32[32,32,512]{2,1,0:T(8,128)} %param.4) | copy-start | bytes 6291460
  20.2 32.6 %copy-start.2 = (f32[32,32,512]{2,1,0:T(8,128)S(1)}, f32[32,32,512]{2,1,0:T(8,128)}, u32[]{:S(2)}) copy-start(f32[32,32,512]{2,1,0:T(8,128)} %param.3) | copy-start | bytes 6291460
  22.5 24.9 %collective-permute-start.2 = (f32[3,40,4,512]{3,2,1,0:T(4,128)S(1)}, f32[3,40,4,512]{3,2,1,0:T(4,128)S(1)}, u32[]{:S(2)}, u32[]{:S(2)}) collective-permute-start(f32[3,40,4,512]{3,2,1,0:T(4,128)S(1)} %get-tuple-element.9), channel_id=1, source_target_pairs={{0,1},{1,2},{2,3},{3,4},{4,5},{5,6},{6,7},{7,8},{8,9},{9,10},{10,1... | collective-permute-start | bytes 2949128 | tf_op jit(solution)/shard_map/level0_down/ppermute | solution.py:19
  25.7 27.0 %collective-permute-start.3 = (f32[3,40,4,512]{3,2,1,0:T(4,128)S(1)}, f32[3,40,4,512]{3,2,1,0:T(4,128)S(1)}, u32[]{:S(2)}, u32[]{:S(2)}) collective-permute-start(f32[3,40,4,512]{3,2,1,0:T(4,128)S(1)} %get-tuple-element.10), channel_id=1, source_target_pairs={{1,0},{2,1},{3,2},{4,3},{5,4},{6,5},{7,6},{8,7},{9,8},{10,9},{11,1... | collective-permute-start | bytes 2949128 | tf_op jit(solution)/shard_map/level0_down/ppermute | solution.py:20
  89.5 6.1 %collective-permute-start.4 = (f32[2,4,16,256]{3,2,1,0:T(8,128)S(1)}, f32[2,4,16,256]{3,2,1,0:T(8,128)S(1)}, u32[]{:S(2)}, u32[]{:S(2)}) collective-permute-start(f32[2,4,16,256]{3,2,1,0:T(8,128)S(1)} %get-tuple-element.37), channel_id=1, source_target_pairs={{0,16},{16,32},{32,48},{48,64},{64,80},{80,96},{96,112},{1,17},{17... | collective-permute-start | bytes 393224 | tf_op jit(solution)/shard_map/level1_down/ppermute | solution.py:19
  93.0 6.3 %collective-permute-start.5 = (f32[2,4,16,256]{3,2,1,0:T(8,128)S(1)}, f32[2,4,16,256]{3,2,1,0:T(8,128)S(1)}, u32[]{:S(2)}, u32[]{:S(2)}) collective-permute-start(f32[2,4,16,256]{3,2,1,0:T(8,128)S(1)} %get-tuple-element.38), channel_id=1, source_target_pairs={{16,0},{32,16},{48,32},{64,48},{80,64},{96,80},{112,96},{17,1},{33... | collective-permute-start | bytes 393224 | tf_op jit(solution)/shard_map/level1_down/ppermute | solution.py:20
  99.4 7.8 %collective-permute-start.6 = (f32[2,24,4,256]{3,2,1,0:T(4,128)S(1)}, f32[2,24,4,256]{3,2,1,0:T(4,128)S(1)}, u32[]{:S(2)}, u32[]{:S(2)}) collective-permute-start(f32[2,24,4,256]{3,2,1,0:T(4,128)S(1)} %get-tuple-element.15), channel_id=1, source_target_pairs={{0,1},{1,2},{2,3},{3,4},{4,5},{5,6},{6,7},{7,8},{8,9},{9,10},{10,1... | collective-permute-start | bytes 589832 | tf_op jit(solution)/shard_map/level1_down/ppermute | solution.py:19
  101.3 9.6 %collective-permute-start.7 = (f32[2,24,4,256]{3,2,1,0:T(4,128)S(1)}, f32[2,24,4,256]{3,2,1,0:T(4,128)S(1)}, u32[]{:S(2)}, u32[]{:S(2)}) collective-permute-start(f32[2,24,4,256]{3,2,1,0:T(4,128)S(1)} %get-tuple-element.16), channel_id=1, source_target_pairs={{1,0},{2,1},{3,2},{4,3},{5,4},{6,5},{7,6},{8,7},{9,8},{10,9},{11,1... | collective-permute-start | bytes 589832 | tf_op jit(solution)/shard_map/level1_down/ppermute | solution.py:20
  115.8 5.4 %collective-permute-start.8 = (f32[2,5,8,128]{3,2,1,0:T(8,128)S(1)}, f32[2,5,8,128]{3,2,1,0:T(8,128)S(1)}, u32[]{:S(2)}, u32[]{:S(2)}) collective-permute-start(f32[2,5,8,128]{3,2,1,0:T(8,128)S(1)} %get-tuple-element.79), channel_id=1, source_target_pairs={{0,16},{16,32},{32,48},{48,64},{64,80},{80,96},{96,112},{1,17},{17... | collective-permute-start | bytes 122888 | tf_op jit(solution)/shard_map/level2/ppermute | solution.py:19
  119.1 5.3 %collective-permute-start.9 = (f32[2,5,8,128]{3,2,1,0:T(8,128)S(1)}, f32[2,5,8,128]{3,2,1,0:T(8,128)S(1)}, u32[]{:S(2)}, u32[]{:S(2)}) collective-permute-start(f32[2,5,8,128]{3,2,1,0:T(8,128)S(1)} %get-tuple-element.80), channel_id=1, source_target_pairs={{16,0},{32,16},{48,32},{64,48},{80,64},{96,80},{112,96},{17,1},{33... | collective-permute-start | bytes 122888 | tf_op jit(solution)/shard_map/level2/ppermute | solution.py:20
  124.5 6.2 %collective-permute-start.10 = (f32[2,18,5,128]{3,2,1,0:T(8,128)S(1)}, f32[2,18,5,128]{3,2,1,0:T(8,128)S(1)}, u32[]{:S(2)}, u32[]{:S(2)}) collective-permute-start(f32[2,18,5,128]{3,2,1,0:T(8,128)S(1)} %get-tuple-element.65), channel_id=1, source_target_pairs={{0,1},{1,2},{2,3},{3,4},{4,5},{5,6},{6,7},{7,8},{8,9},{9,10},{10,1... | collective-permute-start | bytes 276488 | tf_op jit(solution)/shard_map/level2/ppermute | solution.py:19
  126.4 8.3 %collective-permute-start.11 = (f32[2,18,5,128]{3,2,1,0:T(8,128)S(1)}, f32[2,18,5,128]{3,2,1,0:T(8,128)S(1)}, u32[]{:S(2)}, u32[]{:S(2)}) collective-permute-start(f32[2,18,5,128]{3,2,1,0:T(8,128)S(1)} %get-tuple-element.66), channel_id=1, source_target_pairs={{1,0},{2,1},{3,2},{4,3},{5,4},{6,5},{7,6},{8,7},{9,8},{10,9},{11,1... | collective-permute-start | bytes 276488 | tf_op jit(solution)/shard_map/level2/ppermute | solution.py:20
  138.0 0.9 copy-start.4
  138.0 1.0 copy-start.5

commit v4 on v3

--- a/solution.py
+++ b/solution.py
@@ -274,9 +274,15 @@
                   planes=(4, depth_x - 4), inner=True, **common)
 
 
-def _up_kernel(off_ref, u3_ref, s_ref, u5_ref, u4_ref, *, extent_x, extent_y):
+def _up_kernel(off_ref, u2_ref, e_ref, s_ref, u5_ref, u3_ref, u4_ref, *, extent_x, extent_y):
     depth_x = s_ref.shape[1]
     common = dict(scale=1.0, extent_x=extent_x, extent_y=extent_y)
+
+    def add_plane(p, carry):
+        u3_ref[p] = u2_ref[p] + e_ref[p // 2 - 1]
+        return carry
+
+    lax.fori_loop(2, depth_x - 2, add_plane, 0)
     _sweep_planes(off_ref, u3_ref, s_ref.at[1], s_ref.at[2], u4_ref, residual=False,
                   planes=(3, depth_x - 3), inner=False, **common)
     _sweep_planes(off_ref, u4_ref, s_ref.at[1], s_ref.at[2], u5_ref, residual=False,
@@ -337,9 +343,15 @@
         e1 = sweep(e1, trim(rhs1, 3), trim(k1, 2), 0.25, grid_mask(mx, my, 1))
 
     with jax.named_scope("level0_up"):
-        u3 = u2 + jnp.pad(prolong_copy(e1), ((2, 2), (2, 2), (0, 0)))
+        coarse_z = e1.shape[2]
+        coarse_idx = lax.broadcasted_iota(jnp.int32, (coarse_z, 2 * coarse_z), 0)
+        fine_idx = lax.broadcasted_iota(jnp.int32, (coarse_z, 2 * coarse_z), 1)
+        table = jnp.where(fine_idx // 2 == coarse_idx, 1.0, 0.0).astype(jnp.float32)
+        deeper = jnp.dot(e1, table, precision=lax.Precision.HIGHEST, preferred_element_type=jnp.float32)
+        wider = jnp.pad(jnp.repeat(deeper, 2, 1), ((0, 0), (2, 2), (0, 0)))
         kernel = functools.partial(_up_kernel, extent_x=extent_x, extent_y=extent_y)
-        u5 = _frame_call(kernel, offsets, [u3, fine], inner, [pltpu.VMEM(frame.shape, jnp.float32)],
+        u5 = _frame_call(kernel, offsets, [u2, wider, fine], inner,
+                         [pltpu.VMEM(frame.shape, jnp.float32), pltpu.VMEM(frame.shape, jnp.float32)],
                          fine[0].size, 2)
     return u5
 

time: 171 us -> 162 us (0.947)
  the two profiles are of different devices: /device:TPU:27 before, /device:TPU:98 now
where the time goes in v4:
time: 162 us; the launch traced here: 161 us
  Pallas kernels  45 us (28%)
  waiting for transfers between devices  43.5 us (27%)
  starting transfers between devices  31.5 us (19%)
  other arithmetic  22.4 us (14%)
  local copies, waits for them, and re-layouts  13.1 us (8%)
  matrix products  4.9 us (3%)
    pallas_call x2, Pallas kernels, _frame_call(): pl.pallas_call(kernel, grid=(1,), out_shape=outs, in_specs=[pl.BlockSpec(...  45 us
    ppermute x6, waiting for transfers between devices, exchange(): lax.ppermute(lax.slice_in_dim(stack, size - width, size, axis=dim), axis,...  24 us
    ppermute x6, waiting for transfers between devices, exchange(): lax.ppermute(lax.slice_in_dim(stack, 0, width, axis=dim), axis, backward)  19.6 us
    ppermute x6, starting transfers between devices, exchange(): lax.ppermute(lax.slice_in_dim(stack, size - width, size, axis=dim), axis,...  17.2 us
    ppermute x6, starting transfers between devices, exchange(): lax.ppermute(lax.slice_in_dim(stack, 0, width, axis=dim), axis, backward)  14.4 us
    concatenate x4, other arithmetic, exchange(): stack = jnp.concatenate([low, stack, high], axis=dim)  6.7 us
    reduce_sum x4, other arithmetic, restrict_mean(): field.reshape(field.shape[0] // 2, 2, field.shape[1] // 2, 2, depth)  5.89 us
    slice x4, other arithmetic, exchange(): lax.slice_in_dim(stack, size - width, size, axis=dim)  5.3 us
  transfers between devices with their start and end apart: 12, of which 10 were waited for; matrix products, arithmetic and copies ran while one was open for 6% of the time, Pallas kernels for 0%

profile of v4, /device:TPU:98, one launch (start us, length us, event | category | flops | bytes accessed | tf_op | source)
XLA Modules:
  0.0 161.0 jit_solution(14720337502018798046)
XLA Ops:
  0.0 2.8 %pad_maximum_fusion.9 = (f32[3,4,32,512]{3,2,1,0:T(8,128)}, f32[3,4,32,512]{3,2,1,0:T(8,128)}) fusion(f32[1,32,32,512]{3,2,1,0:T(8,128)} %bitcast.40, f32[1,32,32,512]{3,2,1,0:T(8,128)} %bitcast.43, f32[1,32,32,512]{3,2,1,0:T(8,128)} %bitcast.46), kind=kLoop, calls=%fused_computation.11 | loop fusion | flops 786432 | bytes 7864320 | tf_op jit(solution)/shard_map/level0_down/slice | solution.py:19
  2.9 1.9 %collective-permute-start.1 = (f32[3,4,32,512]{3,2,1,0:T(8,128)}, f32[3,4,32,512]{3,2,1,0:T(8,128)S(1)}, u32[]{:S(2)}, u32[]{:S(2)}) collective-permute-start(f32[3,4,32,512]{3,2,1,0:T(8,128)} %get-tuple-element.12), channel_id=1, source_target_pairs={{16,0},{32,16},{48,32},{64,48},{80,64},{96,80},{112,96},{17,1},{33... | collective-permute-start | bytes 2359304 | tf_op jit(solution)/shard_map/level0_down/ppermute | solution.py:20
  4.8 2.4 %collective-permute-start = (f32[3,4,32,512]{3,2,1,0:T(8,128)}, f32[3,4,32,512]{3,2,1,0:T(8,128)}, u32[]{:S(2)}, u32[]{:S(2)}) collective-permute-start(f32[3,4,32,512]{3,2,1,0:T(8,128)} %get-tuple-element.11), channel_id=1, source_target_pairs={{0,16},{16,32},{32,48},{48,64},{64,80},{80,96},{96,112},{1,17},{17... | collective-permute-start | bytes 2359304 | tf_op jit(solution)/shard_map/level0_down/ppermute | solution.py:19
  7.4 2.2 %reshape.400 = f32[16,2,16,2,512]{4,3,2,1,0:T(2,128)} reshape(f32[32,32,512]{2,1,0:T(8,128)S(1)} %copy-done) | data formatting | bytes 4194304 | tf_op jit(solution)/shard_map/level0_down/reshape | solution.py:83
  9.6 4.0 %reduce_sum.37 = f32[16,16,512]{2,1,0:T(8,128)} reduce(f32[16,2,16,2,512]{4,3,2,1,0:T(2,128)} %reshape.400, f32[]{:T(128)} %constant.162.clone.1), dimensions={1,3}, to_apply=%region_1.2 | reduce | flops 393216 | bytes 2621444 | tf_op jit(solution)/shard_map/level0_down/reduce_sum | solution.py:83
  13.8 0.7 collective-permute-done.1
  14.6 3.8 %collective-permute-done = f32[3,4,32,512]{3,2,1,0:T(8,128)} collective-permute-done((f32[3,4,32,512]{3,2,1,0:T(8,128)}, f32[3,4,32,512]{3,2,1,0:T(8,128)}, u32[]{:S(2)}, u32[]{:S(2)}) %collective-permute-start) | collective-permute-done | bytes 786464 | tf_op jit(solution)/shard_map/level0_down/ppermute | solution.py:19
  18.4 2.4 %pad_maximum_fusion.6 = (f32[3,40,4,512]{3,2,1,0:T(4,128)S(1)}, f32[3,40,4,512]{3,2,1,0:T(4,128)S(1)}) fusion(f32[3,4,32,512]{3,2,1,0:T(8,128)S(1)} %collective-permute-done.1, f32[3,4,32,512]{3,2,1,0:T(8,128)} %collective-permute-done, f32[1,32,32,512]{3,2,1,0:T(8,128)S(1)} %bitcast.41, f32[1,32,32,512]{3,2,1,0:T(8,128)} %bitcast.44, ...), kind=kLoop, calls=%fused_computation.8 | loop fusion | flops 1966080 | bytes 9830400 | tf_op jit(solution)/shard_map/level0_down/slice | solution.py:19
  20.8 4.8 %collective-permute-start.3 = (f32[3,40,4,512]{3,2,1,0:T(4,128)S(1)}, f32[3,40,4,512]{3,2,1,0:T(4,128)S(1)}, u32[]{:S(2)}, u32[]{:S(2)}) collective-permute-start(f32[3,40,4,512]{3,2,1,0:T(4,128)S(1)} %get-tuple-element.10), channel_id=1, source_target_pairs={{1,0},{2,1},{3,2},{4,3},{5,4},{6,5},{7,6},{8,7},{9,8},{10,9},{11,1... | collective-permute-start | bytes 2949128 | tf_op jit(solution)/shard_map/level0_down/ppermute | solution.py:20
  25.5 1.9 %collective-permute-start.2 = (f32[3,40,4,512]{3,2,1,0:T(4,128)S(1)}, f32[3,40,4,512]{3,2,1,0:T(4,128)S(1)}, u32[]{:S(2)}, u32[]{:S(2)}) collective-permute-start(f32[3,40,4,512]{3,2,1,0:T(4,128)S(1)} %get-tuple-element.9), channel_id=1, source_target_pairs={{0,1},{1,2},{2,3},{3,4},{4,5},{5,6},{6,7},{7,8},{8,9},{9,10},{10,1... | collective-permute-start | bytes 2949128 | tf_op jit(solution)/shard_map/level0_down/ppermute | solution.py:19
  27.5 0.6 pad_add_fusion.off_ref
  28.3 0.8 fusion.12
  29.1 16.7 %collective-permute-done.3 = f32[3,40,4,512]{3,2,1,0:T(4,128)S(1)} collective-permute-done((f32[3,40,4,512]{3,2,1,0:T(4,128)S(1)}, f32[3,40,4,512]{3,2,1,0:T(4,128)S(1)}, u32[]{:S(2)}, u32[]{:S(2)}) %collective-permute-start.3) | collective-permute-done | bytes 983072 | tf_op jit(solution)/shard_map/level0_down/ppermute | solution.py:20
  45.8 6.2 %collective-permute-done.2 = f32[3,40,4,512]{3,2,1,0:T(4,128)S(1)} collective-permute-done((f32[3,40,4,512]{3,2,1,0:T(4,128)S(1)}, f32[3,40,4,512]{3,2,1,0:T(4,128)S(1)}, u32[]{:S(2)}, u32[]{:S(2)}) %collective-permute-start.2) | collective-permute-done | bytes 983072 | tf_op jit(solution)/shard_map/level0_down/ppermute | solution.py:19
  52.1 6.5 %pad_maximum_fusion.s_ref = f32[3,40,40,512]{3,2,1,0:T(8,128)} fusion(f32[3,40,4,512]{3,2,1,0:T(4,128)S(1)} %collective-permute-done.3, f32[3,4,32,512]{3,2,1,0:T(8,128)S(1)} %collective-permute-done.1, f32[1,32,32,512]{3,2,1,0:T(8,128)S(1)} %bitcast.42, f32[1,32,32,512]{3,2,1,0:T(8,128)S(1)} %bitcast.45, f32[1,32,32,512]{3,2,1,0:T(8,128)S(1)} %bitcast.48, ...), kind=kLoop, calls=%fused_computation | loop fusion | flops 14745600 | bytes 19660800 | tf_op jit(solution)/shard_map/level0_down/concatenate | solution.py:21
  58.5 24.9 %level0_down.1 = (f32[40,40,512]{2,1,0:T(8,128)}, f32[32,32,512]{2,1,0:T(8,128)}) custom-call(s32[2]{0:T(128)} %pad_add_fusion.off_ref, f32[3,40,40,512]{3,2,1,0:T(8,128)} %pad_maximum_fusion.s_ref), custom_call_target="tpu_custom_call" | custom-call | flops 98304000 | bytes 16384000 | tf_op jit(solution)/shard_map/level0_down/pallas_call | solution.py:294
  83.4 2.5 %reshape.399 = f32[16,2,16,2,512]{4,3,2,1,0:T(2,128)S(1)} reshape(f32[32,32,512]{2,1,0:T(8,128)} %get-tuple-element.8) | data formatting | bytes 4194304 | tf_op jit(solution)/shard_map/level0_down/reshape | solution.py:83
  85.9 1.5 reduce_sum.36
  87.5 0.8 fusion.14
  88.3 1.9 %collective-permute-start.5 = (f32[2,4,16,256]{3,2,1,0:T(8,128)S(1)}, f32[2,4,16,256]{3,2,1,0:T(8,128)S(1)}, u32[]{:S(2)}, u32[]{:S(2)}) collective-permute-start(f32[2,4,16,256]{3,2,1,0:T(8,128)S(1)} %get-tuple-element.38), channel_id=1, source_target_pairs={{16,0},{32,16},{48,32},{64,48},{80,64},{96,80},{112,96},{17,1},{33... | collective-permute-start | bytes 393224 | tf_op jit(solution)/shard_map/level1_down/ppermute | solution.py:20
  90.2 2.4 %collective-permute-start.4 = (f32[2,4,16,256]{3,2,1,0:T(8,128)S(1)}, f32[2,4,16,256]{3,2,1,0:T(8,128)S(1)}, u32[]{:S(2)}, u32[]{:S(2)}) collective-permute-start(f32[2,4,16,256]{3,2,1,0:T(8,128)S(1)} %get-tuple-element.37), channel_id=1, source_target_pairs={{0,16},{16,32},{32,48},{48,64},{64,80},{80,96},{96,112},{1,17},{17... | collective-permute-start | bytes 393224 | tf_op jit(solution)/shard_map/level1_down/ppermute | solution.py:19
  92.7 0.1 reshape.402
  92.8 0.2 reduce_sum.39
  93.0 0.4 convolution_bitcast_fusion
  93.4 3.1 %collective-permute-done.4 = f32[2,4,16,256]{3,2,1,0:T(8,128)S(1)} collective-permute-done((f32[2,4,16,256]{3,2,1,0:T(8,128)S(1)}, f32[2,4,16,256]{3,2,1,0:T(8,128)S(1)}, u32[]{:S(2)}, u32[]{:S(2)}) %collective-permute-start.4) | collective-permute-done | bytes 131104 | tf_op jit(solution)/shard_map/level1_down/ppermute | solution.py:19
  96.6 1.9 %collective-permute-start.7 = (f32[2,24,4,256]{3,2,1,0:T(4,128)S(1)}, f32[2,24,4,256]{3,2,1,0:T(4,128)S(1)}, u32[]{:S(2)}, u32[]{:S(2)}) collective-permute-start(f32[2,24,4,256]{3,2,1,0:T(4,128)S(1)} %get-tuple-element.16), channel_id=1, source_target_pairs={{1,0},{2,1},{3,2},{4,3},{5,4},{6,5},{7,6},{8,7},{9,8},{10,9},{11,1... | collective-permute-start | bytes 589832 | tf_op jit(solution)/shard_map/level1_down/ppermute | solution.py:20
  98.5 4.1 %collective-permute-start.6 = (f32[2,24,4,256]{3,2,1,0:T(4,128)S(1)}, f32[2,24,4,256]{3,2,1,0:T(4,128)S(1)}, u32[]{:S(2)}, u32[]{:S(2)}) collective-permute-start(f32[2,24,4,256]{3,2,1,0:T(4,128)S(1)} %get-tuple-element.15), channel_id=1, source_target_pairs={{0,1},{1,2},{2,3},{3,4},{4,5},{5,6},{6,7},{7,8},{8,9},{9,10},{10,1... | collective-permute-start | bytes 589832 | tf_op jit(solution)/shard_map/level1_down/ppermute | solution.py:19
  102.7 1.7 %collective-permute-done.7 = f32[2,24,4,256]{3,2,1,0:T(4,128)S(1)} collective-permute-done((f32[2,24,4,256]{3,2,1,0:T(4,128)S(1)}, f32[2,24,4,256]{3,2,1,0:T(4,128)S(1)}, u32[]{:S(2)}, u32[]{:S(2)}) %collective-permute-start.7) | collective-permute-done | bytes 196640 | tf_op jit(solution)/shard_map/level1_down/ppermute | solution.py:20
  104.4 4.0 %collective-permute-done.6 = f32[2,24,4,256]{3,2,1,0:T(4,128)S(1)} collective-permute-done((f32[2,24,4,256]{3,2,1,0:T(4,128)S(1)}, f32[2,24,4,256]{3,2,1,0:T(4,128)S(1)}, u32[]{:S(2)}, u32[]{:S(2)}) %collective-permute-start.6) | collective-permute-done | bytes 196640 | tf_op jit(solution)/shard_map/level1_down/ppermute | solution.py:19
  108.4 0.2 pad_maximum_fusion.1
  108.7 0.2 fusion.230
  108.9 0.1 fusion.231
  109.1 0.6 fusion.5
  109.8 0.2 fusion.233
  110.2 0.2 fusion.229
  110.4 1.2 fusion.39
  111.6 0.1 fusion.236
  111.9 0.1 fusion.227
  112.1 0.6 fusion.66
  112.6 0.1 reshape.401
  112.8 0.2 reduce_sum.38
  113.0 0.4 convolution_bitcast_fusion.1
  113.4 1.9 %collective-permute-start.9 = (f32[2,5,8,128]{3,2,1,0:T(8,128)S(1)}, f32[2,5,8,128]{3,2,1,0:T(8,128)S(1)}, u32[]{:S(2)}, u32[]{:S(2)}) collective-permute-start(f32[2,5,8,128]{3,2,1,0:T(8,128)S(1)} %get-tuple-element.80), channel_id=1, source_target_pairs={{16,0},{32,16},{48,32},{64,48},{80,64},{96,80},{112,96},{17,1},{33... | collective-permute-start | bytes 122888 | tf_op jit(solution)/shard_map/level2/ppermute | solution.py:20
  115.3 2.4 %collective-permute-start.8 = (f32[2,5,8,128]{3,2,1,0:T(8,128)S(1)}, f32[2,5,8,128]{3,2,1,0:T(8,128)S(1)}, u32[]{:S(2)}, u32[]{:S(2)}) collective-permute-start(f32[2,5,8,128]{3,2,1,0:T(8,128)S(1)} %get-tuple-element.79), channel_id=1, source_target_pairs={{0,16},{16,32},{32,48},{48,64},{64,80},{80,96},{96,112},{1,17},{17... | collective-permute-start | bytes 122888 | tf_op jit(solution)/shard_map/level2/ppermute | solution.py:19
  117.7 0.2 fusion.225
  117.9 2.7 %collective-permute-done.8 = f32[2,5,8,128]{3,2,1,0:T(8,128)S(1)} collective-permute-done((f32[2,5,8,128]{3,2,1,0:T(8,128)S(1)}, f32[2,5,8,128]{3,2,1,0:T(8,128)S(1)}, u32[]{:S(2)}, u32[]{:S(2)}) %collective-permute-start.8) | collective-permute-done | bytes 40992 | tf_op jit(solution)/shard_map/level2/ppermute | solution.py:19
  120.7 1.9 %collective-permute-start.11 = (f32[2,18,5,128]{3,2,1,0:T(8,128)S(1)}, f32[2,18,5,128]{3,2,1,0:T(8,128)S(1)}, u32[]{:S(2)}, u32[]{:S(2)}) collective-permute-start(f32[2,18,5,128]{3,2,1,0:T(8,128)S(1)} %get-tuple-element.66), channel_id=1, source_target_pairs={{1,0},{2,1},{3,2},{4,3},{5,4},{6,5},{7,6},{8,7},{9,8},{10,9},{11,1... | collective-permute-start | bytes 276488 | tf_op jit(solution)/shard_map/level2/ppermute | solution.py:20
  122.6 3.9 %collective-permute-start.10 = (f32[2,18,5,128]{3,2,1,0:T(8,128)S(1)}, f32[2,18,5,128]{3,2,1,0:T(8,128)S(1)}, u32[]{:S(2)}, u32[]{:S(2)}) collective-permute-start(f32[2,18,5,128]{3,2,1,0:T(8,128)S(1)} %get-tuple-element.65), channel_id=1, source_target_pairs={{0,1},{1,2},{2,3},{3,4},{4,5},{5,6},{6,7},{7,8},{8,9},{9,10},{10,1... | collective-permute-start | bytes 276488 | tf_op jit(solution)/shard_map/level2/ppermute | solution.py:19
  126.5 0.8 fusion.224
  127.4 0.4 collective-permute-done.11
  127.7 4.0 %collective-permute-done.10 = f32[2,18,5,128]{3,2,1,0:T(8,128)S(1)} collective-permute-done((f32[2,18,5,128]{3,2,1,0:T(8,128)S(1)}, f32[2,18,5,128]{3,2,1,0:T(8,128)S(1)}, u32[]{:S(2)}, u32[]{:S(2)}) %collective-permute-start.10) | collective-permute-done | bytes 92192 | tf_op jit(solution)/shard_map/level2/ppermute | solution.py:19
  132.1 0.2 fusion.105
  132.7 0.3 fusion.137
  133.4 0.3 fusion.158
  134.0 0.5 fusion.110
  134.6 0.1 broadcast_in_dim.188
  134.8 0.3 reshape.404
  135.1 0.2 fusion.234
  135.5 0.5 copy-done.4
  136.1 2.1 %fusion.10 = f32[18,18,512]{2,1,0:T(8,128)S(1)} fusion(f32[20,20,256]{2,1,0:T(8,128)S(1)} %add.696, f32[24,24,256]{2,1,0:T(8,128)S(1)} %get-tuple-element.13, f32[18,18,255]{2,1,0:T(8,128)S(1)} %get-tuple-element.40, f32[18,18,1]{2,1,0:T(8,128)S(1)} %get-tuple-element.42, f32[18,18,1]{2,1,0:T(8,128)S(1)} %get-tuple-element.41, ...), kind=kOutput, calls=%fused_computation.31 | convolution fusion | flops 513567744 | bytes 8192512 | tf_op jit(solution)/shard_map/level0_up/dot_general | solution.py:350
  138.2 0.5 broadcast_in_dim.192
  138.7 0.9 reshape.405
  139.6 1.3 pad.4.e_ref
  140.9 20.1 %level0_up.1 = f32[32,32,512]{2,1,0:T(8,128)} custom-call(s32[2]{0:T(128)} %pad_add_fusion.off_ref, f32[40,40,512]{2,1,0:T(8,128)} %get-tuple-element.7.u2_ref, f32[18,40,512]{2,1,0:T(8,128)} %pad.4.e_ref, f32[3,40,40,512]{3,2,1,0:T(8,128)} %pad_maximum_fusion.s_ref), custom_call_target="tpu_custom_call" | custom-call | flops 65536000 | bytes 16384000 | tf_op jit(solution)/shard_map/level0_up/pallas_call | solution.py:294
  (62 shorter events, 3.0 us)
Async XLA Ops:
  0.0 7.4 %copy-start = (f32[32,32,512]{2,1,0:T(8,128)S(1)}, f32[32,32,512]{2,1,0:T(8,128)}, u32[]{:S(2)}) copy-start(f32[32,32,512]{2,1,0:T(8,128)} %param.5) | copy-start | bytes 6291460
  2.9 11.7 %collective-permute-start.1 = (f32[3,4,32,512]{3,2,1,0:T(8,128)}, f32[3,4,32,512]{3,2,1,0:T(8,128)S(1)}, u32[]{:S(2)}, u32[]{:S(2)}) collective-permute-start(f32[3,4,32,512]{3,2,1,0:T(8,128)} %get-tuple-element.12), channel_id=1, source_target_pairs={{16,0},{32,16},{48,32},{64,48},{80,64},{96,80},{112,96},{17,1},{33... | collective-permute-start | bytes 2359304 | tf_op jit(solution)/shard_map/level0_down/ppermute | solution.py:20
  4.8 13.6 %collective-permute-start = (f32[3,4,32,512]{3,2,1,0:T(8,128)}, f32[3,4,32,512]{3,2,1,0:T(8,128)}, u32[]{:S(2)}, u32[]{:S(2)}) collective-permute-start(f32[3,4,32,512]{3,2,1,0:T(8,128)} %get-tuple-element.11), channel_id=1, source_target_pairs={{0,16},{16,32},{32,48},{48,64},{64,80},{80,96},{96,112},{1,17},{17... | collective-permute-start | bytes 2359304 | tf_op jit(solution)/shard_map/level0_down/ppermute | solution.py:19
  13.8 14.5 %copy-start.3 = (f32[16,16,512]{2,1,0:T(8,128)S(1)}, f32[16,16,512]{2,1,0:T(8,128)}, u32[]{:S(2)}) copy-start(f32[16,16,512]{2,1,0:T(8,128)} %reduce_sum.37) | copy-start | bytes 1572868
  18.4 33.7 %copy-start.1 = (f32[32,32,512]{2,1,0:T(8,128)S(1)}, f32[32,32,512]{2,1,0:T(8,128)}, u32[]{:S(2)}) copy-start(f32[32,32,512]{2,1,0:T(8,128)} %param.4) | copy-start | bytes 6291460
  18.4 33.7 %copy-start.2 = (f32[32,32,512]{2,1,0:T(8,128)S(1)}, f32[32,32,512]{2,1,0:T(8,128)}, u32[]{:S(2)}) copy-start(f32[32,32,512]{2,1,0:T(8,128)} %param.3) | copy-start | bytes 6291460
  20.8 25.1 %collective-permute-start.3 = (f32[3,40,4,512]{3,2,1,0:T(4,128)S(1)}, f32[3,40,4,512]{3,2,1,0:T(4,128)S(1)}, u32[]{:S(2)}, u32[]{:S(2)}) collective-permute-start(f32[3,40,4,512]{3,2,1,0:T(4,128)S(1)} %get-tuple-element.10), channel_id=1, source_target_pairs={{1,0},{2,1},{3,2},{4,3},{5,4},{6,5},{7,6},{8,7},{9,8},{10,9},{11,1... | collective-permute-start | bytes 2949128 | tf_op jit(solution)/shard_map/level0_down/ppermute | solution.py:20
  25.5 26.5 %collective-permute-start.2 = (f32[3,40,4,512]{3,2,1,0:T(4,128)S(1)}, f32[3,40,4,512]{3,2,1,0:T(4,128)S(1)}, u32[]{:S(2)}, u32[]{:S(2)}) collective-permute-start(f32[3,40,4,512]{3,2,1,0:T(4,128)S(1)} %get-tuple-element.9), channel_id=1, source_target_pairs={{0,1},{1,2},{2,3},{3,4},{4,5},{5,6},{6,7},{7,8},{8,9},{9,10},{10,1... | collective-permute-start | bytes 2949128 | tf_op jit(solution)/shard_map/level0_down/ppermute | solution.py:19
  88.3 5.1 %collective-permute-start.5 = (f32[2,4,16,256]{3,2,1,0:T(8,128)S(1)}, f32[2,4,16,256]{3,2,1,0:T(8,128)S(1)}, u32[]{:S(2)}, u32[]{:S(2)}) collective-permute-start(f32[2,4,16,256]{3,2,1,0:T(8,128)S(1)} %get-tuple-element.38), channel_id=1, source_target_pairs={{16,0},{32,16},{48,32},{64,48},{80,64},{96,80},{112,96},{17,1},{33... | collective-permute-start | bytes 393224 | tf_op jit(solution)/shard_map/level1_down/ppermute | solution.py:20
  90.2 6.3 %collective-permute-start.4 = (f32[2,4,16,256]{3,2,1,0:T(8,128)S(1)}, f32[2,4,16,256]{3,2,1,0:T(8,128)S(1)}, u32[]{:S(2)}, u32[]{:S(2)}) collective-permute-start(f32[2,4,16,256]{3,2,1,0:T(8,128)S(1)} %get-tuple-element.37), channel_id=1, source_target_pairs={{0,16},{16,32},{32,48},{48,64},{64,80},{80,96},{96,112},{1,17},{17... | collective-permute-start | bytes 393224 | tf_op jit(solution)/shard_map/level1_down/ppermute | solution.py:19
  96.6 7.8 %collective-permute-start.7 = (f32[2,24,4,256]{3,2,1,0:T(4,128)S(1)}, f32[2,24,4,256]{3,2,1,0:T(4,128)S(1)}, u32[]{:S(2)}, u32[]{:S(2)}) collective-permute-start(f32[2,24,4,256]{3,2,1,0:T(4,128)S(1)} %get-tuple-element.16), channel_id=1, source_target_pairs={{1,0},{2,1},{3,2},{4,3},{5,4},{6,5},{7,6},{8,7},{9,8},{10,9},{11,1... | collective-permute-start | bytes 589832 | tf_op jit(solution)/shard_map/level1_down/ppermute | solution.py:20
  98.5 9.9 %collective-permute-start.6 = (f32[2,24,4,256]{3,2,1,0:T(4,128)S(1)}, f32[2,24,4,256]{3,2,1,0:T(4,128)S(1)}, u32[]{:S(2)}, u32[]{:S(2)}) collective-permute-start(f32[2,24,4,256]{3,2,1,0:T(4,128)S(1)} %get-tuple-element.15), channel_id=1, source_target_pairs={{0,1},{1,2},{2,3},{3,4},{4,5},{5,6},{6,7},{7,8},{8,9},{9,10},{10,1... | collective-permute-start | bytes 589832 | tf_op jit(solution)/shard_map/level1_down/ppermute | solution.py:19
  113.4 4.5 %collective-permute-start.9 = (f32[2,5,8,128]{3,2,1,0:T(8,128)S(1)}, f32[2,5,8,128]{3,2,1,0:T(8,128)S(1)}, u32[]{:S(2)}, u32[]{:S(2)}) collective-permute-start(f32[2,5,8,128]{3,2,1,0:T(8,128)S(1)} %get-tuple-element.80), channel_id=1, source_target_pairs={{16,0},{32,16},{48,32},{64,48},{80,64},{96,80},{112,96},{17,1},{33... | collective-permute-start | bytes 122888 | tf_op jit(solution)/shard_map/level2/ppermute | solution.py:20
  115.3 5.3 %collective-permute-start.8 = (f32[2,5,8,128]{3,2,1,0:T(8,128)S(1)}, f32[2,5,8,128]{3,2,1,0:T(8,128)S(1)}, u32[]{:S(2)}, u32[]{:S(2)}) collective-permute-start(f32[2,5,8,128]{3,2,1,0:T(8,128)S(1)} %get-tuple-element.79), channel_id=1, source_target_pairs={{0,16},{16,32},{32,48},{48,64},{64,80},{80,96},{96,112},{1,17},{17... | collective-permute-start | bytes 122888 | tf_op jit(solution)/shard_map/level2/ppermute | solution.py:19
  120.7 7.0 %collective-permute-start.11 = (f32[2,18,5,128]{3,2,1,0:T(8,128)S(1)}, f32[2,18,5,128]{3,2,1,0:T(8,128)S(1)}, u32[]{:S(2)}, u32[]{:S(2)}) collective-permute-start(f32[2,18,5,128]{3,2,1,0:T(8,128)S(1)} %get-tuple-element.66), channel_id=1, source_target_pairs={{1,0},{2,1},{3,2},{4,3},{5,4},{6,5},{7,6},{8,7},{9,8},{10,9},{11,1... | collective-permute-start | bytes 276488 | tf_op jit(solution)/shard_map/level2/ppermute | solution.py:20
  122.6 9.1 %collective-permute-start.10 = (f32[2,18,5,128]{3,2,1,0:T(8,128)S(1)}, f32[2,18,5,128]{3,2,1,0:T(8,128)S(1)}, u32[]{:S(2)}, u32[]{:S(2)}) collective-permute-start(f32[2,18,5,128]{3,2,1,0:T(8,128)S(1)} %get-tuple-element.65), channel_id=1, source_target_pairs={{0,1},{1,2},{2,3},{3,4},{4,5},{5,6},{6,7},{7,8},{8,9},{9,10},{10,1... | collective-permute-start | bytes 276488 | tf_op jit(solution)/shard_map/level2/ppermute | solution.py:19
  135.0 0.9 copy-start.4
  135.1 1.0 copy-start.5

commit v5 on v4

--- a/solution.py
+++ b/solution.py
@@ -11,7 +11,7 @@
 
 
 def exchange(stack, width):
-    for axis, dim in (("row", 1), ("col", 2)):
+    for axis, dim in (("col", 2), ("row", 1)):
         count = lax.axis_size(axis)
         forward = [(i, i + 1) for i in range(count - 1)]
         backward = [(i + 1, i) for i in range(count - 1)]

time: 162 us -> 161 us (level)
    ppermute x6, waiting for transfers between devices: 19.6 us -> 17 us  [exchange(): lax.ppermute(lax.slice_in_dim(stack, 0, width, axis=dim), axis, backward)]
  transfers between devices with their start and end apart: 12 -> 12, of which waited for: 10 -> 11; matrix products, arithmetic and copies ran while one was open for 6% -> 6% of each run, Pallas kernels for 0% -> 0%
where the time goes in v5:
time: 161 us
  Pallas kernels  45 us (28%)
  waiting for transfers between devices  41.9 us (26%)
  starting transfers between devices  31.5 us (20%)
  other arithmetic  23.8 us (15%)
  local copies, waits for them, and re-layouts  13.1 us (8%)
  matrix products  4.91 us (3%)
    pallas_call x2, Pallas kernels, _frame_call(): pl.pallas_call(kernel, grid=(1,), out_shape=outs, in_specs=[pl.BlockSpec(...  45 us
    ppermute x6, waiting for transfers between devices, exchange(): lax.ppermute(lax.slice_in_dim(stack, size - width, size, axis=dim), axis,...  24.9 us
    ppermute x6, starting transfers between devices, exchange(): lax.ppermute(lax.slice_in_dim(stack, size - width, size, axis=dim), axis,...  17.2 us
    ppermute x6, waiting for transfers between devices, exchange(): lax.ppermute(lax.slice_in_dim(stack, 0, width, axis=dim), axis, backward)  17 us
    ppermute x6, starting transfers between devices, exchange(): lax.ppermute(lax.slice_in_dim(stack, 0, width, axis=dim), axis, backward)  14.4 us
    concatenate x4, other arithmetic, exchange(): stack = jnp.concatenate([low, stack, high], axis=dim)  8.08 us
    reduce_sum x4, other arithmetic, restrict_mean(): field.reshape(field.shape[0] // 2, 2, field.shape[1] // 2, 2, depth)  5.89 us
    slice x4, other arithmetic, exchange(): lax.slice_in_dim(stack, size - width, size, axis=dim)  5.38 us
  transfers between devices with their start and end apart: 12, of which 11 were waited for; matrix products, arithmetic and copies ran while one was open for 6% of the time, Pallas kernels for 0%

profile of v5, /device:TPU:98, one launch (start us, length us, event | category | flops | bytes accessed | tf_op | source)
XLA Modules:
  0.0 160.8 jit_solution(17372686660162845593)
XLA Ops:
  0.0 3.6 %pad_maximum_fusion.9 = (f32[3,32,4,512]{3,2,1,0:T(4,128)}, f32[3,32,4,512]{3,2,1,0:T(4,128)}) fusion(f32[1,32,32,512]{3,2,1,0:T(8,128)} %bitcast.40, f32[1,32,32,512]{3,2,1,0:T(8,128)} %bitcast.43, f32[1,32,32,512]{3,2,1,0:T(8,128)} %bitcast.46), kind=kLoop, calls=%fused_computation.11 | loop fusion | flops 786432 | bytes 7864320 | tf_op jit(solution)/shard_map/level0_down/slice | solution.py:19
  3.6 4.7 %collective-permute-start.1 = (f32[3,32,4,512]{3,2,1,0:T(4,128)}, f32[3,32,4,512]{3,2,1,0:T(4,128)S(1)}, u32[]{:S(2)}, u32[]{:S(2)}) collective-permute-start(f32[3,32,4,512]{3,2,1,0:T(4,128)} %get-tuple-element.12), channel_id=1, source_target_pairs={{1,0},{2,1},{3,2},{4,3},{5,4},{6,5},{7,6},{8,7},{9,8},{10,9},{11,1... | collective-permute-start | bytes 2359304 | tf_op jit(solution)/shard_map/level0_down/ppermute | solution.py:20
  8.3 1.9 %collective-permute-start = (f32[3,32,4,512]{3,2,1,0:T(4,128)}, f32[3,32,4,512]{3,2,1,0:T(4,128)}, u32[]{:S(2)}, u32[]{:S(2)}) collective-permute-start(f32[3,32,4,512]{3,2,1,0:T(4,128)} %get-tuple-element.11), channel_id=1, source_target_pairs={{0,1},{1,2},{2,3},{3,4},{4,5},{5,6},{6,7},{7,8},{8,9},{9,10},{10,1... | collective-permute-start | bytes 2359304 | tf_op jit(solution)/shard_map/level0_down/ppermute | solution.py:19
  10.4 2.2 %reshape.400 = f32[16,2,16,2,512]{4,3,2,1,0:T(2,128)} reshape(f32[32,32,512]{2,1,0:T(8,128)S(1)} %copy-done) | data formatting | bytes 4194304 | tf_op jit(solution)/shard_map/level0_down/reshape | solution.py:83
  12.7 4.0 %reduce_sum.37 = f32[16,16,512]{2,1,0:T(8,128)} reduce(f32[16,2,16,2,512]{4,3,2,1,0:T(2,128)} %reshape.400, f32[]{:T(128)} %constant.162.clone.1), dimensions={1,3}, to_apply=%region_1.2 | reduce | flops 393216 | bytes 2621444 | tf_op jit(solution)/shard_map/level0_down/reduce_sum | solution.py:83
  16.9 8.5 %collective-permute-done.1 = f32[3,32,4,512]{3,2,1,0:T(4,128)S(1)} collective-permute-done((f32[3,32,4,512]{3,2,1,0:T(4,128)}, f32[3,32,4,512]{3,2,1,0:T(4,128)S(1)}, u32[]{:S(2)}, u32[]{:S(2)}) %collective-permute-start.1) | collective-permute-done | bytes 786464 | tf_op jit(solution)/shard_map/level0_down/ppermute | solution.py:20
  25.4 6.2 %collective-permute-done = f32[3,32,4,512]{3,2,1,0:T(4,128)} collective-permute-done((f32[3,32,4,512]{3,2,1,0:T(4,128)}, f32[3,32,4,512]{3,2,1,0:T(4,128)}, u32[]{:S(2)}, u32[]{:S(2)}) %collective-permute-start) | collective-permute-done | bytes 786464 | tf_op jit(solution)/shard_map/level0_down/ppermute | solution.py:19
  31.6 1.7 %pad_maximum_fusion.6 = (f32[3,4,40,512]{3,2,1,0:T(8,128)S(1)}, f32[3,4,40,512]{3,2,1,0:T(8,128)S(1)}) fusion(f32[3,32,4,512]{3,2,1,0:T(4,128)S(1)} %collective-permute-done.1, f32[3,32,4,512]{3,2,1,0:T(4,128)} %collective-permute-done, f32[1,32,32,512]{3,2,1,0:T(8,128)S(1)} %bitcast.41, f32[1,32,32,512]{3,2,1,0:T(8,128)} %bitcast.44, ...), kind=kLoop, calls=%fused_computation.8 | loop fusion | flops 1966080 | bytes 9830400 | tf_op jit(solution)/shard_map/level0_down/slice | solution.py:19
  33.4 1.9 %collective-permute-start.3 = (f32[3,4,40,512]{3,2,1,0:T(8,128)S(1)}, f32[3,4,40,512]{3,2,1,0:T(8,128)S(1)}, u32[]{:S(2)}, u32[]{:S(2)}) collective-permute-start(f32[3,4,40,512]{3,2,1,0:T(8,128)S(1)} %get-tuple-element.10), channel_id=1, source_target_pairs={{16,0},{32,16},{48,32},{64,48},{80,64},{96,80},{112,96},{17,1},{33... | collective-permute-start | bytes 2949128 | tf_op jit(solution)/shard_map/level0_down/ppermute | solution.py:20
  35.3 2.4 %collective-permute-start.2 = (f32[3,4,40,512]{3,2,1,0:T(8,128)S(1)}, f32[3,4,40,512]{3,2,1,0:T(8,128)S(1)}, u32[]{:S(2)}, u32[]{:S(2)}) collective-permute-start(f32[3,4,40,512]{3,2,1,0:T(8,128)S(1)} %get-tuple-element.9), channel_id=1, source_target_pairs={{0,16},{16,32},{32,48},{48,64},{64,80},{80,96},{96,112},{1,17},{17... | collective-permute-start | bytes 2949128 | tf_op jit(solution)/shard_map/level0_down/ppermute | solution.py:19
  37.7 0.6 pad_add_fusion.off_ref
  38.5 0.8 fusion.12
  39.3 7.6 %collective-permute-done.3 = f32[3,4,40,512]{3,2,1,0:T(8,128)S(1)} collective-permute-done((f32[3,4,40,512]{3,2,1,0:T(8,128)S(1)}, f32[3,4,40,512]{3,2,1,0:T(8,128)S(1)}, u32[]{:S(2)}, u32[]{:S(2)}) %collective-permute-start.3) | collective-permute-done | bytes 983072 | tf_op jit(solution)/shard_map/level0_down/ppermute | solution.py:20
  46.9 3.8 %collective-permute-done.2 = f32[3,4,40,512]{3,2,1,0:T(8,128)S(1)} collective-permute-done((f32[3,4,40,512]{3,2,1,0:T(8,128)S(1)}, f32[3,4,40,512]{3,2,1,0:T(8,128)S(1)}, u32[]{:S(2)}, u32[]{:S(2)}) %collective-permute-start.2) | collective-permute-done | bytes 983072 | tf_op jit(solution)/shard_map/level0_down/ppermute | solution.py:19
  50.7 7.9 %pad_maximum_fusion.s_ref = f32[3,40,40,512]{3,2,1,0:T(8,128)} fusion(f32[3,4,40,512]{3,2,1,0:T(8,128)S(1)} %collective-permute-done.3, f32[3,32,4,512]{3,2,1,0:T(4,128)S(1)} %collective-permute-done.1, f32[1,32,32,512]{3,2,1,0:T(8,128)S(1)} %bitcast.42, f32[1,32,32,512]{3,2,1,0:T(8,128)S(1)} %bitcast.45, f32[1,32,32,512]{3,2,1,0:T(8,128)S(1)} %bitcast.48, ...), kind=kLoop, calls=%fused_computation | loop fusion | flops 14745600 | bytes 19660800 | tf_op jit(solution)/shard_map/level0_down/concatenate | solution.py:21
  58.6 24.9 %level0_down.1 = (f32[40,40,512]{2,1,0:T(8,128)}, f32[32,32,512]{2,1,0:T(8,128)}) custom-call(s32[2]{0:T(128)} %pad_add_fusion.off_ref, f32[3,40,40,512]{3,2,1,0:T(8,128)} %pad_maximum_fusion.s_ref), custom_call_target="tpu_custom_call" | custom-call | flops 98304000 | bytes 16384000 | tf_op jit(solution)/shard_map/level0_down/pallas_call | solution.py:294
  83.5 2.5 %reshape.399 = f32[16,2,16,2,512]{4,3,2,1,0:T(2,128)S(1)} reshape(f32[32,32,512]{2,1,0:T(8,128)} %get-tuple-element.8) | data formatting | bytes 4194304 | tf_op jit(solution)/shard_map/level0_down/reshape | solution.py:83
  86.0 1.5 reduce_sum.36
  87.6 0.8 fusion.14
  88.4 1.9 %collective-permute-start.5 = (f32[2,16,4,256]{3,2,1,0:T(4,128)S(1)}, f32[2,16,4,256]{3,2,1,0:T(4,128)S(1)}, u32[]{:S(2)}, u32[]{:S(2)}) collective-permute-start(f32[2,16,4,256]{3,2,1,0:T(4,128)S(1)} %get-tuple-element.38), channel_id=1, source_target_pairs={{1,0},{2,1},{3,2},{4,3},{5,4},{6,5},{7,6},{8,7},{9,8},{10,9},{11,1... | collective-permute-start | bytes 393224 | tf_op jit(solution)/shard_map/level1_down/ppermute | solution.py:20
  90.3 3.9 %collective-permute-start.4 = (f32[2,16,4,256]{3,2,1,0:T(4,128)S(1)}, f32[2,16,4,256]{3,2,1,0:T(4,128)S(1)}, u32[]{:S(2)}, u32[]{:S(2)}) collective-permute-start(f32[2,16,4,256]{3,2,1,0:T(4,128)S(1)} %get-tuple-element.37), channel_id=1, source_target_pairs={{0,1},{1,2},{2,3},{3,4},{4,5},{5,6},{6,7},{7,8},{8,9},{9,10},{10,1... | collective-permute-start | bytes 393224 | tf_op jit(solution)/shard_map/level1_down/ppermute | solution.py:19
  94.3 0.1 reshape.402
  94.4 0.2 reduce_sum.39
  94.6 0.4 convolution_bitcast_fusion
  95.0 0.3 collective-permute-done.5
  95.3 4.0 %collective-permute-done.4 = f32[2,16,4,256]{3,2,1,0:T(4,128)S(1)} collective-permute-done((f32[2,16,4,256]{3,2,1,0:T(4,128)S(1)}, f32[2,16,4,256]{3,2,1,0:T(4,128)S(1)}, u32[]{:S(2)}, u32[]{:S(2)}) %collective-permute-start.4) | collective-permute-done | bytes 131104 | tf_op jit(solution)/shard_map/level1_down/ppermute | solution.py:19
  99.4 1.9 %collective-permute-start.7 = (f32[2,4,24,256]{3,2,1,0:T(8,128)S(1)}, f32[2,4,24,256]{3,2,1,0:T(8,128)S(1)}, u32[]{:S(2)}, u32[]{:S(2)}) collective-permute-start(f32[2,4,24,256]{3,2,1,0:T(8,128)S(1)} %get-tuple-element.16), channel_id=1, source_target_pairs={{16,0},{32,16},{48,32},{64,48},{80,64},{96,80},{112,96},{17,1},{33... | collective-permute-start | bytes 589832 | tf_op jit(solution)/shard_map/level1_down/ppermute | solution.py:20
  101.3 2.6 %collective-permute-start.6 = (f32[2,4,24,256]{3,2,1,0:T(8,128)S(1)}, f32[2,4,24,256]{3,2,1,0:T(8,128)S(1)}, u32[]{:S(2)}, u32[]{:S(2)}) collective-permute-start(f32[2,4,24,256]{3,2,1,0:T(8,128)S(1)} %get-tuple-element.15), channel_id=1, source_target_pairs={{0,16},{16,32},{32,48},{48,64},{64,80},{80,96},{96,112},{1,17},{17... | collective-permute-start | bytes 589832 | tf_op jit(solution)/shard_map/level1_down/ppermute | solution.py:19
  104.0 0.5 collective-permute-done.7
  104.5 3.8 %collective-permute-done.6 = f32[2,4,24,256]{3,2,1,0:T(8,128)S(1)} collective-permute-done((f32[2,4,24,256]{3,2,1,0:T(8,128)S(1)}, f32[2,4,24,256]{3,2,1,0:T(8,128)S(1)}, u32[]{:S(2)}, u32[]{:S(2)}) %collective-permute-start.6) | collective-permute-done | bytes 196640 | tf_op jit(solution)/shard_map/level1_down/ppermute | solution.py:19
  108.3 0.1 pad_maximum_fusion.1
  108.5 0.2 fusion.229
  108.7 0.1 fusion.230
  108.9 0.6 fusion.5
  109.6 0.2 fusion.232
  110.0 0.2 fusion.228
  110.2 1.2 fusion.39
  111.4 0.1 fusion.235
  111.7 0.1 fusion.226
  111.9 0.6 fusion.66
  112.5 0.1 reshape.401
  112.6 0.2 reduce_sum.38
  112.8 0.4 convolution_bitcast_fusion.1
  113.2 1.9 %collective-permute-start.9 = (f32[2,8,5,128]{3,2,1,0:T(8,128)S(1)}, f32[2,8,5,128]{3,2,1,0:T(8,128)S(1)}, u32[]{:S(2)}, u32[]{:S(2)}) collective-permute-start(f32[2,8,5,128]{3,2,1,0:T(8,128)S(1)} %get-tuple-element.80), channel_id=1, source_target_pairs={{1,0},{2,1},{3,2},{4,3},{5,4},{6,5},{7,6},{8,7},{9,8},{10,9},{11,1... | collective-permute-start | bytes 122888 | tf_op jit(solution)/shard_map/level2/ppermute | solution.py:20
  115.1 3.9 %collective-permute-start.8 = (f32[2,8,5,128]{3,2,1,0:T(8,128)S(1)}, f32[2,8,5,128]{3,2,1,0:T(8,128)S(1)}, u32[]{:S(2)}, u32[]{:S(2)}) collective-permute-start(f32[2,8,5,128]{3,2,1,0:T(8,128)S(1)} %get-tuple-element.79), channel_id=1, source_target_pairs={{0,1},{1,2},{2,3},{3,4},{4,5},{5,6},{6,7},{7,8},{8,9},{9,10},{10,1... | collective-permute-start | bytes 122888 | tf_op jit(solution)/shard_map/level2/ppermute | solution.py:19
  119.0 0.2 fusion.224
  119.3 4.0 %collective-permute-done.8 = f32[2,8,5,128]{3,2,1,0:T(8,128)S(1)} collective-permute-done((f32[2,8,5,128]{3,2,1,0:T(8,128)S(1)}, f32[2,8,5,128]{3,2,1,0:T(8,128)S(1)}, u32[]{:S(2)}, u32[]{:S(2)}) %collective-permute-start.8) | collective-permute-done | bytes 40992 | tf_op jit(solution)/shard_map/level2/ppermute | solution.py:19
  123.4 1.9 %collective-permute-start.11 = (f32[2,5,18,128]{3,2,1,0:T(8,128)S(1)}, f32[2,5,18,128]{3,2,1,0:T(8,128)S(1)}, u32[]{:S(2)}, u32[]{:S(2)}) collective-permute-start(f32[2,5,18,128]{3,2,1,0:T(8,128)S(1)} %get-tuple-element.66), channel_id=1, source_target_pairs={{16,0},{32,16},{48,32},{64,48},{80,64},{96,80},{112,96},{17,1},{33... | collective-permute-start | bytes 276488 | tf_op jit(solution)/shard_map/level2/ppermute | solution.py:20
  125.4 2.4 %collective-permute-start.10 = (f32[2,5,18,128]{3,2,1,0:T(8,128)S(1)}, f32[2,5,18,128]{3,2,1,0:T(8,128)S(1)}, u32[]{:S(2)}, u32[]{:S(2)}) collective-permute-start(f32[2,5,18,128]{3,2,1,0:T(8,128)S(1)} %get-tuple-element.65), channel_id=1, source_target_pairs={{0,16},{16,32},{32,48},{48,64},{64,80},{80,96},{96,112},{1,17},{17... | collective-permute-start | bytes 276488 | tf_op jit(solution)/shard_map/level2/ppermute | solution.py:19
  127.8 0.8 fusion.223
  128.6 3.0 %collective-permute-done.10 = f32[2,5,18,128]{3,2,1,0:T(8,128)S(1)} collective-permute-done((f32[2,5,18,128]{3,2,1,0:T(8,128)S(1)}, f32[2,5,18,128]{3,2,1,0:T(8,128)S(1)}, u32[]{:S(2)}, u32[]{:S(2)}) %collective-permute-start.10) | collective-permute-done | bytes 92192 | tf_op jit(solution)/shard_map/level2/ppermute | solution.py:19
  131.9 0.2 fusion.105
  132.5 0.3 fusion.137
  133.2 0.3 fusion.158
  133.8 0.5 fusion.110
  134.4 0.1 broadcast_in_dim.188
  134.6 0.3 reshape.404
  134.9 0.2 fusion.233
  135.3 0.5 copy-done.4
  135.9 2.1 %fusion.10 = f32[18,18,512]{2,1,0:T(8,128)S(1)} fusion(f32[20,20,256]{2,1,0:T(8,128)S(1)} %add.696, f32[24,24,256]{2,1,0:T(8,128)S(1)} %get-tuple-element.13, f32[18,18,255]{2,1,0:T(8,128)S(1)} %get-tuple-element.40, f32[18,18,1]{2,1,0:T(8,128)S(1)} %get-tuple-element.42, f32[18,18,1]{2,1,0:T(8,128)S(1)} %get-tuple-element.41, ...), kind=kOutput, calls=%fused_computation.31 | convolution fusion | flops 513567744 | bytes 8192512 | tf_op jit(solution)/shard_map/level0_up/dot_general | solution.py:350
  138.0 0.5 broadcast_in_dim.192
  138.5 0.9 reshape.405
  139.4 1.3 pad.4.e_ref
  140.7 20.1 %level0_up.1 = f32[32,32,512]{2,1,0:T(8,128)} custom-call(s32[2]{0:T(128)} %pad_add_fusion.off_ref, f32[40,40,512]{2,1,0:T(8,128)} %get-tuple-element.7.u2_ref, f32[18,40,512]{2,1,0:T(8,128)} %pad.4.e_ref, f32[3,40,40,512]{3,2,1,0:T(8,128)} %pad_maximum_fusion.s_ref), custom_call_target="tpu_custom_call" | custom-call | flops 65536000 | bytes 16384000 | tf_op jit(solution)/shard_map/level0_up/pallas_call | solution.py:294
  (62 shorter events, 3.1 us)
Async XLA Ops:
  0.0 10.4 %copy-start = (f32[32,32,512]{2,1,0:T(8,128)S(1)}, f32[32,32,512]{2,1,0:T(8,128)}, u32[]{:S(2)}) copy-start(f32[32,32,512]{2,1,0:T(8,128)} %param.5) | copy-start | bytes 6291460
  3.6 21.8 %collective-permute-start.1 = (f32[3,32,4,512]{3,2,1,0:T(4,128)}, f32[3,32,4,512]{3,2,1,0:T(4,128)S(1)}, u32[]{:S(2)}, u32[]{:S(2)}) collective-permute-start(f32[3,32,4,512]{3,2,1,0:T(4,128)} %get-tuple-element.12), channel_id=1, source_target_pairs={{1,0},{2,1},{3,2},{4,3},{5,4},{6,5},{7,6},{8,7},{9,8},{10,9},{11,1... | collective-permute-start | bytes 2359304 | tf_op jit(solution)/shard_map/level0_down/ppermute | solution.py:20
  8.3 23.3 %collective-permute-start = (f32[3,32,4,512]{3,2,1,0:T(4,128)}, f32[3,32,4,512]{3,2,1,0:T(4,128)}, u32[]{:S(2)}, u32[]{:S(2)}) collective-permute-start(f32[3,32,4,512]{3,2,1,0:T(4,128)} %get-tuple-element.11), channel_id=1, source_target_pairs={{0,1},{1,2},{2,3},{3,4},{4,5},{5,6},{6,7},{7,8},{8,9},{9,10},{10,1... | collective-permute-start | bytes 2359304 | tf_op jit(solution)/shard_map/level0_down/ppermute | solution.py:19
  16.9 21.6 %copy-start.3 = (f32[16,16,512]{2,1,0:T(8,128)S(1)}, f32[16,16,512]{2,1,0:T(8,128)}, u32[]{:S(2)}) copy-start(f32[16,16,512]{2,1,0:T(8,128)} %reduce_sum.37) | copy-start | bytes 1572868
  31.6 19.1 %copy-start.1 = (f32[32,32,512]{2,1,0:T(8,128)S(1)}, f32[32,32,512]{2,1,0:T(8,128)}, u32[]{:S(2)}) copy-start(f32[32,32,512]{2,1,0:T(8,128)} %param.4) | copy-start | bytes 6291460
  31.6 19.1 %copy-start.2 = (f32[32,32,512]{2,1,0:T(8,128)S(1)}, f32[32,32,512]{2,1,0:T(8,128)}, u32[]{:S(2)}) copy-start(f32[32,32,512]{2,1,0:T(8,128)} %param.3) | copy-start | bytes 6291460
  33.4 13.5 %collective-permute-start.3 = (f32[3,4,40,512]{3,2,1,0:T(8,128)S(1)}, f32[3,4,40,512]{3,2,1,0:T(8,128)S(1)}, u32[]{:S(2)}, u32[]{:S(2)}) collective-permute-start(f32[3,4,40,512]{3,2,1,0:T(8,128)S(1)} %get-tuple-element.10), channel_id=1, source_target_pairs={{16,0},{32,16},{48,32},{64,48},{80,64},{96,80},{112,96},{17,1},{33... | collective-permute-start | bytes 2949128 | tf_op jit(solution)/shard_map/level0_down/ppermute | solution.py:20
  35.3 15.4 %collective-permute-start.2 = (f32[3,4,40,512]{3,2,1,0:T(8,128)S(1)}, f32[3,4,40,512]{3,2,1,0:T(8,128)S(1)}, u32[]{:S(2)}, u32[]{:S(2)}) collective-permute-start(f32[3,4,40,512]{3,2,1,0:T(8,128)S(1)} %get-tuple-element.9), channel_id=1, source_target_pairs={{0,16},{16,32},{32,48},{48,64},{64,80},{80,96},{96,112},{1,17},{17... | collective-permute-start | bytes 2949128 | tf_op jit(solution)/shard_map/level0_down/ppermute | solution.py:19
  88.4 6.9 %collective-permute-start.5 = (f32[2,16,4,256]{3,2,1,0:T(4,128)S(1)}, f32[2,16,4,256]{3,2,1,0:T(4,128)S(1)}, u32[]{:S(2)}, u32[]{:S(2)}) collective-permute-start(f32[2,16,4,256]{3,2,1,0:T(4,128)S(1)} %get-tuple-element.38), channel_id=1, source_target_pairs={{1,0},{2,1},{3,2},{4,3},{5,4},{6,5},{7,6},{8,7},{9,8},{10,9},{11,1... | collective-permute-start | bytes 393224 | tf_op jit(solution)/shard_map/level1_down/ppermute | solution.py:20
  90.3 9.0 %collective-permute-start.4 = (f32[2,16,4,256]{3,2,1,0:T(4,128)S(1)}, f32[2,16,4,256]{3,2,1,0:T(4,128)S(1)}, u32[]{:S(2)}, u32[]{:S(2)}) collective-permute-start(f32[2,16,4,256]{3,2,1,0:T(4,128)S(1)} %get-tuple-element.37), channel_id=1, source_target_pairs={{0,1},{1,2},{2,3},{3,4},{4,5},{5,6},{6,7},{7,8},{8,9},{9,10},{10,1... | collective-permute-start | bytes 393224 | tf_op jit(solution)/shard_map/level1_down/ppermute | solution.py:19
  99.4 5.1 %collective-permute-start.7 = (f32[2,4,24,256]{3,2,1,0:T(8,128)S(1)}, f32[2,4,24,256]{3,2,1,0:T(8,128)S(1)}, u32[]{:S(2)}, u32[]{:S(2)}) collective-permute-start(f32[2,4,24,256]{3,2,1,0:T(8,128)S(1)} %get-tuple-element.16), channel_id=1, source_target_pairs={{16,0},{32,16},{48,32},{64,48},{80,64},{96,80},{112,96},{17,1},{33... | collective-permute-start | bytes 589832 | tf_op jit(solution)/shard_map/level1_down/ppermute | solution.py:20
  101.3 7.0 %collective-permute-start.6 = (f32[2,4,24,256]{3,2,1,0:T(8,128)S(1)}, f32[2,4,24,256]{3,2,1,0:T(8,128)S(1)}, u32[]{:S(2)}, u32[]{:S(2)}) collective-permute-start(f32[2,4,24,256]{3,2,1,0:T(8,128)S(1)} %get-tuple-element.15), channel_id=1, source_target_pairs={{0,16},{16,32},{32,48},{48,64},{64,80},{80,96},{96,112},{1,17},{17... | collective-permute-start | bytes 589832 | tf_op jit(solution)/shard_map/level1_down/ppermute | solution.py:19
  113.2 6.2 %collective-permute-start.9 = (f32[2,8,5,128]{3,2,1,0:T(8,128)S(1)}, f32[2,8,5,128]{3,2,1,0:T(8,128)S(1)}, u32[]{:S(2)}, u32[]{:S(2)}) collective-permute-start(f32[2,8,5,128]{3,2,1,0:T(8,128)S(1)} %get-tuple-element.80), channel_id=1, source_target_pairs={{1,0},{2,1},{3,2},{4,3},{5,4},{6,5},{7,6},{8,7},{9,8},{10,9},{11,1... | collective-permute-start | bytes 122888 | tf_op jit(solution)/shard_map/level2/ppermute | solution.py:20
  115.1 8.3 %collective-permute-start.8 = (f32[2,8,5,128]{3,2,1,0:T(8,128)S(1)}, f32[2,8,5,128]{3,2,1,0:T(8,128)S(1)}, u32[]{:S(2)}, u32[]{:S(2)}) collective-permute-start(f32[2,8,5,128]{3,2,1,0:T(8,128)S(1)} %get-tuple-element.79), channel_id=1, source_target_pairs={{0,1},{1,2},{2,3},{3,4},{4,5},{5,6},{6,7},{7,8},{8,9},{9,10},{10,1... | collective-permute-start | bytes 122888 | tf_op jit(solution)/shard_map/level2/ppermute | solution.py:19
  123.4 5.2 %collective-permute-start.11 = (f32[2,5,18,128]{3,2,1,0:T(8,128)S(1)}, f32[2,5,18,128]{3,2,1,0:T(8,128)S(1)}, u32[]{:S(2)}, u32[]{:S(2)}) collective-permute-start(f32[2,5,18,128]{3,2,1,0:T(8,128)S(1)} %get-tuple-element.66), channel_id=1, source_target_pairs={{16,0},{32,16},{48,32},{64,48},{80,64},{96,80},{112,96},{17,1},{33... | collective-permute-start | bytes 276488 | tf_op jit(solution)/shard_map/level2/ppermute | solution.py:20
  125.4 6.2 %collective-permute-start.10 = (f32[2,5,18,128]{3,2,1,0:T(8,128)S(1)}, f32[2,5,18,128]{3,2,1,0:T(8,128)S(1)}, u32[]{:S(2)}, u32[]{:S(2)}) collective-permute-start(f32[2,5,18,128]{3,2,1,0:T(8,128)S(1)} %get-tuple-element.65), channel_id=1, source_target_pairs={{0,16},{16,32},{32,48},{48,64},{64,80},{80,96},{96,112},{1,17},{17... | collective-permute-start | bytes 276488 | tf_op jit(solution)/shard_map/level2/ppermute | solution.py:19
  134.8 0.9 copy-start.4
  134.9 1.0 copy-start.5

commit v6 on v5

--- a/solution.py
+++ b/solution.py
@@ -10,16 +10,21 @@
 damping = 2.0 / 3.0
 
 
-def exchange(stack, width):
-    for axis, dim in (("col", 2), ("row", 1)):
-        count = lax.axis_size(axis)
-        forward = [(i, i + 1) for i in range(count - 1)]
-        backward = [(i + 1, i) for i in range(count - 1)]
-        size = stack.shape[dim]
-        low = lax.ppermute(lax.slice_in_dim(stack, size - width, size, axis=dim), axis, forward)
-        high = lax.ppermute(lax.slice_in_dim(stack, 0, width, axis=dim), axis, backward)
-        stack = jnp.concatenate([low, stack, high], axis=dim)
-    return stack
+def _shift_pairs(axis, step):
+    count = lax.axis_size(axis)
+    return [(i, i + step) for i in range(count) if 0 <= i + step < count]
+
+
+def exchange(arrays, width):
+    w = width
+    y_lo = lax.ppermute(jnp.stack([a[:, -w:] for a in arrays]), "col", _shift_pairs("col", 1))
+    y_hi = lax.ppermute(jnp.stack([a[:, :w] for a in arrays]), "col", _shift_pairs("col", -1))
+    first_x = jnp.concatenate([y_lo[:, :w], jnp.stack([a[:w] for a in arrays]), y_hi[:, :w]], axis=2)
+    last_x = jnp.concatenate([y_lo[:, -w:], jnp.stack([a[-w:] for a in arrays]), y_hi[:, -w:]], axis=2)
+    x_lo = lax.ppermute(last_x, "row", _shift_pairs("row", 1))
+    x_hi = lax.ppermute(first_x, "row", _shift_pairs("row", -1))
+    middle = jnp.concatenate([y_lo, jnp.stack(arrays), y_hi], axis=2)
+    return jnp.concatenate([x_lo, middle, x_hi], axis=1)
 
 
 def trim(field, k):
@@ -310,7 +315,7 @@
     lx, ly = nx // 4, ny // 4
 
     with jax.named_scope("level0_down"):
-        fine = exchange(jnp.stack([start_field, source, conductance]), 4)
+        fine = exchange([start_field, source, conductance], 4)
         extent_x, extent_y = nx * lax.axis_size("row"), ny * lax.axis_size("col")
         offsets = jnp.stack([lax.axis_index("row") * nx - 4, lax.axis_index("col") * ny - 4]).astype(jnp.int32)
         depth_x, depth_y, depth_z = fine.shape[1:]
@@ -323,7 +328,7 @@
         mid_cond = restrict_mean(conductance)
 
     with jax.named_scope("level1_down"):
-        mid = exchange(jnp.stack([mid_rhs, mid_cond]), 4)
+        mid = exchange([mid_rhs, mid_cond], 4)
         rhs1, k1 = mid[0], mid[1]
         e1 = first_guess(trim(rhs1, 1), k1, 0.25, grid_mask(mx, my, 3))
         e1 = sweep(e1, trim(rhs1, 2), trim(k1, 1), 0.25, grid_mask(mx, my, 2))
@@ -332,7 +337,7 @@
         low_cond = restrict_mean(mid_cond)
 
     with jax.named_scope("level2"):
-        low = exchange(jnp.stack([low_rhs, low_cond]), 5)
+        low = exchange([low_rhs, low_cond], 5)
         rhs2, k2 = low[0], low[1]
         e2 = first_guess(trim(rhs2, 1), k2, 0.0625, grid_mask(lx, ly, 4))
         for halo in (3, 2, 1):

time: 161 us -> 165 us (1.025)
  the two profiles are of different devices: /device:TPU:98 before, /device:TPU:102 now
where the time goes in v6:
time: 165 us; the launch traced here: 164 us
  Pallas kernels  45 us (27%)
  waiting for transfers between devices  34.6 us (21%)
  starting transfers between devices  31.8 us (19%)
  other arithmetic  25.1 us (15%)
  local copies, waits for them, and re-layouts  20.4 us (12%)
  matrix products  5.95 us (4%)
    pallas_call x2, Pallas kernels, _frame_call(): pl.pallas_call(kernel, grid=(1,), out_shape=outs, in_specs=[pl.BlockSpec(...  45 us
    ppermute x3, waiting for transfers between devices, exchange(): lax.ppermute(jnp.stack([a[:, -w:] for a in arrays]), 'col', _shift_pairs(...  13.8 us
    ppermute x3, waiting for transfers between devices, exchange(): x_lo = lax.ppermute(last_x, 'row', _shift_pairs('row', 1))  10.9 us
    ppermute x3, starting transfers between devices, exchange(): lax.ppermute(jnp.stack([a[:, -w:] for a in arrays]), 'col', _shift_pairs(...  9.75 us
    ppermute x3, waiting for transfers between devices, exchange(): x_hi = lax.ppermute(first_x, 'row', _shift_pairs('row', -1))  8.7 us
    ppermute x3, starting transfers between devices, exchange(): lax.ppermute(jnp.stack([a[:, :w] for a in arrays]), 'col', _shift_pairs('...  8.59 us
    concatenate x3, other arithmetic, exchange(): return jnp.concatenate([x_lo, middle, x_hi], axis=1)  8 us
    ppermute x3, starting transfers between devices, exchange(): x_lo = lax.ppermute(last_x, 'row', _shift_pairs('row', 1))  7.47 us
  transfers between devices with their start and end apart: 12, of which 10 were waited for; matrix products, arithmetic and copies ran while one was open for 11% of the time, Pallas kernels for 0%

profile of v6, /device:TPU:102, one launch (start us, length us, event | category | flops | bytes accessed | tf_op | source)
XLA Modules:
  0.0 163.9 jit_solution(12157109641300627403)
XLA Ops:
  0.0 1.3 slice_bitcast_fusion.13
  1.3 1.8 %slice_bitcast_fusion.11 = (f32[1,32,4,512]{3,2,1,0:T(4,128)S(1)}, f32[1,32,4,512]{3,2,1,0:T(4,128)S(1)}, f32[1,32,4,512]{3,2,1,0:T(4,128)S(1)}, f32[1,32,4,512]{3,2,1,0:T(4,128)S(1)}) fusion(f32[32,32,512]{2,1,0:T(8,128)} %param.5, f32[32,32,512]{2,1,0:T(8,128)} %param.4), kind=kLoop, calls=%fused_computation.154 | loop fusion | bytes 2097152 | tf_op jit(solution)/shard_map/level0_down/stack | solution.py:20
  3.1 1.1 pad_maximum_fusion.5
  4.2 4.7 %collective-permute-start.1 = (f32[3,32,4,512]{3,2,1,0:T(4,128)}, f32[3,32,4,512]{3,2,1,0:T(4,128)S(1)}, u32[]{:S(2)}, u32[]{:S(2)}) collective-permute-start(f32[3,32,4,512]{3,2,1,0:T(4,128)} %pad_maximum_fusion.5), channel_id=1, source_target_pairs={{1,0},{2,1},{3,2},{4,3},{5,4},{6,5},{7,6},{8,7},{9,8},{10,9},{11,1... | collective-permute-start | bytes 2359304 | tf_op jit(solution)/shard_map/level0_down/ppermute | solution.py:21
  8.9 1.1 pad_maximum_fusion.4
  10.0 1.9 %collective-permute-start = (f32[3,32,4,512]{3,2,1,0:T(4,128)}, f32[3,32,4,512]{3,2,1,0:T(4,128)}, u32[]{:S(2)}, u32[]{:S(2)}) collective-permute-start(f32[3,32,4,512]{3,2,1,0:T(4,128)} %pad_maximum_fusion.4), channel_id=1, source_target_pairs={{0,1},{1,2},{2,3},{3,4},{4,5},{5,6},{6,7},{7,8},{8,9},{9,10},{10,1... | collective-permute-start | bytes 2359304 | tf_op jit(solution)/shard_map/level0_down/ppermute | solution.py:20
  11.9 2.2 %reshape.400 = f32[16,2,16,2,512]{4,3,2,1,0:T(2,128)} reshape(f32[32,32,512]{2,1,0:T(8,128)S(1)} %copy-done) | data formatting | bytes 4194304 | tf_op jit(solution)/shard_map/level0_down/reshape | solution.py:88
  14.3 4.0 %reduce_sum.37 = f32[16,16,512]{2,1,0:T(8,128)} reduce(f32[16,2,16,2,512]{4,3,2,1,0:T(2,128)} %reshape.400, f32[]{:T(128)} %constant.162.clone.1), dimensions={1,3}, to_apply=%region_1.2 | reduce | flops 393216 | bytes 2621444 | tf_op jit(solution)/shard_map/level0_down/reduce_sum | solution.py:88
  18.3 1.8 %fusion.12 = f32[16,16,256]{2,1,0:T(8,128)S(1)} fusion(f32[16,16,512]{2,1,0:T(8,128)} %reduce_sum.37, s32[512]{0:T(512)S(1)} %get-tuple-element.113, s32[512]{0:T(512)S(1)} %get-tuple-element.114, pred[512]{0:T(512)(128)(4,1)S(1)} %fusion.206), kind=kOutput, calls=%fused_computation.27 | convolution fusion | flops 403046400 | bytes 791040 | tf_op jit(solution)/shard_map/level0_down/dot_general | solution.py:92
  20.6 0.7 broadcast_and_fusion.3
  21.3 0.7 broadcast_and_fusion.4
  22.0 0.7 broadcast_and_fusion.5
  22.6 0.7 broadcast_and_fusion.2
  23.3 0.4 fusion.112
  23.7 0.5 iota_compare_fusion.10
  24.2 0.6 iota_compare_fusion.12
  24.8 0.6 compare_and_fusion.7
  25.4 1.1 slice_bitcast_fusion.10
  26.5 1.1 slice_bitcast_fusion.8
  27.6 5.7 %collective-permute-done = f32[3,32,4,512]{3,2,1,0:T(4,128)} collective-permute-done((f32[3,32,4,512]{3,2,1,0:T(4,128)}, f32[3,32,4,512]{3,2,1,0:T(4,128)}, u32[]{:S(2)}, u32[]{:S(2)}) %collective-permute-start) | collective-permute-done | bytes 786464 | tf_op jit(solution)/shard_map/level0_down/ppermute | solution.py:20
  33.3 1.0 fusion.225
  34.5 2.2 %collective-permute-start.3 = (f32[3,4,40,512]{3,2,1,0:T(8,128)S(1)}, f32[3,4,40,512]{3,2,1,0:T(8,128)S(1)}, u32[]{:S(2)}, u32[]{:S(2)}) collective-permute-start(f32[3,4,40,512]{3,2,1,0:T(8,128)S(1)} %pad_maximum_fusion.3), channel_id=1, source_target_pairs={{16,0},{32,16},{48,32},{64,48},{80,64},{96,80},{112,96},{17,1},{33... | collective-permute-start | bytes 2949128 | tf_op jit(solution)/shard_map/level0_down/ppermute | solution.py:25
  36.8 2.5 %collective-permute-start.2 = (f32[3,4,40,512]{3,2,1,0:T(8,128)S(1)}, f32[3,4,40,512]{3,2,1,0:T(8,128)S(1)}, u32[]{:S(2)}, u32[]{:S(2)}) collective-permute-start(f32[3,4,40,512]{3,2,1,0:T(8,128)S(1)} %pad_maximum_fusion.2), channel_id=1, source_target_pairs={{0,16},{16,32},{32,48},{48,64},{64,80},{80,96},{96,112},{1,17},{17... | collective-permute-start | bytes 2949128 | tf_op jit(solution)/shard_map/level0_down/ppermute | solution.py:24
  39.3 0.6 pad_add_fusion.off_ref
  40.0 8.3 %collective-permute-done.3 = f32[3,4,40,512]{3,2,1,0:T(8,128)S(1)} collective-permute-done((f32[3,4,40,512]{3,2,1,0:T(8,128)S(1)}, f32[3,4,40,512]{3,2,1,0:T(8,128)S(1)}, u32[]{:S(2)}, u32[]{:S(2)}) %collective-permute-start.3) | collective-permute-done | bytes 983072 | tf_op jit(solution)/shard_map/level0_down/ppermute | solution.py:25
  48.2 4.0 %collective-permute-done.2 = f32[3,4,40,512]{3,2,1,0:T(8,128)S(1)} collective-permute-done((f32[3,4,40,512]{3,2,1,0:T(8,128)S(1)}, f32[3,4,40,512]{3,2,1,0:T(8,128)S(1)}, u32[]{:S(2)}, u32[]{:S(2)}) %collective-permute-start.2) | collective-permute-done | bytes 983072 | tf_op jit(solution)/shard_map/level0_down/ppermute | solution.py:24
  52.2 7.8 %pad_maximum_fusion.s_ref = f32[3,40,40,512]{3,2,1,0:T(8,128)} fusion(f32[3,4,40,512]{3,2,1,0:T(8,128)S(1)} %collective-permute-done.3, f32[3,32,4,512]{3,2,1,0:T(4,128)S(1)} %collective-permute-done.1, f32[1,32,32,512]{3,2,1,0:T(8,128)S(1)} %bitcast.94, f32[1,32,32,512]{3,2,1,0:T(8,128)S(1)} %bitcast.96, f32[1,32,32,512]{3,2,1,0:T(8,128)S(1)} %bitcast.95, ...), kind=kLoop, calls=%fused_computation | loop fusion | flops 14745600 | bytes 19660800 | tf_op jit(solution)/shard_map/level0_down/concatenate | solution.py:27
  60.1 25.0 %level0_down.1 = (f32[40,40,512]{2,1,0:T(8,128)}, f32[32,32,512]{2,1,0:T(8,128)}) custom-call(s32[2]{0:T(128)} %pad_add_fusion.off_ref, f32[3,40,40,512]{3,2,1,0:T(8,128)} %pad_maximum_fusion.s_ref), custom_call_target="tpu_custom_call" | custom-call | flops 98304000 | bytes 16384000 | tf_op jit(solution)/shard_map/level0_down/pallas_call | solution.py:299
  85.0 2.5 %reshape.399 = f32[16,2,16,2,512]{4,3,2,1,0:T(2,128)S(1)} reshape(f32[32,32,512]{2,1,0:T(8,128)} %get-tuple-element.8) | data formatting | bytes 4194304 | tf_op jit(solution)/shard_map/level0_down/reshape | solution.py:88
  87.6 1.5 reduce_sum.36
  89.2 0.8 fusion.14
  90.0 1.9 %collective-permute-start.5 = (f32[2,16,4,256]{3,2,1,0:T(4,128)S(1)}, f32[2,16,4,256]{3,2,1,0:T(4,128)S(1)}, u32[]{:S(2)}, u32[]{:S(2)}) collective-permute-start(f32[2,16,4,256]{3,2,1,0:T(4,128)S(1)} %pad_maximum_fusion.10), channel_id=1, source_target_pairs={{1,0},{2,1},{3,2},{4,3},{5,4},{6,5},{7,6},{8,7},{9,8},{10,9},{11,1... | collective-permute-start | bytes 393224 | tf_op jit(solution)/shard_map/level1_down/ppermute | solution.py:21
  92.0 3.9 %collective-permute-start.4 = (f32[2,16,4,256]{3,2,1,0:T(4,128)S(1)}, f32[2,16,4,256]{3,2,1,0:T(4,128)S(1)}, u32[]{:S(2)}, u32[]{:S(2)}) collective-permute-start(f32[2,16,4,256]{3,2,1,0:T(4,128)S(1)} %pad_maximum_fusion.9), channel_id=1, source_target_pairs={{0,1},{1,2},{2,3},{3,4},{4,5},{5,6},{6,7},{7,8},{8,9},{9,10},{10,1... | collective-permute-start | bytes 393224 | tf_op jit(solution)/shard_map/level1_down/ppermute | solution.py:20
  95.9 0.9 collective-permute-done.5
  96.9 4.1 %collective-permute-done.4 = f32[2,16,4,256]{3,2,1,0:T(4,128)S(1)} collective-permute-done((f32[2,16,4,256]{3,2,1,0:T(4,128)S(1)}, f32[2,16,4,256]{3,2,1,0:T(4,128)S(1)}, u32[]{:S(2)}, u32[]{:S(2)}) %collective-permute-start.4) | collective-permute-done | bytes 131104 | tf_op jit(solution)/shard_map/level1_down/ppermute | solution.py:20
  101.0 1.9 %collective-permute-start.7 = (f32[2,4,24,256]{3,2,1,0:T(8,128)S(1)}, f32[2,4,24,256]{3,2,1,0:T(8,128)S(1)}, u32[]{:S(2)}, u32[]{:S(2)}) collective-permute-start(f32[2,4,24,256]{3,2,1,0:T(8,128)S(1)} %pad_maximum_fusion.8), channel_id=1, source_target_pairs={{16,0},{32,16},{48,32},{64,48},{80,64},{96,80},{112,96},{17,1},{33... | collective-permute-start | bytes 589832 | tf_op jit(solution)/shard_map/level1_down/ppermute | solution.py:25
  103.0 2.6 %collective-permute-start.6 = (f32[2,4,24,256]{3,2,1,0:T(8,128)S(1)}, f32[2,4,24,256]{3,2,1,0:T(8,128)S(1)}, u32[]{:S(2)}, u32[]{:S(2)}) collective-permute-start(f32[2,4,24,256]{3,2,1,0:T(8,128)S(1)} %pad_maximum_fusion.7), channel_id=1, source_target_pairs={{0,16},{16,32},{32,48},{48,64},{64,80},{80,96},{96,112},{1,17},{17... | collective-permute-start | bytes 589832 | tf_op jit(solution)/shard_map/level1_down/ppermute | solution.py:24
  105.7 0.4 collective-permute-done.7
  106.1 3.9 %collective-permute-done.6 = f32[2,4,24,256]{3,2,1,0:T(8,128)S(1)} collective-permute-done((f32[2,4,24,256]{3,2,1,0:T(8,128)S(1)}, f32[2,4,24,256]{3,2,1,0:T(8,128)S(1)}, u32[]{:S(2)}, u32[]{:S(2)}) %collective-permute-start.6) | collective-permute-done | bytes 196640 | tf_op jit(solution)/shard_map/level1_down/ppermute | solution.py:24
  110.2 0.2 fusion.233
  110.6 0.2 copy-done.8
  110.8 0.6 fusion.5
  112.1 1.2 fusion.39
  113.9 0.6 fusion.66
  114.8 0.4 fusion.114
  115.2 1.0 fusion.228
  116.1 1.9 %collective-permute-start.9 = (f32[2,8,5,128]{3,2,1,0:T(8,128)S(1)}, f32[2,8,5,128]{3,2,1,0:T(8,128)S(1)}, u32[]{:S(2)}, u32[]{:S(2)}) collective-permute-start(f32[2,8,5,128]{3,2,1,0:T(8,128)S(1)} %pad_maximum_fusion.14), channel_id=1, source_target_pairs={{1,0},{2,1},{3,2},{4,3},{5,4},{6,5},{7,6},{8,7},{9,8},{10,9},{11,1... | collective-permute-start | bytes 122888 | tf_op jit(solution)/shard_map/level2/ppermute | solution.py:21
  118.1 3.9 %collective-permute-start.8 = (f32[2,8,5,128]{3,2,1,0:T(8,128)S(1)}, f32[2,8,5,128]{3,2,1,0:T(8,128)S(1)}, u32[]{:S(2)}, u32[]{:S(2)}) collective-permute-start(f32[2,8,5,128]{3,2,1,0:T(8,128)S(1)} %pad_maximum_fusion.13), channel_id=1, source_target_pairs={{0,1},{1,2},{2,3},{3,4},{4,5},{5,6},{6,7},{7,8},{8,9},{9,10},{10,1... | collective-permute-start | bytes 122888 | tf_op jit(solution)/shard_map/level2/ppermute | solution.py:20
  122.0 0.3 collective-permute-done.9
  122.3 4.0 %collective-permute-done.8 = f32[2,8,5,128]{3,2,1,0:T(8,128)S(1)} collective-permute-done((f32[2,8,5,128]{3,2,1,0:T(8,128)S(1)}, f32[2,8,5,128]{3,2,1,0:T(8,128)S(1)}, u32[]{:S(2)}, u32[]{:S(2)}) %collective-permute-start.8) | collective-permute-done | bytes 40992 | tf_op jit(solution)/shard_map/level2/ppermute | solution.py:20
  126.4 1.9 %collective-permute-start.11 = (f32[2,5,18,128]{3,2,1,0:T(8,128)S(1)}, f32[2,5,18,128]{3,2,1,0:T(8,128)S(1)}, u32[]{:S(2)}, u32[]{:S(2)}) collective-permute-start(f32[2,5,18,128]{3,2,1,0:T(8,128)S(1)} %pad_maximum_fusion.12), channel_id=1, source_target_pairs={{16,0},{32,16},{48,32},{64,48},{80,64},{96,80},{112,96},{17,1},{33... | collective-permute-start | bytes 276488 | tf_op jit(solution)/shard_map/level2/ppermute | solution.py:25
  128.4 2.4 %collective-permute-start.10 = (f32[2,5,18,128]{3,2,1,0:T(8,128)S(1)}, f32[2,5,18,128]{3,2,1,0:T(8,128)S(1)}, u32[]{:S(2)}, u32[]{:S(2)}) collective-permute-start(f32[2,5,18,128]{3,2,1,0:T(8,128)S(1)} %pad_maximum_fusion.11), channel_id=1, source_target_pairs={{0,16},{16,32},{32,48},{48,64},{64,80},{80,96},{96,112},{1,17},{17... | collective-permute-start | bytes 276488 | tf_op jit(solution)/shard_map/level2/ppermute | solution.py:24
  130.8 0.7 fusion.227
  131.5 3.0 %collective-permute-done.10 = f32[2,5,18,128]{3,2,1,0:T(8,128)S(1)} collective-permute-done((f32[2,5,18,128]{3,2,1,0:T(8,128)S(1)}, f32[2,5,18,128]{3,2,1,0:T(8,128)S(1)}, u32[]{:S(2)}, u32[]{:S(2)}) %collective-permute-start.10) | collective-permute-done | bytes 92192 | tf_op jit(solution)/shard_map/level2/ppermute | solution.py:24
  135.5 0.3 fusion.139
  136.3 0.3 fusion.160
  136.9 0.5 fusion.110
  137.6 0.3 reshape.404
  138.4 0.6 copy-done.3
  139.0 2.1 %fusion.10 = f32[18,18,512]{2,1,0:T(8,128)S(1)} fusion(f32[20,20,256]{2,1,0:T(8,128)S(1)} %add.696, f32[24,24,256]{2,1,0:T(8,128)S(1)} %get-tuple-element.21, f32[18,18,255]{2,1,0:T(8,128)S(1)} %get-tuple-element.48, f32[18,18,1]{2,1,0:T(8,128)S(1)} %get-tuple-element.50, f32[18,18,1]{2,1,0:T(8,128)S(1)} %get-tuple-element.49, ...), kind=kOutput, calls=%fused_computation.25 | convolution fusion | flops 513567744 | bytes 8192512 | tf_op jit(solution)/shard_map/level0_up/dot_general | solution.py:355
  141.1 0.5 broadcast_in_dim.192
  141.6 0.9 reshape.405
  142.5 1.3 pad.4.e_ref
  143.8 20.1 %level0_up.1 = f32[32,32,512]{2,1,0:T(8,128)} custom-call(s32[2]{0:T(128)} %pad_add_fusion.off_ref, f32[40,40,512]{2,1,0:T(8,128)} %get-tuple-element.7.u2_ref, f32[18,40,512]{2,1,0:T(8,128)} %pad.4.e_ref, f32[3,40,40,512]{3,2,1,0:T(8,128)} %pad_maximum_fusion.s_ref), custom_call_target="tpu_custom_call" | custom-call | flops 65536000 | bytes 16384000 | tf_op jit(solution)/shard_map/level0_up/pallas_call | solution.py:299
  (133 shorter events, 5.4 us)
Async XLA Ops:
  3.1 8.8 %copy-start = (f32[32,32,512]{2,1,0:T(8,128)S(1)}, f32[32,32,512]{2,1,0:T(8,128)}, u32[]{:S(2)}) copy-start(f32[32,32,512]{2,1,0:T(8,128)} %param.5) | copy-start | bytes 6291460
  4.2 23.4 %collective-permute-start.1 = (f32[3,32,4,512]{3,2,1,0:T(4,128)}, f32[3,32,4,512]{3,2,1,0:T(4,128)S(1)}, u32[]{:S(2)}, u32[]{:S(2)}) collective-permute-start(f32[3,32,4,512]{3,2,1,0:T(4,128)} %pad_maximum_fusion.5), channel_id=1, source_target_pairs={{1,0},{2,1},{3,2},{4,3},{5,4},{6,5},{7,6},{8,7},{9,8},{10,9},{11,1... | collective-permute-start | bytes 2359304 | tf_op jit(solution)/shard_map/level0_down/ppermute | solution.py:21
  10.0 23.3 %collective-permute-start = (f32[3,32,4,512]{3,2,1,0:T(4,128)}, f32[3,32,4,512]{3,2,1,0:T(4,128)}, u32[]{:S(2)}, u32[]{:S(2)}) collective-permute-start(f32[3,32,4,512]{3,2,1,0:T(4,128)} %pad_maximum_fusion.4), channel_id=1, source_target_pairs={{0,1},{1,2},{2,3},{3,4},{4,5},{5,6},{6,7},{7,8},{8,9},{9,10},{10,1... | collective-permute-start | bytes 2359304 | tf_op jit(solution)/shard_map/level0_down/ppermute | solution.py:20
  14.2 4.1 %copy-start.13 = (s32[512]{0:T(512)}, s32[512]{0:T(512)S(1)}, u32[]{:S(2)}) copy-start(s32[512]{0:T(512)S(1)} %get-tuple-element.113) | copy-start | bytes 6148
  14.2 4.1 %copy-start.16 = (s32[512]{0:T(512)}, s32[512]{0:T(512)S(1)}, u32[]{:S(2)}) copy-start(s32[512]{0:T(512)S(1)} %get-tuple-element.114) | copy-start | bytes 6148
  14.2 4.1 %copy-start.25 = (pred[512]{0:T(512)(128)(4,1)}, pred[512]{0:T(512)(128)(4,1)S(1)}, u32[]{:S(2)}) copy-start(pred[512]{0:T(512)(128)(4,1)S(1)} %fusion.206) | copy-start | bytes 1540
  14.2 9.1 %copy-start.21 = (s32[256]{0:T(256)}, s32[256]{0:T(256)S(1)}, u32[]{:S(2)}) copy-start(s32[256]{0:T(256)S(1)} %get-tuple-element.121) | copy-start | bytes 3076
  14.2 9.1 %copy-start.23 = (s32[256]{0:T(256)}, s32[256]{0:T(256)S(1)}, u32[]{:S(2)}) copy-start(s32[256]{0:T(256)S(1)} %get-tuple-element.122) | copy-start | bytes 3076
  14.3 9.1 %copy-start.28 = (pred[256]{0:T(512)(128)(4,1)}, pred[256]{0:T(512)(128)(4,1)S(1)}, u32[]{:S(2)}) copy-start(pred[256]{0:T(512)(128)(4,1)S(1)} %compare_and_fusion) | copy-start | bytes 772
  34.3 18.0 %copy-start.1 = (f32[32,32,512]{2,1,0:T(8,128)S(1)}, f32[32,32,512]{2,1,0:T(8,128)}, u32[]{:S(2)}) copy-start(f32[32,32,512]{2,1,0:T(8,128)} %param.3) | copy-start | bytes 6291460
  34.3 18.0 %copy-start.2 = (f32[32,32,512]{2,1,0:T(8,128)S(1)}, f32[32,32,512]{2,1,0:T(8,128)}, u32[]{:S(2)}) copy-start(f32[32,32,512]{2,1,0:T(8,128)} %param.4) | copy-start | bytes 6291460
  34.5 13.8 %collective-permute-start.3 = (f32[3,4,40,512]{3,2,1,0:T(8,128)S(1)}, f32[3,4,40,512]{3,2,1,0:T(8,128)S(1)}, u32[]{:S(2)}, u32[]{:S(2)}) collective-permute-start(f32[3,4,40,512]{3,2,1,0:T(8,128)S(1)} %pad_maximum_fusion.3), channel_id=1, source_target_pairs={{16,0},{32,16},{48,32},{64,48},{80,64},{96,80},{112,96},{17,1},{33... | collective-permute-start | bytes 2949128 | tf_op jit(solution)/shard_map/level0_down/ppermute | solution.py:25
  36.8 15.4 %collective-permute-start.2 = (f32[3,4,40,512]{3,2,1,0:T(8,128)S(1)}, f32[3,4,40,512]{3,2,1,0:T(8,128)S(1)}, u32[]{:S(2)}, u32[]{:S(2)}) collective-permute-start(f32[3,4,40,512]{3,2,1,0:T(8,128)S(1)} %pad_maximum_fusion.2), channel_id=1, source_target_pairs={{0,16},{16,32},{32,48},{48,64},{64,80},{80,96},{96,112},{1,17},{17... | collective-permute-start | bytes 2949128 | tf_op jit(solution)/shard_map/level0_down/ppermute | solution.py:24
  87.5 1.6 copy-start.14
  87.5 1.6 copy-start.17
  87.5 1.6 copy-start.26
  89.1 16.4 %copy-start.19 = (pred[10]{0:T(512)(128)(4,1)S(1)}, pred[10]{0:T(512)(128)(4,1)}, u32[]{:S(2)}) copy-start(pred[10]{0:T(512)(128)(4,1)} %get-tuple-element.131) | copy-start | bytes 34
  89.2 16.4 %copy-start.20 = (pred[10]{0:T(512)(128)(4,1)S(1)}, pred[10]{0:T(512)(128)(4,1)}, u32[]{:S(2)}) copy-start(pred[10]{0:T(512)(128)(4,1)} %get-tuple-element.132) | copy-start | bytes 34
  90.0 6.9 %collective-permute-start.5 = (f32[2,16,4,256]{3,2,1,0:T(4,128)S(1)}, f32[2,16,4,256]{3,2,1,0:T(4,128)S(1)}, u32[]{:S(2)}, u32[]{:S(2)}) collective-permute-start(f32[2,16,4,256]{3,2,1,0:T(4,128)S(1)} %pad_maximum_fusion.10), channel_id=1, source_target_pairs={{1,0},{2,1},{3,2},{4,3},{5,4},{6,5},{7,6},{8,7},{9,8},{10,9},{11,1... | collective-permute-start | bytes 393224 | tf_op jit(solution)/shard_map/level1_down/ppermute | solution.py:21
  92.0 9.0 %collective-permute-start.4 = (f32[2,16,4,256]{3,2,1,0:T(4,128)S(1)}, f32[2,16,4,256]{3,2,1,0:T(4,128)S(1)}, u32[]{:S(2)}, u32[]{:S(2)}) collective-permute-start(f32[2,16,4,256]{3,2,1,0:T(4,128)S(1)} %pad_maximum_fusion.9), channel_id=1, source_target_pairs={{0,1},{1,2},{2,3},{3,4},{4,5},{5,6},{6,7},{7,8},{8,9},{9,10},{10,1... | collective-permute-start | bytes 393224 | tf_op jit(solution)/shard_map/level1_down/ppermute | solution.py:20
  101.0 5.1 %collective-permute-start.7 = (f32[2,4,24,256]{3,2,1,0:T(8,128)S(1)}, f32[2,4,24,256]{3,2,1,0:T(8,128)S(1)}, u32[]{:S(2)}, u32[]{:S(2)}) collective-permute-start(f32[2,4,24,256]{3,2,1,0:T(8,128)S(1)} %pad_maximum_fusion.8), channel_id=1, source_target_pairs={{16,0},{32,16},{48,32},{64,48},{80,64},{96,80},{112,96},{17,1},{33... | collective-permute-start | bytes 589832 | tf_op jit(solution)/shard_map/level1_down/ppermute | solution.py:25
  103.0 7.0 %collective-permute-start.6 = (f32[2,4,24,256]{3,2,1,0:T(8,128)S(1)}, f32[2,4,24,256]{3,2,1,0:T(8,128)S(1)}, u32[]{:S(2)}, u32[]{:S(2)}) collective-permute-start(f32[2,4,24,256]{3,2,1,0:T(8,128)S(1)} %pad_maximum_fusion.7), channel_id=1, source_target_pairs={{0,16},{16,32},{32,48},{48,64},{64,80},{80,96},{96,112},{1,17},{17... | collective-permute-start | bytes 589832 | tf_op jit(solution)/shard_map/level1_down/ppermute | solution.py:24
  110.2 0.6 copy-start.8
  110.2 0.6 copy-start.9
  113.8 0.9 copy-start.22
  113.8 0.9 copy-start.24
  113.8 0.9 copy-start.29
  116.1 6.2 %collective-permute-start.9 = (f32[2,8,5,128]{3,2,1,0:T(8,128)S(1)}, f32[2,8,5,128]{3,2,1,0:T(8,128)S(1)}, u32[]{:S(2)}, u32[]{:S(2)}) collective-permute-start(f32[2,8,5,128]{3,2,1,0:T(8,128)S(1)} %pad_maximum_fusion.14), channel_id=1, source_target_pairs={{1,0},{2,1},{3,2},{4,3},{5,4},{6,5},{7,6},{8,7},{9,8},{10,9},{11,1... | collective-permute-start | bytes 122888 | tf_op jit(solution)/shard_map/level2/ppermute | solution.py:21
  118.1 8.3 %collective-permute-start.8 = (f32[2,8,5,128]{3,2,1,0:T(8,128)S(1)}, f32[2,8,5,128]{3,2,1,0:T(8,128)S(1)}, u32[]{:S(2)}, u32[]{:S(2)}) collective-permute-start(f32[2,8,5,128]{3,2,1,0:T(8,128)S(1)} %pad_maximum_fusion.13), channel_id=1, source_target_pairs={{0,1},{1,2},{2,3},{3,4},{4,5},{5,6},{6,7},{7,8},{8,9},{9,10},{10,1... | collective-permute-start | bytes 122888 | tf_op jit(solution)/shard_map/level2/ppermute | solution.py:20
  126.4 8.5 %copy-start.6 = (pred[16,16]{1,0:T(8,128)(4,1)S(1)}, pred[16,16]{1,0:T(8,128)(4,1)}, u32[]{:S(2)}) copy-start(pred[16,16]{1,0:T(8,128)(4,1)} %broadcast_and_fusion.3) | copy-start | bytes 772
  126.4 8.5 %copy-start.10 = (pred[128]{0:T(512)(128)(4,1)S(1)}, pred[128]{0:T(512)(128)(4,1)}, u32[]{:S(2)}) copy-start(pred[128]{0:T(512)(128)(4,1)} %get-tuple-element.125) | copy-start | bytes 388
  126.4 8.5 %copy-start.11 = (pred[128]{0:T(512)(128)(4,1)S(1)}, pred[128]{0:T(512)(128)(4,1)}, u32[]{:S(2)}) copy-start(pred[128]{0:T(512)(128)(4,1)} %get-tuple-element.126) | copy-start | bytes 388
  126.4 5.1 %collective-permute-start.11 = (f32[2,5,18,128]{3,2,1,0:T(8,128)S(1)}, f32[2,5,18,128]{3,2,1,0:T(8,128)S(1)}, u32[]{:S(2)}, u32[]{:S(2)}) collective-permute-start(f32[2,5,18,128]{3,2,1,0:T(8,128)S(1)} %pad_maximum_fusion.12), channel_id=1, source_target_pairs={{16,0},{32,16},{48,32},{64,48},{80,64},{96,80},{112,96},{17,1},{33... | collective-permute-start | bytes 276488 | tf_op jit(solution)/shard_map/level2/ppermute | solution.py:25
  128.4 6.2 %collective-permute-start.10 = (f32[2,5,18,128]{3,2,1,0:T(8,128)S(1)}, f32[2,5,18,128]{3,2,1,0:T(8,128)S(1)}, u32[]{:S(2)}, u32[]{:S(2)}) collective-permute-start(f32[2,5,18,128]{3,2,1,0:T(8,128)S(1)} %pad_maximum_fusion.11), channel_id=1, source_target_pairs={{0,16},{16,32},{32,48},{48,64},{64,80},{80,96},{96,112},{1,17},{17... | collective-permute-start | bytes 276488 | tf_op jit(solution)/shard_map/level2/ppermute | solution.py:24
  134.7 0.9 copy-start.5
  135.4 0.8 copy-start.7
  137.9 1.0 copy-start.3
  137.9 1.1 copy-start.4
  137.9 1.1 copy-start.12
  138.0 1.0 copy-start.15
  138.0 1.0 copy-start.18
  138.0 1.0 copy-start.27

commit v7 on v5

--- a/solution.py
+++ b/solution.py
@@ -81,6 +81,17 @@
 def restrict_mean(field):
     depth = field.shape[2]
     planar = field.reshape(field.shape[0] // 2, 2, field.shape[1] // 2, 2, depth).sum(axis=(1, 3))
+    fine_idx = lax.broadcasted_iota(jnp.int32, (depth, depth // 2), 0)
+    coarse_idx = lax.broadcasted_iota(jnp.int32, (depth, depth // 2), 1)
+    table = jnp.where(fine_idx // 2 == coarse_idx, 0.125, 0.0).astype(jnp.float32)
+    return jnp.dot(
+        planar, table, precision=lax.Precision.HIGHEST, preferred_element_type=jnp.float32
+    )
+
+
+def restrict_pairs(field):
+    depth = field.shape[2]
+    planar = field.reshape(field.shape[0], field.shape[1] // 2, 2, depth).sum(axis=2)
     fine_idx = lax.broadcasted_iota(jnp.int32, (depth, depth // 2), 0)
     coarse_idx = lax.broadcasted_iota(jnp.int32, (depth, depth // 2), 1)
     table = jnp.where(fine_idx // 2 == coarse_idx, 0.125, 0.0).astype(jnp.float32)
@@ -263,7 +274,7 @@
     lax.fori_loop(planes[0], planes[1], plane_body, 0)
 
 
-def _down_kernel(off_ref, s_ref, u2_ref, r_ref, u1_ref, *, extent_x, extent_y):
+def _down_kernel(off_ref, s_ref, u2_ref, pairs_ref, u1_ref, r_ref, *, extent_x, extent_y):
     depth_x = s_ref.shape[1]
     common = dict(scale=1.0, extent_x=extent_x, extent_y=extent_y)
     _sweep_planes(off_ref, s_ref.at[0], s_ref.at[1], s_ref.at[2], u1_ref, residual=False,
@@ -272,6 +283,12 @@
                   planes=(2, depth_x - 2), inner=False, **common)
     _sweep_planes(off_ref, u2_ref, s_ref.at[1], s_ref.at[2], r_ref, residual=True,
                   planes=(4, depth_x - 4), inner=True, **common)
+
+    def add_pair(q, carry):
+        pairs_ref[q] = r_ref[2 * q] + r_ref[2 * q + 1]
+        return carry
+
+    lax.fori_loop(0, pairs_ref.shape[0], add_pair, 0)
 
 
 def _up_kernel(off_ref, u2_ref, e_ref, s_ref, u5_ref, u3_ref, u4_ref, *, extent_x, extent_y):
@@ -316,10 +333,12 @@
         depth_x, depth_y, depth_z = fine.shape[1:]
         frame = jax.ShapeDtypeStruct((depth_x, depth_y, depth_z), jnp.float32)
         inner = jax.ShapeDtypeStruct((depth_x - 8, depth_y - 8, depth_z), jnp.float32)
+        paired = jax.ShapeDtypeStruct(((depth_x - 8) // 2, depth_y - 8, depth_z), jnp.float32)
         kernel = functools.partial(_down_kernel, extent_x=extent_x, extent_y=extent_y)
-        u2, residual = _frame_call(kernel, offsets, [fine], [frame, inner],
-                                   [pltpu.VMEM(frame.shape, jnp.float32)], fine[0].size, 3)
-        mid_rhs = restrict_mean(residual)
+        u2, x_pairs = _frame_call(kernel, offsets, [fine], [frame, paired],
+                                  [pltpu.VMEM(frame.shape, jnp.float32), pltpu.VMEM(inner.shape, jnp.float32)],
+                                  fine[0].size, 3)
+        mid_rhs = restrict_pairs(x_pairs)
         mid_cond = restrict_mean(conductance)
 
     with jax.named_scope("level1_down"):

time: 161 us -> 160 us (level)
  the two profiles are of different devices: /device:TPU:98 before, /device:TPU:100 now
where the time goes in v7:
time: 160 us
  Pallas kernels  45 us (28%)
  waiting for transfers between devices  41.9 us (26%)
  starting transfers between devices  31.5 us (20%)
  other arithmetic  23.5 us (15%)
  local copies, waits for them, and re-layouts  12.4 us (8%)
  matrix products  4.9 us (3%)
    pallas_call x2, Pallas kernels, _frame_call(): pl.pallas_call(kernel, grid=(1,), out_shape=outs, in_specs=[pl.BlockSpec(...  45 us
    ppermute x6, waiting for transfers between devices, exchange(): lax.ppermute(lax.slice_in_dim(stack, size - width, size, axis=dim), axis,...  24.9 us
    ppermute x6, starting transfers between devices, exchange(): lax.ppermute(lax.slice_in_dim(stack, size - width, size, axis=dim), axis,...  17.2 us
    ppermute x6, waiting for transfers between devices, exchange(): lax.ppermute(lax.slice_in_dim(stack, 0, width, axis=dim), axis, backward)  17 us
    ppermute x6, starting transfers between devices, exchange(): lax.ppermute(lax.slice_in_dim(stack, 0, width, axis=dim), axis, backward)  14.4 us
    concatenate x4, other arithmetic, exchange(): stack = jnp.concatenate([low, stack, high], axis=dim)  8.08 us
    slice x4, other arithmetic, exchange(): lax.slice_in_dim(stack, size - width, size, axis=dim)  5.38 us
    reduce_sum x3, other arithmetic, restrict_mean(): field.reshape(field.shape[0] // 2, 2, field.shape[1] // 2, 2, depth)  4.34 us
  transfers between devices with their start and end apart: 12, of which 11 were waited for; matrix products, arithmetic and copies ran while one was open for 6% of the time, Pallas kernels for 0%

profile of v7, /device:TPU:100, one launch (start us, length us, event | category | flops | bytes accessed | tf_op | source)
XLA Modules:
  0.0 159.8 jit_solution(17623571359965106086)
XLA Ops:
  0.0 3.6 %pad_maximum_fusion.9 = (f32[3,32,4,512]{3,2,1,0:T(4,128)}, f32[3,32,4,512]{3,2,1,0:T(4,128)}) fusion(f32[1,32,32,512]{3,2,1,0:T(8,128)} %bitcast.40, f32[1,32,32,512]{3,2,1,0:T(8,128)} %bitcast.43, f32[1,32,32,512]{3,2,1,0:T(8,128)} %bitcast.46), kind=kLoop, calls=%fused_computation.11 | loop fusion | flops 786432 | bytes 7864320 | tf_op jit(solution)/shard_map/level0_down/slice | solution.py:19
  3.6 4.7 %collective-permute-start.1 = (f32[3,32,4,512]{3,2,1,0:T(4,128)}, f32[3,32,4,512]{3,2,1,0:T(4,128)S(1)}, u32[]{:S(2)}, u32[]{:S(2)}) collective-permute-start(f32[3,32,4,512]{3,2,1,0:T(4,128)} %get-tuple-element.12), channel_id=1, source_target_pairs={{1,0},{2,1},{3,2},{4,3},{5,4},{6,5},{7,6},{8,7},{9,8},{10,9},{11,1... | collective-permute-start | bytes 2359304 | tf_op jit(solution)/shard_map/level0_down/ppermute | solution.py:20
  8.3 1.9 %collective-permute-start = (f32[3,32,4,512]{3,2,1,0:T(4,128)}, f32[3,32,4,512]{3,2,1,0:T(4,128)}, u32[]{:S(2)}, u32[]{:S(2)}) collective-permute-start(f32[3,32,4,512]{3,2,1,0:T(4,128)} %get-tuple-element.11), channel_id=1, source_target_pairs={{0,1},{1,2},{2,3},{3,4},{4,5},{5,6},{6,7},{7,8},{8,9},{9,10},{10,1... | collective-permute-start | bytes 2359304 | tf_op jit(solution)/shard_map/level0_down/ppermute | solution.py:19
  10.4 2.2 %reshape.400 = f32[16,2,16,2,512]{4,3,2,1,0:T(2,128)} reshape(f32[32,32,512]{2,1,0:T(8,128)S(1)} %copy-done) | data formatting | bytes 4194304 | tf_op jit(solution)/shard_map/level0_down/reshape | solution.py:83
  12.7 4.0 %reduce_sum.37 = f32[16,16,512]{2,1,0:T(8,128)} reduce(f32[16,2,16,2,512]{4,3,2,1,0:T(2,128)} %reshape.400, f32[]{:T(128)} %constant.162.clone.1), dimensions={1,3}, to_apply=%region_1.2 | reduce | flops 393216 | bytes 2621444 | tf_op jit(solution)/shard_map/level0_down/reduce_sum | solution.py:83
  16.9 8.5 %collective-permute-done.1 = f32[3,32,4,512]{3,2,1,0:T(4,128)S(1)} collective-permute-done((f32[3,32,4,512]{3,2,1,0:T(4,128)}, f32[3,32,4,512]{3,2,1,0:T(4,128)S(1)}, u32[]{:S(2)}, u32[]{:S(2)}) %collective-permute-start.1) | collective-permute-done | bytes 786464 | tf_op jit(solution)/shard_map/level0_down/ppermute | solution.py:20
  25.4 6.2 %collective-permute-done = f32[3,32,4,512]{3,2,1,0:T(4,128)} collective-permute-done((f32[3,32,4,512]{3,2,1,0:T(4,128)}, f32[3,32,4,512]{3,2,1,0:T(4,128)}, u32[]{:S(2)}, u32[]{:S(2)}) %collective-permute-start) | collective-permute-done | bytes 786464 | tf_op jit(solution)/shard_map/level0_down/ppermute | solution.py:19
  31.6 1.7 %pad_maximum_fusion.6 = (f32[3,4,40,512]{3,2,1,0:T(8,128)S(1)}, f32[3,4,40,512]{3,2,1,0:T(8,128)S(1)}) fusion(f32[3,32,4,512]{3,2,1,0:T(4,128)S(1)} %collective-permute-done.1, f32[3,32,4,512]{3,2,1,0:T(4,128)} %collective-permute-done, f32[1,32,32,512]{3,2,1,0:T(8,128)S(1)} %bitcast.41, f32[1,32,32,512]{3,2,1,0:T(8,128)} %bitcast.44, ...), kind=kLoop, calls=%fused_computation.8 | loop fusion | flops 1966080 | bytes 9830400 | tf_op jit(solution)/shard_map/level0_down/slice | solution.py:19
  33.4 1.9 %collective-permute-start.3 = (f32[3,4,40,512]{3,2,1,0:T(8,128)S(1)}, f32[3,4,40,512]{3,2,1,0:T(8,128)S(1)}, u32[]{:S(2)}, u32[]{:S(2)}) collective-permute-start(f32[3,4,40,512]{3,2,1,0:T(8,128)S(1)} %get-tuple-element.10), channel_id=1, source_target_pairs={{16,0},{32,16},{48,32},{64,48},{80,64},{96,80},{112,96},{17,1},{33... | collective-permute-start | bytes 2949128 | tf_op jit(solution)/shard_map/level0_down/ppermute | solution.py:20
  35.3 2.4 %collective-permute-start.2 = (f32[3,4,40,512]{3,2,1,0:T(8,128)S(1)}, f32[3,4,40,512]{3,2,1,0:T(8,128)S(1)}, u32[]{:S(2)}, u32[]{:S(2)}) collective-permute-start(f32[3,4,40,512]{3,2,1,0:T(8,128)S(1)} %get-tuple-element.9), channel_id=1, source_target_pairs={{0,16},{16,32},{32,48},{48,64},{64,80},{80,96},{96,112},{1,17},{17... | collective-permute-start | bytes 2949128 | tf_op jit(solution)/shard_map/level0_down/ppermute | solution.py:19
  37.7 0.6 pad_add_fusion.off_ref
  38.5 0.8 fusion.12
  39.3 7.6 %collective-permute-done.3 = f32[3,4,40,512]{3,2,1,0:T(8,128)S(1)} collective-permute-done((f32[3,4,40,512]{3,2,1,0:T(8,128)S(1)}, f32[3,4,40,512]{3,2,1,0:T(8,128)S(1)}, u32[]{:S(2)}, u32[]{:S(2)}) %collective-permute-start.3) | collective-permute-done | bytes 983072 | tf_op jit(solution)/shard_map/level0_down/ppermute | solution.py:20
  46.9 3.8 %collective-permute-done.2 = f32[3,4,40,512]{3,2,1,0:T(8,128)S(1)} collective-permute-done((f32[3,4,40,512]{3,2,1,0:T(8,128)S(1)}, f32[3,4,40,512]{3,2,1,0:T(8,128)S(1)}, u32[]{:S(2)}, u32[]{:S(2)}) %collective-permute-start.2) | collective-permute-done | bytes 983072 | tf_op jit(solution)/shard_map/level0_down/ppermute | solution.py:19
  50.7 7.9 %pad_maximum_fusion.s_ref = f32[3,40,40,512]{3,2,1,0:T(8,128)} fusion(f32[3,4,40,512]{3,2,1,0:T(8,128)S(1)} %collective-permute-done.3, f32[3,32,4,512]{3,2,1,0:T(4,128)S(1)} %collective-permute-done.1, f32[1,32,32,512]{3,2,1,0:T(8,128)S(1)} %bitcast.42, f32[1,32,32,512]{3,2,1,0:T(8,128)S(1)} %bitcast.45, f32[1,32,32,512]{3,2,1,0:T(8,128)S(1)} %bitcast.48, ...), kind=kLoop, calls=%fused_computation | loop fusion | flops 14745600 | bytes 19660800 | tf_op jit(solution)/shard_map/level0_down/concatenate | solution.py:21
  58.6 24.9 %level0_down.1 = (f32[40,40,512]{2,1,0:T(8,128)}, f32[16,32,512]{2,1,0:T(8,128)}) custom-call(s32[2]{0:T(128)} %pad_add_fusion.off_ref, f32[3,40,40,512]{3,2,1,0:T(8,128)} %pad_maximum_fusion.s_ref), custom_call_target="tpu_custom_call" | custom-call | flops 98304000 | bytes 16384000 | tf_op jit(solution)/shard_map/level0_down/pallas_call | solution.py:311
  83.5 1.8 %reshape.399 = f32[16,16,2,512]{3,2,1,0:T(2,128)S(1)} reshape(f32[16,32,512]{2,1,0:T(8,128)} %get-tuple-element.8) | data formatting | bytes 2097152 | tf_op jit(solution)/shard_map/level0_down/reshape | solution.py:94
  85.4 1.2 reduce_sum.36
  86.6 0.8 fusion.14
  87.5 1.9 %collective-permute-start.5 = (f32[2,16,4,256]{3,2,1,0:T(4,128)S(1)}, f32[2,16,4,256]{3,2,1,0:T(4,128)S(1)}, u32[]{:S(2)}, u32[]{:S(2)}) collective-permute-start(f32[2,16,4,256]{3,2,1,0:T(4,128)S(1)} %get-tuple-element.38), channel_id=1, source_target_pairs={{1,0},{2,1},{3,2},{4,3},{5,4},{6,5},{7,6},{8,7},{9,8},{10,9},{11,1... | collective-permute-start | bytes 393224 | tf_op jit(solution)/shard_map/level1_down/ppermute | solution.py:20
  89.4 3.9 %collective-permute-start.4 = (f32[2,16,4,256]{3,2,1,0:T(4,128)S(1)}, f32[2,16,4,256]{3,2,1,0:T(4,128)S(1)}, u32[]{:S(2)}, u32[]{:S(2)}) collective-permute-start(f32[2,16,4,256]{3,2,1,0:T(4,128)S(1)} %get-tuple-element.37), channel_id=1, source_target_pairs={{0,1},{1,2},{2,3},{3,4},{4,5},{5,6},{6,7},{7,8},{8,9},{9,10},{10,1... | collective-permute-start | bytes 393224 | tf_op jit(solution)/shard_map/level1_down/ppermute | solution.py:19
  93.3 0.1 reshape.402
  93.5 0.2 reduce_sum.39
  93.7 0.4 convolution_bitcast_fusion
  94.1 0.3 collective-permute-done.5
  94.3 4.0 %collective-permute-done.4 = f32[2,16,4,256]{3,2,1,0:T(4,128)S(1)} collective-permute-done((f32[2,16,4,256]{3,2,1,0:T(4,128)S(1)}, f32[2,16,4,256]{3,2,1,0:T(4,128)S(1)}, u32[]{:S(2)}, u32[]{:S(2)}) %collective-permute-start.4) | collective-permute-done | bytes 131104 | tf_op jit(solution)/shard_map/level1_down/ppermute | solution.py:19
  98.4 1.9 %collective-permute-start.7 = (f32[2,4,24,256]{3,2,1,0:T(8,128)S(1)}, f32[2,4,24,256]{3,2,1,0:T(8,128)S(1)}, u32[]{:S(2)}, u32[]{:S(2)}) collective-permute-start(f32[2,4,24,256]{3,2,1,0:T(8,128)S(1)} %get-tuple-element.16), channel_id=1, source_target_pairs={{16,0},{32,16},{48,32},{64,48},{80,64},{96,80},{112,96},{17,1},{33... | collective-permute-start | bytes 589832 | tf_op jit(solution)/shard_map/level1_down/ppermute | solution.py:20
  100.4 2.6 %collective-permute-start.6 = (f32[2,4,24,256]{3,2,1,0:T(8,128)S(1)}, f32[2,4,24,256]{3,2,1,0:T(8,128)S(1)}, u32[]{:S(2)}, u32[]{:S(2)}) collective-permute-start(f32[2,4,24,256]{3,2,1,0:T(8,128)S(1)} %get-tuple-element.15), channel_id=1, source_target_pairs={{0,16},{16,32},{32,48},{48,64},{64,80},{80,96},{96,112},{1,17},{17... | collective-permute-start | bytes 589832 | tf_op jit(solution)/shard_map/level1_down/ppermute | solution.py:19
  103.0 0.5 collective-permute-done.7
  103.5 3.8 %collective-permute-done.6 = f32[2,4,24,256]{3,2,1,0:T(8,128)S(1)} collective-permute-done((f32[2,4,24,256]{3,2,1,0:T(8,128)S(1)}, f32[2,4,24,256]{3,2,1,0:T(8,128)S(1)}, u32[]{:S(2)}, u32[]{:S(2)}) %collective-permute-start.6) | collective-permute-done | bytes 196640 | tf_op jit(solution)/shard_map/level1_down/ppermute | solution.py:19
  107.3 0.1 pad_maximum_fusion.1
  107.6 0.2 fusion.229
  107.8 0.1 fusion.230
  107.9 0.6 fusion.5
  108.7 0.2 fusion.232
  109.0 0.2 fusion.228
  109.3 1.2 fusion.39
  110.4 0.1 fusion.235
  110.8 0.1 fusion.226
  111.0 0.6 fusion.66
  111.5 0.1 reshape.401
  111.7 0.2 reduce_sum.38
  111.9 0.4 convolution_bitcast_fusion.1
  112.2 1.9 %collective-permute-start.9 = (f32[2,8,5,128]{3,2,1,0:T(8,128)S(1)}, f32[2,8,5,128]{3,2,1,0:T(8,128)S(1)}, u32[]{:S(2)}, u32[]{:S(2)}) collective-permute-start(f32[2,8,5,128]{3,2,1,0:T(8,128)S(1)} %get-tuple-element.80), channel_id=1, source_target_pairs={{1,0},{2,1},{3,2},{4,3},{5,4},{6,5},{7,6},{8,7},{9,8},{10,9},{11,1... | collective-permute-start | bytes 122888 | tf_op jit(solution)/shard_map/level2/ppermute | solution.py:20
  114.2 3.9 %collective-permute-start.8 = (f32[2,8,5,128]{3,2,1,0:T(8,128)S(1)}, f32[2,8,5,128]{3,2,1,0:T(8,128)S(1)}, u32[]{:S(2)}, u32[]{:S(2)}) collective-permute-start(f32[2,8,5,128]{3,2,1,0:T(8,128)S(1)} %get-tuple-element.79), channel_id=1, source_target_pairs={{0,1},{1,2},{2,3},{3,4},{4,5},{5,6},{6,7},{7,8},{8,9},{9,10},{10,1... | collective-permute-start | bytes 122888 | tf_op jit(solution)/shard_map/level2/ppermute | solution.py:19
  118.1 0.2 fusion.224
  118.4 4.0 %collective-permute-done.8 = f32[2,8,5,128]{3,2,1,0:T(8,128)S(1)} collective-permute-done((f32[2,8,5,128]{3,2,1,0:T(8,128)S(1)}, f32[2,8,5,128]{3,2,1,0:T(8,128)S(1)}, u32[]{:S(2)}, u32[]{:S(2)}) %collective-permute-start.8) | collective-permute-done | bytes 40992 | tf_op jit(solution)/shard_map/level2/ppermute | solution.py:19
  122.5 1.9 %collective-permute-start.11 = (f32[2,5,18,128]{3,2,1,0:T(8,128)S(1)}, f32[2,5,18,128]{3,2,1,0:T(8,128)S(1)}, u32[]{:S(2)}, u32[]{:S(2)}) collective-permute-start(f32[2,5,18,128]{3,2,1,0:T(8,128)S(1)} %get-tuple-element.66), channel_id=1, source_target_pairs={{16,0},{32,16},{48,32},{64,48},{80,64},{96,80},{112,96},{17,1},{33... | collective-permute-start | bytes 276488 | tf_op jit(solution)/shard_map/level2/ppermute | solution.py:20
  124.4 2.4 %collective-permute-start.10 = (f32[2,5,18,128]{3,2,1,0:T(8,128)S(1)}, f32[2,5,18,128]{3,2,1,0:T(8,128)S(1)}, u32[]{:S(2)}, u32[]{:S(2)}) collective-permute-start(f32[2,5,18,128]{3,2,1,0:T(8,128)S(1)} %get-tuple-element.65), channel_id=1, source_target_pairs={{0,16},{16,32},{32,48},{48,64},{64,80},{80,96},{96,112},{1,17},{17... | collective-permute-start | bytes 276488 | tf_op jit(solution)/shard_map/level2/ppermute | solution.py:19
  126.8 0.8 fusion.223
  127.7 3.0 %collective-permute-done.10 = f32[2,5,18,128]{3,2,1,0:T(8,128)S(1)} collective-permute-done((f32[2,5,18,128]{3,2,1,0:T(8,128)S(1)}, f32[2,5,18,128]{3,2,1,0:T(8,128)S(1)}, u32[]{:S(2)}, u32[]{:S(2)}) %collective-permute-start.10) | collective-permute-done | bytes 92192 | tf_op jit(solution)/shard_map/level2/ppermute | solution.py:19
  130.9 0.2 fusion.105
  131.5 0.3 fusion.137
  132.2 0.3 fusion.158
  132.9 0.5 fusion.110
  133.5 0.1 broadcast_in_dim.188
  133.6 0.3 reshape.404
  134.0 0.2 fusion.233
  134.3 0.5 copy-done.4
  135.0 2.1 %fusion.10 = f32[18,18,512]{2,1,0:T(8,128)S(1)} fusion(f32[20,20,256]{2,1,0:T(8,128)S(1)} %add.696, f32[24,24,256]{2,1,0:T(8,128)S(1)} %get-tuple-element.13, f32[18,18,255]{2,1,0:T(8,128)S(1)} %get-tuple-element.40, f32[18,18,1]{2,1,0:T(8,128)S(1)} %get-tuple-element.42, f32[18,18,1]{2,1,0:T(8,128)S(1)} %get-tuple-element.41, ...), kind=kOutput, calls=%fused_computation.31 | convolution fusion | flops 513567744 | bytes 8192512 | tf_op jit(solution)/shard_map/level0_up/dot_general | solution.py:369
  137.1 0.5 broadcast_in_dim.192
  137.5 0.9 reshape.405
  138.5 1.3 pad.4.e_ref
  139.8 20.1 %level0_up.1 = f32[32,32,512]{2,1,0:T(8,128)} custom-call(s32[2]{0:T(128)} %pad_add_fusion.off_ref, f32[40,40,512]{2,1,0:T(8,128)} %get-tuple-element.7.u2_ref, f32[18,40,512]{2,1,0:T(8,128)} %pad.4.e_ref, f32[3,40,40,512]{3,2,1,0:T(8,128)} %pad_maximum_fusion.s_ref), custom_call_target="tpu_custom_call" | custom-call | flops 65536000 | bytes 16384000 | tf_op jit(solution)/shard_map/level0_up/pallas_call | solution.py:311
  (62 shorter events, 3.1 us)
Async XLA Ops:
  0.0 10.4 %copy-start = (f32[32,32,512]{2,1,0:T(8,128)S(1)}, f32[32,32,512]{2,1,0:T(8,128)}, u32[]{:S(2)}) copy-start(f32[32,32,512]{2,1,0:T(8,128)} %param.5) | copy-start | bytes 6291460
  3.6 21.8 %collective-permute-start.1 = (f32[3,32,4,512]{3,2,1,0:T(4,128)}, f32[3,32,4,512]{3,2,1,0:T(4,128)S(1)}, u32[]{:S(2)}, u32[]{:S(2)}) collective-permute-start(f32[3,32,4,512]{3,2,1,0:T(4,128)} %get-tuple-element.12), channel_id=1, source_target_pairs={{1,0},{2,1},{3,2},{4,3},{5,4},{6,5},{7,6},{8,7},{9,8},{10,9},{11,1... | collective-permute-start | bytes 2359304 | tf_op jit(solution)/shard_map/level0_down/ppermute | solution.py:20
  8.3 23.3 %collective-permute-start = (f32[3,32,4,512]{3,2,1,0:T(4,128)}, f32[3,32,4,512]{3,2,1,0:T(4,128)}, u32[]{:S(2)}, u32[]{:S(2)}) collective-permute-start(f32[3,32,4,512]{3,2,1,0:T(4,128)} %get-tuple-element.11), channel_id=1, source_target_pairs={{0,1},{1,2},{2,3},{3,4},{4,5},{5,6},{6,7},{7,8},{8,9},{9,10},{10,1... | collective-permute-start | bytes 2359304 | tf_op jit(solution)/shard_map/level0_down/ppermute | solution.py:19
  16.9 21.6 %copy-start.3 = (f32[16,16,512]{2,1,0:T(8,128)S(1)}, f32[16,16,512]{2,1,0:T(8,128)}, u32[]{:S(2)}) copy-start(f32[16,16,512]{2,1,0:T(8,128)} %reduce_sum.37) | copy-start | bytes 1572868
  31.6 19.1 %copy-start.1 = (f32[32,32,512]{2,1,0:T(8,128)S(1)}, f32[32,32,512]{2,1,0:T(8,128)}, u32[]{:S(2)}) copy-start(f32[32,32,512]{2,1,0:T(8,128)} %param.4) | copy-start | bytes 6291460
  31.6 19.1 %copy-start.2 = (f32[32,32,512]{2,1,0:T(8,128)S(1)}, f32[32,32,512]{2,1,0:T(8,128)}, u32[]{:S(2)}) copy-start(f32[32,32,512]{2,1,0:T(8,128)} %param.3) | copy-start | bytes 6291460
  33.4 13.5 %collective-permute-start.3 = (f32[3,4,40,512]{3,2,1,0:T(8,128)S(1)}, f32[3,4,40,512]{3,2,1,0:T(8,128)S(1)}, u32[]{:S(2)}, u32[]{:S(2)}) collective-permute-start(f32[3,4,40,512]{3,2,1,0:T(8,128)S(1)} %get-tuple-element.10), channel_id=1, source_target_pairs={{16,0},{32,16},{48,32},{64,48},{80,64},{96,80},{112,96},{17,1},{33... | collective-permute-start | bytes 2949128 | tf_op jit(solution)/shard_map/level0_down/ppermute | solution.py:20
  35.3 15.4 %collective-permute-start.2 = (f32[3,4,40,512]{3,2,1,0:T(8,128)S(1)}, f32[3,4,40,512]{3,2,1,0:T(8,128)S(1)}, u32[]{:S(2)}, u32[]{:S(2)}) collective-permute-start(f32[3,4,40,512]{3,2,1,0:T(8,128)S(1)} %get-tuple-element.9), channel_id=1, source_target_pairs={{0,16},{16,32},{32,48},{48,64},{64,80},{80,96},{96,112},{1,17},{17... | collective-permute-start | bytes 2949128 | tf_op jit(solution)/shard_map/level0_down/ppermute | solution.py:19
  87.5 6.9 %collective-permute-start.5 = (f32[2,16,4,256]{3,2,1,0:T(4,128)S(1)}, f32[2,16,4,256]{3,2,1,0:T(4,128)S(1)}, u32[]{:S(2)}, u32[]{:S(2)}) collective-permute-start(f32[2,16,4,256]{3,2,1,0:T(4,128)S(1)} %get-tuple-element.38), channel_id=1, source_target_pairs={{1,0},{2,1},{3,2},{4,3},{5,4},{6,5},{7,6},{8,7},{9,8},{10,9},{11,1... | collective-permute-start | bytes 393224 | tf_op jit(solution)/shard_map/level1_down/ppermute | solution.py:20
  89.4 9.0 %collective-permute-start.4 = (f32[2,16,4,256]{3,2,1,0:T(4,128)S(1)}, f32[2,16,4,256]{3,2,1,0:T(4,128)S(1)}, u32[]{:S(2)}, u32[]{:S(2)}) collective-permute-start(f32[2,16,4,256]{3,2,1,0:T(4,128)S(1)} %get-tuple-element.37), channel_id=1, source_target_pairs={{0,1},{1,2},{2,3},{3,4},{4,5},{5,6},{6,7},{7,8},{8,9},{9,10},{10,1... | collective-permute-start | bytes 393224 | tf_op jit(solution)/shard_map/level1_down/ppermute | solution.py:19
  98.4 5.1 %collective-permute-start.7 = (f32[2,4,24,256]{3,2,1,0:T(8,128)S(1)}, f32[2,4,24,256]{3,2,1,0:T(8,128)S(1)}, u32[]{:S(2)}, u32[]{:S(2)}) collective-permute-start(f32[2,4,24,256]{3,2,1,0:T(8,128)S(1)} %get-tuple-element.16), channel_id=1, source_target_pairs={{16,0},{32,16},{48,32},{64,48},{80,64},{96,80},{112,96},{17,1},{33... | collective-permute-start | bytes 589832 | tf_op jit(solution)/shard_map/level1_down/ppermute | solution.py:20
  100.4 7.0 %collective-permute-start.6 = (f32[2,4,24,256]{3,2,1,0:T(8,128)S(1)}, f32[2,4,24,256]{3,2,1,0:T(8,128)S(1)}, u32[]{:S(2)}, u32[]{:S(2)}) collective-permute-start(f32[2,4,24,256]{3,2,1,0:T(8,128)S(1)} %get-tuple-element.15), channel_id=1, source_target_pairs={{0,16},{16,32},{32,48},{48,64},{64,80},{80,96},{96,112},{1,17},{17... | collective-permute-start | bytes 589832 | tf_op jit(solution)/shard_map/level1_down/ppermute | solution.py:19
  112.2 6.2 %collective-permute-start.9 = (f32[2,8,5,128]{3,2,1,0:T(8,128)S(1)}, f32[2,8,5,128]{3,2,1,0:T(8,128)S(1)}, u32[]{:S(2)}, u32[]{:S(2)}) collective-permute-start(f32[2,8,5,128]{3,2,1,0:T(8,128)S(1)} %get-tuple-element.80), channel_id=1, source_target_pairs={{1,0},{2,1},{3,2},{4,3},{5,4},{6,5},{7,6},{8,7},{9,8},{10,9},{11,1... | collective-permute-start | bytes 122888 | tf_op jit(solution)/shard_map/level2/ppermute | solution.py:20
  114.2 8.3 %collective-permute-start.8 = (f32[2,8,5,128]{3,2,1,0:T(8,128)S(1)}, f32[2,8,5,128]{3,2,1,0:T(8,128)S(1)}, u32[]{:S(2)}, u32[]{:S(2)}) collective-permute-start(f32[2,8,5,128]{3,2,1,0:T(8,128)S(1)} %get-tuple-element.79), channel_id=1, source_target_pairs={{0,1},{1,2},{2,3},{3,4},{4,5},{5,6},{6,7},{7,8},{8,9},{9,10},{10,1... | collective-permute-start | bytes 122888 | tf_op jit(solution)/shard_map/level2/ppermute | solution.py:19
  122.5 5.2 %collective-permute-start.11 = (f32[2,5,18,128]{3,2,1,0:T(8,128)S(1)}, f32[2,5,18,128]{3,2,1,0:T(8,128)S(1)}, u32[]{:S(2)}, u32[]{:S(2)}) collective-permute-start(f32[2,5,18,128]{3,2,1,0:T(8,128)S(1)} %get-tuple-element.66), channel_id=1, source_target_pairs={{16,0},{32,16},{48,32},{64,48},{80,64},{96,80},{112,96},{17,1},{33... | collective-permute-start | bytes 276488 | tf_op jit(solution)/shard_map/level2/ppermute | solution.py:20
  124.4 6.2 %collective-permute-start.10 = (f32[2,5,18,128]{3,2,1,0:T(8,128)S(1)}, f32[2,5,18,128]{3,2,1,0:T(8,128)S(1)}, u32[]{:S(2)}, u32[]{:S(2)}) collective-permute-start(f32[2,5,18,128]{3,2,1,0:T(8,128)S(1)} %get-tuple-element.65), channel_id=1, source_target_pairs={{0,16},{16,32},{32,48},{48,64},{64,80},{80,96},{96,112},{1,17},{17... | collective-permute-start | bytes 276488 | tf_op jit(solution)/shard_map/level2/ppermute | solution.py:19
  133.9 0.9 copy-start.4
  133.9 1.0 copy-start.5
